TPU v7x, 128 devices: a whole 4x4x4 slice. The times are simulated.
128 devices in a mesh: req: 4 (over z), wide: 32 (over x, y, core).
Axes of the slice: x: 4, y: 4, z: 4, core: 2. Of those that a mesh axis runs over, the one named last changes fastest.
Arguments:
- tokens: bfloat16 [512, 7168], P(('req', 'wide')), may hold values from -6 to 6
- attn_gain: bfloat16 [7168], replicated, may hold values from 0.099609375 to 1.8984375
- qkv_weight: bfloat16 [7168, 3, 7168], P(None, None, 'wide'), may hold values from -0.122756126 to 0.122756126
- adapter_down: bfloat16 [7168, 384], P('wide'), may hold values from -0.0625 to 0.0625
- adapter_up: bfloat16 [3, 128, 7168], P(None, None, 'wide'), may hold values from -0.5 to 0.5
- out_weight: bfloat16 [7168, 3584], P('wide'), may hold values from -0.0625 to 0.0625
- mlp_gain: bfloat16 [3584], replicated, may hold values from 0.099609375 to 1.8984375
- gate_up: bfloat16 [2, 14336, 3584], P(None, ('req', 'wide')), may hold values from -0.09375 to 0.09375
- down_weight: bfloat16 [14336, 3584], P(('req', 'wide')), may hold values from -0.046875 to 0.046875
- key_cache: bfloat16 [4, 8192, 7168], P('req', 'wide'), may hold values from -12 to 12
- value_cache: bfloat16 [4, 8192, 7168], P('req', 'wide'), may hold values from -6 to 6
- cache_lengths: int32 [4], P('req'), may hold values from 129 to 8192, as said below
- slot_mask: int32 [4, 8192], P('req', 'wide'), may hold values 0 or 1
- span_counts: int32 [4], P('req'), may hold values from 32 to 128, as said below
Outputs:
- hidden_out: bfloat16 [512, 3584], P(('req', 'wide'))
- attention: bfloat16 [512, 7168], P('req', 'wide')
- new_keys: bfloat16 [512, 7168], P('req', 'wide')
- new_values: bfloat16 [512, 7168], P('req', 'wide')
Inputs may be any that keep to these rules, and one draw needn't show every extreme that they name: `cache_lengths`: the longest request has exactly 8192 filled positions in every draw. `span_counts`: some request fills all 128 slots in every draw.
All inputs are finite; a program needn't handle non-finite values. No bound on the sum of `slot_mask` on one device may be relied on, other than what follows from the above.
Results may differ from a plain program's by a relative error of at most 0.024.
Values may be sent and summed in bfloat16 or wider, within the bound.
No kernel may reach another device: no remote copies, remote signals or barrier semaphores. Data moves between devices by JAX's collectives and lax.ppermute only.
A program may use at most 512 MiB of HBM per device.

v0:
```python
import jax
import jax.numpy as jnp
from jax import lax
from jax.sharding import PartitionSpec as P

D = 7168
HEADS = 32
HD = 224
RANK = 128
SPAN = 128


EPSILON = 1e-05
NEG_LARGE = -1e30


def joined_2(value, axis, join):
    pieces = jax.tree.map(lambda part: lax.all_gather(part, axis), value)
    head = jax.tree.map(lambda part: part[0], pieces)
    tail = jax.tree.map(lambda part: part[1:], pieces)
    so_far, _ = lax.scan(lambda so_far, slab: (join(so_far, slab), None), head, tail)
    return so_far


def rms_scale(values, gains):
    widened = values.astype(jnp.float32)
    meansq = jnp.mean(widened * widened, axis=-1, keepdims=True)
    return (widened * lax.rsqrt(meansq + EPSILON) * gains.astype(jnp.float32)).astype(jnp.bfloat16)


def softmax_join(first, second):
    first_num, first_max, first_sum = first
    second_num, second_max, second_sum = second
    highest = jnp.maximum(first_max, second_max)
    first_factor = jnp.exp(first_max - highest)
    second_factor = jnp.exp(second_max - highest)
    joined_num = first_num * first_factor[..., None] + second_num * second_factor[..., None]
    return (joined_num, highest, first_sum * first_factor + second_sum * second_factor)


def feed_forward(row_block, gate_rows, down_rows):
    both = jnp.einsum("td,cfd->ctf", row_block, gate_rows, preferred_element_type=jnp.float32)
    hidden = (jax.nn.silu(both[0]) * both[1]).astype(jnp.bfloat16)
    return jnp.dot(hidden, down_rows, preferred_element_type=jnp.float32)


def body(
    tokens,
    attn_gain,
    qkv_weight,
    adapter_down,
    adapter_up,
    out_weight,
    mlp_gain,
    gate_up,
    down_weight,
    key_cache,
    value_cache,
    cache_lengths,
    slot_mask,
    span_counts,
):
    score_scale = HD ** (-0.5)
    local_width = qkv_weight.shape[2]
    local_heads = local_width // HD
    wide_index = lax.axis_index("wide")
    feature_start = wide_index * local_width
    head_start = wide_index * local_heads
    normed = rms_scale(tokens, attn_gain)
    flat_weight = qkv_weight.reshape(D, 3 * local_width)
    shard_rows = lax.all_gather(normed, "wide", axis=0, tiled=True)
    base_part = jnp.dot(shard_rows, flat_weight, preferred_element_type=jnp.float32)
    sliced = lax.dynamic_slice_in_dim(shard_rows, feature_start, local_width, 1)
    partial_low = jnp.dot(sliced, adapter_down, preferred_element_type=jnp.float32)
    united_rows = jnp.concatenate([base_part, partial_low], axis=1)
    lowrank = lax.psum(united_rows[:, 3 * local_width :], "wide").astype(jnp.bfloat16)
    adapted = jnp.einsum(
        "tcr,crd->tcd",
        lowrank.reshape(SPAN, 3, RANK),
        adapter_up,
        preferred_element_type=jnp.float32,
    )
    projected = (united_rows[:, : 3 * local_width].reshape(SPAN, 3, local_width) + adapted).astype(
        jnp.bfloat16
    )
    query_own = projected[:, 0]
    new_keys = projected[:, 1]
    new_values = projected[:, 2]
    query_all = lax.all_gather(query_own, "wide", axis=1, tiled=True)
    block_len = key_cache.shape[1]
    block_start = wide_index * block_len
    length = cache_lengths[0]
    usable = (block_start + jnp.arange(block_len) < length) & (slot_mask[0] == 1)
    query_heads = query_all.reshape(SPAN, HEADS, HD)

    def cache_block(unused):
        key_heads = key_cache[0].reshape(block_len, HEADS, HD)
        value_heads = value_cache[0].reshape(block_len, HEADS, HD)
        scores = (
            jnp.einsum("qhd,khd->qhk", query_heads, key_heads, preferred_element_type=jnp.float32)
            * score_scale
        )
        scores = jnp.where(usable, scores, NEG_LARGE)
        highest = jnp.max(scores, axis=-1)
        weights = jnp.where(usable, jnp.exp(scores - highest[..., None]), 0.0)
        totals = jnp.sum(weights, axis=-1)
        numerator = jnp.einsum(
            "qhk,khd->qhd",
            weights.astype(jnp.bfloat16),
            value_heads,
            preferred_element_type=jnp.float32,
        )
        return (numerator, highest, totals)

    def skipped(unused):
        return (
            jnp.zeros((SPAN, HEADS, HD), jnp.float32),
            jnp.full((SPAN, HEADS), NEG_LARGE, jnp.float32),
            jnp.zeros((SPAN, HEADS), jnp.float32),
        )

    partial_value = lax.cond(block_start < length, cache_block, skipped, 0)
    span_count = span_counts[0]
    query_pos = jnp.arange(SPAN)[:, None]
    key_pos = jnp.arange(SPAN)[None, :]
    span_ok = ((key_pos <= query_pos) & ((key_pos < span_count) | (key_pos == query_pos)))[
        :, None, :
    ]
    own_query = query_own.reshape(SPAN, local_heads, HD)
    own_keys = new_keys.reshape(SPAN, local_heads, HD)
    own_values = new_values.reshape(SPAN, local_heads, HD)
    own_scores = (
        jnp.einsum("qhd,khd->qhk", own_query, own_keys, preferred_element_type=jnp.float32)
        * score_scale
    )
    own_scores = jnp.where(span_ok, own_scores, NEG_LARGE)
    own_max = jnp.max(own_scores, axis=-1)
    own_weights = jnp.where(span_ok, jnp.exp(own_scores - own_max[..., None]), 0.0)
    own_sum = jnp.sum(own_weights, axis=-1)
    own_num = jnp.einsum(
        "qhk,khd->qhd",
        own_weights.astype(jnp.bfloat16),
        own_values,
        preferred_element_type=jnp.float32,
    )
    sliced_part = tuple(
        (lax.dynamic_slice_in_dim(member, head_start, local_heads, 1) for member in partial_value)
    )
    joined = softmax_join(sliced_part, (own_num, own_max, own_sum))
    partial_value = tuple(
        (
            lax.dynamic_update_slice_in_dim(member, update, head_start, 1)
            for member, update in zip(partial_value, joined)
        )
    )

    def flat_join(first, second):
        first_heads = (first[0].reshape(SPAN, HEADS, HD), first[1], first[2])
        second_heads = (second[0].reshape(SPAN, HEADS, HD), second[1], second[2])
        joined_all = softmax_join(first_heads, second_heads)
        return (joined_all[0].reshape(SPAN, D), joined_all[1], joined_all[2])

    merged = joined_2(
        (partial_value[0].reshape(SPAN, D), partial_value[1], partial_value[2]), "wide", flat_join
    )
    numerator = lax.dynamic_slice_in_dim(merged[0], feature_start, local_width, 1).reshape(
        SPAN, local_heads, HD
    )
    totals = lax.dynamic_slice_in_dim(merged[2], head_start, local_heads, 1)
    attention = (numerator / totals[..., None]).reshape(SPAN, local_width).astype(jnp.bfloat16)
    attn_out = lax.psum_scatter(
        jnp.dot(attention, out_weight, preferred_element_type=jnp.float32),
        "wide",
        scatter_dimension=0,
        tiled=True,
    )
    normed_mid = rms_scale(attn_out, mlp_gain)
    every_row = lax.all_gather(normed_mid, ("req", "wide"), axis=0, tiled=True)
    mlp_out = lax.psum_scatter(
        feed_forward(every_row, gate_up, down_weight),
        ("req", "wide"),
        scatter_dimension=0,
        tiled=True,
    )
    hidden_out = mlp_out.astype(jnp.bfloat16)
    return (hidden_out, attention, new_keys, new_values)


def solution(mesh):
    return jax.shard_map(
        body,
        mesh=mesh,
        in_specs=(
            P(("req", "wide"), None),
            P(),
            P(None, None, "wide"),
            P("wide", None),
            P(None, None, "wide"),
            P("wide", None),
            P(),
            P(None, ("req", "wide"), None),
            P(("req", "wide"), None),
            P("req", "wide", None),
            P("req", "wide", None),
            P("req"),
            P("req", "wide"),
            P("req"),
        ),
        out_specs=(P(("req", "wide"), None), P("req", "wide"), P("req", "wide"), P("req", "wide")),
        check_vma=False,
    )
```

profile of v0, /device:TPU:1, one launch (start us, length us, event | category | flops | bytes accessed | tf_op | source)
XLA Modules:
  0.0 1460.9 jit_solution(12147504431665695407)
XLA Ops:
  10.7 46.9 %all-gather.12.cloned.1.call-done = bf16[32,4,7168]{2,1,0:T(4,128)(2,1)} async-done(((bf16[1,4,7168]{2,1,0:T(4,128)(2,1)}), bf16[32,4,7168]{2,1,0:T(4,128)(2,1)}) %all-gather.12.cloned.1.call-update) | async-done | bytes 1835024 | tf_op jit(solution)/shard_map/all_gather | solution.py:71
  62.4 122.9 %all-reduce.7 = bf16[128,384]{1,0:T(8,128)(2,1)S(1)} all-reduce(f32[128,384]{1,0:T(8,128)} %fusion.39), channel_id=1, replica_groups=mesh['req'=4,'wide'=32] {'wide'}, use_global_device_ids=true, to_apply=%region_1.0 | all-reduce | flops 49152 | bytes 294912 | tf_op jit(solution)/shard_map/psum | solution.py:76
  188.3 5.3 fusion.21
  196.2 43.4 %all-gather.10.cloned.1.call-done = bf16[128,1,7168]{0,2,1:T(8,128)(2,1)} async-done(((bf16[128,1,224]{0,2,1:T(8,128)(2,1)}), bf16[128,1,7168]{0,2,1:T(8,128)(2,1)}) %all-gather.10.cloned.1.call-update) | async-done | bytes 1835024 | tf_op jit(solution)/shard_map/all_gather | solution.py:89
  239.6 29.0 %conditional.1 = (f32[128,32,224]{0,2,1:T(8,128)}, f32[128,32]{0,1:T(8,128)}, f32[128,32]{0,1:T(8,128)}, f32[1,128,32]{1,2,0:T(8,128)S(1)}, f32[1,128,32]{1,2,0:T(8,128)S(1)}) conditional(s32[]{:T(128)} %convert_element_type.39, () %tuple.24, (s32[]{:T(128)}, bf16[1,256,7168]{2,1,0:T(8,128)(2,1)}, bf16[128,7168]{0,1:T(8,128)(2,1)}, ...), branch_computations={%region_2.0_spmd, %region_3.6_spmd.clone} | conditional | flops 953148416 | bytes 64425604 | solution.py:122
  241.0 6.1 copy.44
  255.1 5.9 copy.45
  261.0 6.8 fusion.15
  271.1 5.3 copy.46
  276.5 22.6 %all_gather.36 = f32[32,128,32]{1,2,0:T(8,128)S(1)} all-gather(f32[1,128,32]{1,2,0:T(8,128)S(1)} %dynamic_update_slice.12), channel_id=1, replica_groups=mesh['req'=4,'wide'=32] {'wide'}, dimensions={0}, use_global_device_ids=true | all-gather | bytes 540672 | tf_op jit(solution)/shard_map/all_gather | solution.py:18
  299.2 26.3 %all_gather.38 = f32[32,128,32]{1,2,0:T(8,128)S(1)} all-gather(f32[1,128,32]{1,2,0:T(8,128)S(1)} %dynamic_update_slice.13), channel_id=1, replica_groups=mesh['req'=4,'wide'=32] {'wide'}, dimensions={0}, use_global_device_ids=true | all-gather | bytes 540672 | tf_op jit(solution)/shard_map/all_gather | solution.py:18
  325.5 282.4 %all-gather.8.cloned.1.call-done = f32[32,128,7168]{2,1,0:T(8,128)} async-done(((f32[1,128,7168]{2,1,0:T(8,128)}), f32[32,128,7168]{2,1,0:T(8,128)}) %all-gather.8.cloned.1.call-update) | async-done | bytes 117440528 | tf_op jit(solution)/shard_map/all_gather | solution.py:18
  617.3 75.9 %slice.51 = f32[31,128,7168]{2,1,0:T(8,128)} slice(f32[32,128,7168]{2,1,0:T(8,128)} %all-gather.8.cloned.1.call-done), slice={[1:32], [0:128], [0:7168]} | slice | bytes 227540992 | tf_op jit(solution)/shard_map/slice | solution.py:20
  693.2 460.7 %while.14 = (s32[]{:T(128)}, f32[128,7168]{0,1:T(8,128)}, f32[128,32]{0,1:T(8,128)S(1)}, f32[128,32]{0,1:T(8,128)S(1)}, f32[31,128,32]{1,2,0:T(8,128)S(1)}, /*in...) while((s32[]{:T(128)}, f32[128,7168]{0,1:T(8,128)}, f32[128,32]{0,1:T(8,128)S(1)}, ...), condition=%wide.region_9.10_spmd, body=%wide.region_8.9_spmd.sunk | while | flops 2777090 | bytes 25854044 | solution.py:21
  697.5 5.3 copy.53
  702.8 5.3 fusion.85
  712.4 5.3 copy.53
  717.6 5.3 fusion.85
  727.2 5.3 copy.53
  732.5 5.3 fusion.85
  742.1 5.3 copy.53
  747.4 5.3 fusion.85
  756.9 5.3 copy.53
  762.2 5.3 fusion.85
  771.8 5.3 copy.53
  777.1 5.3 fusion.85
  786.7 5.3 copy.53
  791.9 5.3 fusion.85
  801.5 5.3 copy.53
  806.8 5.3 fusion.85
  816.4 5.3 copy.53
  821.7 5.3 fusion.85
  831.2 5.3 copy.53
  836.5 5.3 fusion.85
  846.1 5.3 copy.53
  851.4 5.3 fusion.85
  861.0 5.3 copy.53
  866.2 5.3 fusion.85
  875.8 5.3 copy.53
  881.1 5.3 fusion.85
  890.7 5.3 copy.53
  896.0 5.3 fusion.85
  905.5 5.3 copy.53
  910.8 5.3 fusion.85
  925.7 5.3 fusion.85
  940.5 5.3 fusion.85
  955.4 5.3 fusion.85
  970.3 5.3 fusion.85
  985.1 5.3 fusion.85
  1000.0 5.3 fusion.85
  1014.8 5.3 fusion.85
  1029.7 5.3 fusion.85
  1044.6 5.3 fusion.85
  1059.4 5.3 fusion.85
  1074.3 5.3 fusion.85
  1089.1 5.3 fusion.85
  1104.0 5.3 fusion.85
  1118.9 5.3 fusion.85
  1133.7 5.3 fusion.85
  1148.6 5.3 fusion.85
  1157.9 103.5 %all-reduce.6.cloned.1.call-done = f32[128,3584]{1,0:T(8,128)} async-done(((f32[128,3584]{1,0:T(8,128)}), f32[128,3584]{1,0:T(8,128)}) %all-reduce.6.cloned.1.call-update) | async-done | bytes 1835024
  1264.1 67.2 %all-gather.14.cloned.1.call-done = bf16[128,4,3584]{2,1,0:T(4,128)(2,1)} async-done(((bf16[1,4,3584]{2,1,0:T(4,128)(2,1)}), bf16[128,4,3584]{2,1,0:T(4,128)(2,1)}) %all-gather.14.cloned.1.call-update) | async-done | bytes 3670032 | tf_op jit(solution)/shard_map/all_gather | solution.py:178
  1331.3 6.7 reshape.165
  1345.5 107.4 %all-reduce.8 = bf16[512,3584]{1,0:T(8,128)(2,1)} all-reduce(f32[512,3584]{1,0:T(8,128)} %fusion.36), channel_id=4, replica_groups=mesh['req'=4,'wide'=32] {'req','wide'}, use_global_device_ids=true, to_apply=%region_12.13.clone | all-reduce | flops 1835008 | bytes 11010048
  (157 shorter events, 265.3 us)
Async XLA Ops:
  7.2 1147.7 %copy-start = (bf16[224,3584]{1,0:T(8,128)(2,1)S(1)}, bf16[224,3584]{1,0:T(8,128)(2,1)}, u32[]{:S(2)}) copy-start(bf16[224,3584]{1,0:T(8,128)(2,1)} %param.23) | copy-start | bytes 4816900
  7.2 50.4 %all-gather.12.cloned.1.call-start = ((), (), s32[]{:S(2)}) async-start(), calls=%async_computation.2 | async-start | bytes 1892352 | tf_op jit(solution)/shard_map/all_gather | solution.py:71
  10.6 229.0 %all-gather.10.cloned.1.call-start = ((), (), s32[]{:S(2)}) async-start(), calls=%async_computation.1 | async-start | bytes 1892352 | tf_op jit(solution)/shard_map/all_gather | solution.py:89
  188.3 5.3 copy-start.7
  194.5 45.1 %copy-start.9 = (bf16[128,224]{0,1:T(8,128)(2,1)}, bf16[128,224]{0,1:T(8,128)(2,1)S(1)}, u32[]{:S(2)}) copy-start(bf16[128,224]{0,1:T(8,128)(2,1)S(1)} %get-tuple-element.149) | copy-start | bytes 172036
  194.5 413.4 %all-gather.8.cloned.1.call-start = ((), (), s32[]{:S(2)}) async-start(), calls=%async_computation | async-start | bytes 121110528 | tf_op jit(solution)/shard_map/all_gather | solution.py:18
  241.0 6.1 copy-start.4
  251.2 1.9 copy-start.1
  255.1 5.9 copy-start.8
  276.5 984.9 %all-reduce.6.cloned.1.call-start = ((), (), s32[]{:S(2)}) async-start(), calls=%async_computation.4 | async-start | bytes 3670016
  299.2 312.9 %copy-start.2 = (f32[32,128,32]{1,2,0:T(8,128)}, f32[32,128,32]{1,2,0:T(8,128)S(1)}, u32[]{:S(2)}) copy-start(f32[32,128,32]{1,2,0:T(8,128)S(1)} %all_gather.36) | copy-start | bytes 1572868
  325.5 286.6 %copy-start.3 = (f32[32,128,32]{1,2,0:T(8,128)}, f32[32,128,32]{1,2,0:T(8,128)S(1)}, u32[]{:S(2)}) copy-start(f32[32,128,32]{1,2,0:T(8,128)S(1)} %all_gather.38) | copy-start | bytes 1572868
  617.3 75.9 %slice-start = ((f32[32,128,32]{1,2,0:T(8,128)}), f32[31,128,32]{1,2,0:T(8,128)S(1)}, s32[]{:S(2)}) async-start(f32[32,128,32]{1,2,0:T(8,128)} %copy-done.2), calls=%async_computation.5 | async-start | bytes 1015808 | tf_op jit(solution)/shard_map/slice | solution.py:20
  617.3 75.9 %slice-start.1 = ((f32[32,128,32]{1,2,0:T(8,128)}), f32[31,128,32]{1,2,0:T(8,128)S(1)}, s32[]{:S(2)}) async-start(f32[32,128,32]{1,2,0:T(8,128)} %copy-done.3), calls=%async_computation.6 | async-start | bytes 1015808 | tf_op jit(solution)/shard_map/slice | solution.py:20
  1153.9 2.7 copy-start.10
  1153.9 2.8 copy-start.12
  1154.9 183.2 %copy-start.6 = (bf16[128,224]{0,1:T(8,128)(2,1)}, bf16[128,224]{0,1:T(8,128)(2,1)S(1)}, u32[]{:S(2)}) copy-start(bf16[128,224]{0,1:T(8,128)(2,1)S(1)} %divide_convert_fusion) | copy-start | bytes 172036
  1156.6 174.7 %all-gather.14.cloned.1.call-start = ((), (), s32[]{:S(2)}) async-start(), calls=%async_computation.3 | async-start | bytes 3698688 | tf_op jit(solution)/shard_map/all_gather | solution.py:178
  1264.1 74.0 %copy-start.11 = (bf16[2,112,3584]{2,1,0:T(8,128)(2,1)S(1)}, bf16[2,112,3584]{2,1,0:T(8,128)(2,1)}, u32[]{:S(2)}) copy-start(bf16[2,112,3584]{2,1,0:T(8,128)(2,1)} %param.25) | copy-start | bytes 4816900
  1338.1 3.3 copy-start.5
Sparse Core Ops, SparseCore 0:
  10.8 46.7 all-gather.11
  194.7 44.9 all-gather.9
  276.6 331.2 all-gather.7
  1156.7 104.6 all-reduce.5
  1264.8 66.4 all-gather.13
where the time goes:
time: 1470 us; the launch traced here: 1460 us
  waiting for transfers between devices  543 us (37%)
  local copies, waits for them, and re-layouts  415 us (28%)
  blocking collectives  279 us (19%)
  other arithmetic  177 us (12%)
  matrix products  29.5 us (2%)
  between operations  15.9 us (1%)
    dynamic_slice x62, local copies, waits for them, and re-layouts, joined_2(): lax.scan(lambda so_far, slab: (join(so_far, slab), None), head, tail)  294 us
    all_gather x1, waiting for transfers between devices, joined_2(): pieces = jax.tree.map(lambda part: lax.all_gather(part, axis), value)  282 us
    add x31, other arithmetic, softmax_join(): first_num * first_factor[..., None] + second_num * second_factor[..., None]  166 us
    psum x1, blocking collectives, body(): lax.psum(united_rows[:, 3 * local_width:], 'wide').astype(jnp.bfloat16)  123 us
    unnamed x1, blocking collectives  107 us
    unnamed x6, waiting for transfers between devices  104 us
    slice x5, local copies, waits for them, and re-layouts, joined_2(): tail = jax.tree.map(lambda part: part[1:], pieces)  75.9 us
    all_gather x1, waiting for transfers between devices, body(): every_row = lax.all_gather(normed_mid, ('req', 'wide'), axis=0, tiled=True)  67.2 us
  transfers between devices with their start and end apart: 5, of which 5 were waited for; matrix products, arithmetic and copies ran while one was open for 0% of the time, Pallas kernels for 0%

commit v1 on v0

v1 whole, which is shorter than its diff:
```python
import jax
import jax.numpy as jnp
from jax import lax
from jax.sharding import PartitionSpec as P

D = 7168
HEADS = 32
HD = 224
RANK = 128
SPAN = 128


EPSILON = 1e-05
NEG_LARGE = -1e30
ALL = ("req", "wide")


def rms_scale(values, gains):
    widened = values.astype(jnp.float32)
    meansq = jnp.mean(widened * widened, axis=-1, keepdims=True)
    return (widened * lax.rsqrt(meansq + EPSILON) * gains.astype(jnp.float32)).astype(jnp.bfloat16)


def gather_rows(piece, axis, count):
    flat = piece.reshape(1, -1)
    spread = jnp.broadcast_to(flat, (count, flat.shape[1]))
    return lax.all_to_all(spread, axis, 0, 0, tiled=True)


def send_rows(values, axis, count):
    return lax.all_to_all(values.reshape(count, -1), axis, 0, 0, tiled=True)


def split_pair(values):
    high = lax.reduce_precision(values, exponent_bits=8, mantissa_bits=7)
    low = lax.reduce_precision(values - high, exponent_bits=8, mantissa_bits=7)
    return high, low


def join_pair(high, low):
    return high.astype(jnp.float32) + low.astype(jnp.float32)


def body(
    tokens,
    attn_gain,
    qkv_weight,
    adapter_down,
    adapter_up,
    out_weight,
    mlp_gain,
    gate_up,
    down_weight,
    key_cache,
    value_cache,
    cache_lengths,
    slot_mask,
    span_counts,
):
    score_scale = HD ** (-0.5)
    wide_size = lax.psum(1, "wide")
    all_size = lax.psum(1, ALL)
    local_width = qkv_weight.shape[2]
    local_heads = local_width // HD
    own_rows = tokens.shape[0]
    wide_index = lax.axis_index("wide")
    feature_start = wide_index * local_width

    normed = rms_scale(tokens, attn_gain)
    shard_rows = gather_rows(normed, "wide", wide_size).reshape(SPAN, D)
    base_part = jnp.dot(
        shard_rows, qkv_weight.reshape(D, 3 * local_width), preferred_element_type=jnp.float32
    )
    sliced = lax.dynamic_slice_in_dim(shard_rows, feature_start, local_width, 1)
    partial_low = jnp.dot(sliced, adapter_down, preferred_element_type=jnp.float32)
    low_parts = send_rows(partial_low, "wide", wide_size)
    own_low = jnp.sum(low_parts, axis=0).astype(jnp.bfloat16).reshape(own_rows, 3 * RANK)
    lowrank = gather_rows(own_low, "wide", wide_size).reshape(SPAN, 3, RANK)
    adapted = jnp.einsum("tcr,crd->tcd", lowrank, adapter_up, preferred_element_type=jnp.float32)
    projected = (base_part.reshape(SPAN, 3, local_width) + adapted).astype(jnp.bfloat16)
    query_own = projected[:, 0]
    new_keys = projected[:, 1]
    new_values = projected[:, 2]

    query_heads = gather_rows(query_own, "wide", wide_size).reshape(HEADS, SPAN, HD)
    block_len = key_cache.shape[1]
    block_start = wide_index * block_len
    length = cache_lengths[0]
    usable = (block_start + jnp.arange(block_len) < length) & (slot_mask[0] == 1)

    def cache_block(unused):
        key_heads = key_cache[0].reshape(block_len, HEADS, HD)
        value_heads = value_cache[0].reshape(block_len, HEADS, HD)
        scores = (
            jnp.einsum("hqd,khd->hqk", query_heads, key_heads, preferred_element_type=jnp.float32)
            * score_scale
        )
        scores = jnp.where(usable, scores, NEG_LARGE)
        highest = jnp.max(scores, axis=-1)
        high, low = split_pair(highest)
        reference_max = high + low
        weights = jnp.where(usable, jnp.exp(scores - reference_max[..., None]), 0.0)
        totals = jnp.sum(weights, axis=-1)
        numerator = jnp.einsum(
            "hqk,khd->hqd",
            weights.astype(jnp.bfloat16),
            value_heads,
            preferred_element_type=jnp.float32,
        )
        total_high, total_low = split_pair(totals)
        stats = jnp.stack([high, low, total_high, total_low], axis=-1).astype(jnp.bfloat16)
        return jnp.concatenate([numerator.astype(jnp.bfloat16), stats], axis=-1)

    def skipped(unused):
        stats = jnp.zeros((HEADS, SPAN, 4), jnp.bfloat16).at[..., 0].set(NEG_LARGE)
        return jnp.concatenate([jnp.zeros((HEADS, SPAN, HD), jnp.bfloat16), stats], axis=-1)

    packed = lax.cond(block_start < length, cache_block, skipped, 0)
    parts = lax.all_to_all(packed, "wide", 0, 0, tiled=True)
    part_num = parts[..., :HD].astype(jnp.float32)
    part_max = join_pair(parts[..., HD], parts[..., HD + 1])
    part_sum = join_pair(parts[..., HD + 2], parts[..., HD + 3])

    span_count = span_counts[0]
    query_pos = jnp.arange(SPAN)[:, None]
    key_pos = jnp.arange(SPAN)[None, :]
    span_ok = ((key_pos <= query_pos) & ((key_pos < span_count) | (key_pos == query_pos)))[
        :, None, :
    ]
    own_query = query_own.reshape(SPAN, local_heads, HD)
    own_keys = new_keys.reshape(SPAN, local_heads, HD)
    own_values = new_values.reshape(SPAN, local_heads, HD)
    own_scores = (
        jnp.einsum("qhd,khd->qhk", own_query, own_keys, preferred_element_type=jnp.float32)
        * score_scale
    )
    own_scores = jnp.where(span_ok, own_scores, NEG_LARGE)
    own_max = jnp.max(own_scores, axis=-1)
    own_weights = jnp.where(span_ok, jnp.exp(own_scores - own_max[..., None]), 0.0)
    own_sum = jnp.sum(own_weights, axis=-1)
    own_num = jnp.einsum(
        "qhk,khd->qhd",
        own_weights.astype(jnp.bfloat16),
        own_values,
        preferred_element_type=jnp.float32,
    )
    own_num = own_num.reshape(SPAN, HD)
    own_max = own_max.reshape(SPAN)
    own_sum = own_sum.reshape(SPAN)

    highest = jnp.maximum(jnp.max(part_max, axis=0), own_max)
    part_factor = jnp.exp(part_max - highest)
    own_factor = jnp.exp(own_max - highest)
    numerator = jnp.sum(part_num * part_factor[..., None], axis=0) + own_num * own_factor[:, None]
    totals = jnp.sum(part_sum * part_factor, axis=0) + own_sum * own_factor
    attention = (numerator / totals[:, None]).astype(jnp.bfloat16)

    head_out = jnp.dot(attention, out_weight, preferred_element_type=jnp.float32)
    out_parts = send_rows(head_out.astype(jnp.bfloat16), "wide", wide_size)
    attn_out = jnp.sum(out_parts.astype(jnp.float32), axis=0).reshape(own_rows, -1)
    normed_mid = rms_scale(attn_out, mlp_gain)
    every_row = gather_rows(normed_mid, ALL, all_size).reshape(all_size * own_rows, -1)
    both = jnp.einsum("td,cfd->ctf", every_row, gate_up, preferred_element_type=jnp.float32)
    hidden = (jax.nn.silu(both[0]) * both[1]).astype(jnp.bfloat16)
    ffn_part = jnp.dot(hidden, down_weight, preferred_element_type=jnp.float32)
    ffn_parts = send_rows(ffn_part.astype(jnp.bfloat16), ALL, all_size)
    hidden_out = jnp.sum(ffn_parts.astype(jnp.float32), axis=0).astype(jnp.bfloat16)
    hidden_out = hidden_out.reshape(own_rows, -1)
    return (hidden_out, attention, new_keys, new_values)


def solution(mesh):
    return jax.shard_map(
        body,
        mesh=mesh,
        in_specs=(
            P(("req", "wide"), None),
            P(),
            P(None, None, "wide"),
            P("wide", None),
            P(None, None, "wide"),
            P("wide", None),
            P(),
            P(None, ("req", "wide"), None),
            P(("req", "wide"), None),
            P("req", "wide", None),
            P("req", "wide", None),
            P("req"),
            P("req", "wide"),
            P("req"),
        ),
        out_specs=(P(("req", "wide"), None), P("req", "wide"), P("req", "wide"), P("req", "wide")),
        check_vma=False,
    )
```

time: 1470 us -> 579 us (0.39)
  waiting for transfers between devices: 543 us -> 97.2 us
  local copies, waits for them, and re-layouts: 415 us -> 158 us
  blocking collectives: 279 us -> 107 us
  other arithmetic: 177 us -> 143 us
  starting transfers between devices: 0.21 us -> 33.4 us
    all_gather x4 -> x0, waiting for transfers between devices: 440 us -> none  [the longest x1 282 us: joined_2(): pieces = jax.tree.map(lambda part: lax.all_gather(part, axis), value)]
    dynamic_slice x62 -> x0, local copies, waits for them, and re-layouts: 294 us -> none  [joined_2(): lax.scan(lambda so_far, slab: (join(so_far, slab), None), head, tail)]
    add x62 -> x3, other arithmetic: 166 us -> 0.05 us  [the longest x1 0.03 us: join_pair(): return high.astype(jnp.float32) + low.astype(jnp.float32)]
    psum x1 -> x0, blocking collectives: 123 us -> none  [body(): lax.psum(united_rows[:, 3 * local_width:], 'wide').astype(jnp.bfloat16)]
    unnamed x1 -> x0, blocking collectives: 107 us -> none
    all_to_all x0 -> x2, blocking collectives: none -> 107 us  [the longest x1 54.5 us: gather_rows(): return lax.all_to_all(spread, axis, 0, 0, tiled=True)]
    unnamed x6 -> x0, waiting for transfers between devices: 104 us -> none
    all_to_all x0 -> x6, waiting for transfers between devices: none -> 97.2 us  [the longest x3 51.9 us: gather_rows(): return lax.all_to_all(spread, axis, 0, 0, tiled=True)]
  transfers between devices with their start and end apart: 5 -> 6, of which waited for: 5 -> 6; matrix products, arithmetic and copies ran while one was open for 0% -> 2% of each run, Pallas kernels for 0% -> 0%
where the time goes in v1:
time: 579 us; the launch traced here: 568 us
  local copies, waits for them, and re-layouts  158 us (27%)
  other arithmetic  143 us (25%)
  blocking collectives  107 us (18%)
  waiting for transfers between devices  97.2 us (17%)
  starting transfers between devices  33.4 us (6%)
  matrix products  26.1 us (5%)
    unnamed x33, local copies, waits for them, and re-layouts  80.8 us
    all_to_all x1, blocking collectives, gather_rows(): return lax.all_to_all(spread, axis, 0, 0, tiled=True)  54.5 us
    all_to_all x1, blocking collectives, send_rows(): return lax.all_to_all(values.reshape(count, -1), axis, 0, 0, tiled=True)  52.9 us
    all_to_all x3, waiting for transfers between devices, gather_rows(): return lax.all_to_all(spread, axis, 0, 0, tiled=True)  51.9 us
    broadcast_in_dim x4, other arithmetic, gather_rows(): spread = jnp.broadcast_to(flat, (count, flat.shape[1]))  49.7 us
    all_to_all x3, other arithmetic, gather_rows(): return lax.all_to_all(spread, axis, 0, 0, tiled=True)  35.5 us
    all_to_all x2, other arithmetic, send_rows(): return lax.all_to_all(values.reshape(count, -1), axis, 0, 0, tiled=True)  29.9 us
    all_to_all x1, waiting for transfers between devices, body(): parts = lax.all_to_all(packed, 'wide', 0, 0, tiled=True)  23.7 us
  transfers between devices with their start and end apart: 6, of which 6 were waited for; matrix products, arithmetic and copies ran while one was open for 2% of the time, Pallas kernels for 0%

profile of v1, /device:TPU:1, one launch (start us, length us, event | category | flops | bytes accessed | tf_op | source)
XLA Modules:
  0.0 567.7 jit_solution(15535498938341474050)
XLA Ops:
  0.6 0.8 convert_element_type.83
  1.5 1.0 fusion.33
  2.5 0.9 fusion.43
  3.4 5.1 broadcast_in_dim.57
  9.1 12.4 %reduce.16 = bf16[32,28672]{1,0:T(8,128)(2,1)S(1)} reduce(bf16[32,1,28672]{2,1,0:T(2,128)(2,1)} %broadcast_in_dim.57, bf16[]{:T(256)} %broadcast.156), dimensions={1}, to_apply=%broadcast_in_dim.57.reduce_sub_computation | reduce | bytes 3670018 | tf_op jit(solution)/shard_map/broadcast_in_dim | solution.py:26
  21.5 2.3 reshape.325
  23.8 8.6 %all-to-all-start = ((bf16[32,2,14336]{2,1,0:T(2,128)(2,1)}), bf16[32,2,14336]{2,1,0:T(2,128)(2,1)S(1)}, u32[]{:S(2)}, u32[]{:S(2)}) async-start(bf16[32,2,14336]{2,1,0:T(2,128)(2,1)} %reshape.325), calls=%async_computation | async-start | bytes 3670016 | tf_op jit(solution)/shard_map/all_to_all | solution.py:27
  32.4 25.5 %all-to-all-done = bf16[32,2,14336]{2,1,0:T(2,128)(2,1)S(1)} async-done(((bf16[32,2,14336]{2,1,0:T(2,128)(2,1)}), bf16[32,2,14336]{2,1,0:T(2,128)(2,1)S(1)}, u32[]{:S(2)}, u32[]{:S(2)}) %all-to-all-start) | async-done | bytes 1835040 | tf_op jit(solution)/shard_map/all_to_all | solution.py:27
  57.9 6.5 %reshape.326 = bf16[32,1,28672]{2,1,0:T(2,128)(2,1)} reshape(bf16[32,2,14336]{2,1,0:T(2,128)(2,1)S(1)} %all-to-all-done) | data formatting | bytes 3670016
  64.4 11.8 %reduce.11 = bf16[32,28672]{1,0:T(8,128)(2,1)S(1)} reduce(bf16[32,1,28672]{2,1,0:T(2,128)(2,1)} %reshape.326, bf16[]{:T(256)} %constant.86), dimensions={1}, to_apply=%all_to_all.37.reduce_sub_computation | reduce | bytes 3670018 | tf_op jit(solution)/shard_map/all_to_all | solution.py:27
  76.2 2.4 reshape.301
  78.6 1.9 fusion.39
  80.5 1.8 all_to_all.48
  82.3 4.9 all-to-all-start.1
  87.2 2.4 reshape.314
  89.7 6.0 %all-to-all-done.1 = f32[32,1,1536]{2,1,0:T(1,128)} async-done(((f32[32,1,1536]{2,1,0:T(1,128)}), f32[32,1,1536]{2,1,0:T(1,128)}, u32[]{:S(2)}, u32[]{:S(2)}) %all-to-all-start.1) | async-done | bytes 196640 | tf_op jit(solution)/shard_map/all_to_all | solution.py:31
  95.7 1.1 reduce_sum.87
  96.9 1.2 reduce.17
  98.7 4.4 all-to-all-start.2
  103.1 5.9 %fusion.21 = f32[128,3,224]{0,2,1:T(8,128)S(1)} fusion(bf16[128,7168,1]{1,0,2:T(8,128)(2,1)} %reshape.314, bf16[7168,3,224]{0,2,1:T(8,128)(2,1)} %param.20), kind=kOutput, calls=%fused_computation.28 | convolution fusion | flops 1233125376 | bytes 11812864 | tf_op jit(solution)/shard_map/dot_general | solution.py:71
  109.0 1.6 all-to-all-done.2
  113.0 5.1 broadcast_in_dim.60
  118.1 12.4 %reduce.18 = bf16[32,28672]{1,0:T(8,128)(2,1)S(1)} reduce(bf16[32,1,28672]{2,1,0:T(2,128)(2,1)} %broadcast_in_dim.60, bf16[]{:T(256)} %broadcast.156), dimensions={1}, to_apply=%broadcast_in_dim.60.reduce_sub_computation | reduce | bytes 3670018 | tf_op jit(solution)/shard_map/broadcast_in_dim | solution.py:26
  130.5 2.3 reshape.329
  132.9 6.0 %all-to-all-start.3 = ((bf16[32,2,14336]{2,1,0:T(2,128)(2,1)}), bf16[32,2,14336]{2,1,0:T(2,128)(2,1)S(1)}, u32[]{:S(2)}, u32[]{:S(2)}) async-start(bf16[32,2,14336]{2,1,0:T(2,128)(2,1)} %reshape.329), calls=%async_computation.3 | async-start | bytes 3670016 | tf_op jit(solution)/shard_map/all_to_all | solution.py:27
  139.5 24.8 %all-to-all-done.3 = bf16[32,2,14336]{2,1,0:T(2,128)(2,1)S(1)} async-done(((bf16[32,2,14336]{2,1,0:T(2,128)(2,1)}), bf16[32,2,14336]{2,1,0:T(2,128)(2,1)S(1)}, u32[]{:S(2)}, u32[]{:S(2)}) %all-to-all-start.3) | async-done | bytes 1835040 | tf_op jit(solution)/shard_map/all_to_all | solution.py:27
  164.3 6.5 %reshape.330 = bf16[32,1,28672]{2,1,0:T(2,128)(2,1)} reshape(bf16[32,2,14336]{2,1,0:T(2,128)(2,1)S(1)} %all-to-all-done.3) | data formatting | bytes 3670016
  170.9 46.3 %conditional.1 = (bf16[32,128,228]{1,2,0:T(8,128)(2,1)}) conditional(s32[]{:T(128)} %convert_element_type.81, () %tuple.18, (s32[]{:T(128)}, bf16[1,256,7168]{2,1,0:T(8,128)(2,1)}, bf16[32,1,28672]{2,1,0:T(2,128)(2,1)}, bf16[1,256,7168]{2,1,0:T(8,128)(2,1)}, s32[1,256]{1,0:T(1,128)S(1)}, /*index=5*/s32[]{:T(128)}, s32[256]{0:T(256)S(1)}) %tuple.39), branch_computations={%region_2.3_spmd, %region_3.6_spmd.clone} | conditional | flops 954123264 | bytes 66358832 | solution.py:118
  171.7 11.8 %reduce.10 = bf16[32,28672]{1,0:T(8,128)(2,1)S(1)} reduce(bf16[32,1,28672]{2,1,0:T(2,128)(2,1)} %get-tuple-element.101, bf16[]{:T(256)} %constant.85), dimensions={1}, to_apply=%get-tuple-element.101.reduce_sub_computation | reduce | bytes 3670018 | tf_op jit(solution)/shard_map
  183.5 4.0 reshape.313
  187.4 5.9 %copy.78 = bf16[1,256,7168]{1,2,0:T(8,128)(2,1)} copy(bf16[1,256,7168]{2,1,0:T(8,128)(2,1)} %get-tuple-element.100) | data formatting | bytes 7340032 | tf_op jit(solution)/shard_map
  193.3 3.7 fusion
  197.0 1.9 copy-done.2
  198.9 1.5 fusion.1
  200.6 5.9 %copy.80 = bf16[1,256,7168]{1,2,0:T(8,128)(2,1)} copy(bf16[1,256,7168]{2,1,0:T(8,128)(2,1)} %get-tuple-element.102) | data formatting | bytes 7340032 | tf_op jit(solution)/shard_map
  206.5 4.5 fusion.10
  211.1 6.1 %concatenate.7 = bf16[32,128,228]{1,2,0:T(8,128)(2,1)} concatenate(bf16[32,128,224]{1,2,0:T(8,128)(2,1)S(1)} %fusion.10, bf16[32,128,1]{1,2,0:T(2,128)(2,1)S(1)} %copy.71, bf16[32,128,1]{1,2,0:T(2,128)(2,1)S(1)} %copy.72, bf16[32,128,1]{1,2,0:T(2,128)(2,1)S(1)} %copy.73, bf16[32,128,1]{1,2,0:T(2,128)(2,1)S(1)} %copy.74), dimensions={2} | concatenate | bytes 3735552 | tf_op jit(solution)/shard_map/cond/branch_1_fun/concatenate | solution.py:112
  217.2 4.7 all-to-all-start.4
  222.5 1.1 fusion.62
  224.3 23.7 %all-to-all-done.4 = bf16[32,128,228]{1,2,0:T(8,128)(2,1)S(1)} async-done(((bf16[32,128,228]{1,2,0:T(8,128)(2,1)}), bf16[32,128,228]{1,2,0:T(8,128)(2,1)S(1)}, u32[]{:S(2)}, u32[]{:S(2)}) %all-to-all-start.4) | async-done | bytes 1867808 | tf_op jit(solution)/shard_map/all_to_all | solution.py:119
  248.6 1.1 fusion.28
  249.8 1.4 convolution_convert_fusion.1
  251.1 4.3 all_to_all.49
  255.5 6.2 %reduce.19 = bf16[32,14336]{1,0:T(8,128)(2,1)S(1)} reduce(bf16[32,1,14336]{2,1,0:T(2,128)(2,1)S(1)} %all_to_all.49, bf16[]{:T(256)} %broadcast.156), dimensions={1}, to_apply=%all_to_all.49.reduce_sub_computation | reduce | bytes 1835010 | tf_op jit(solution)/shard_map/all_to_all | solution.py:31
  261.6 1.6 reshape.331
  263.2 4.9 all-to-all-start.5
  268.2 15.5 %all-to-all-done.5 = bf16[32,2,7168]{2,1,0:T(2,128)(2,1)S(1)} async-done(((bf16[32,2,7168]{2,1,0:T(2,128)(2,1)}), bf16[32,2,7168]{2,1,0:T(2,128)(2,1)S(1)}, u32[]{:S(2)}, u32[]{:S(2)}) %all-to-all-start.5) | async-done | bytes 917536 | tf_op jit(solution)/shard_map/all_to_all | solution.py:31
  283.6 0.7 reshape.332
  284.4 1.9 convert_reduce_fusion
  286.6 5.0 broadcast_in_dim.63
  291.6 23.8 %reduce.20 = bf16[128,14336]{1,0:T(8,128)(2,1)} reduce(bf16[128,1,14336]{2,1,0:T(2,128)(2,1)} %broadcast_in_dim.63, bf16[]{:T(256)} %broadcast.156), dimensions={1}, to_apply=%broadcast_in_dim.63.reduce_sub_computation | reduce | bytes 7340034 | tf_op jit(solution)/shard_map/broadcast_in_dim | solution.py:26
  315.4 8.8 %reshape.333 = bf16[128,2,7168]{2,1,0:T(2,128)(2,1)} reshape(bf16[128,14336]{1,0:T(8,128)(2,1)} %reduce.20) | data formatting | bytes 7340032
  324.2 54.5 %all_to_all.59 = bf16[128,2,7168]{2,1,0:T(2,128)(2,1)} all-to-all(bf16[128,2,7168]{2,1,0:T(2,128)(2,1)} %reshape.333), channel_id=1, replica_groups=mesh['req'=4,'wide'=32] {'req','wide'}, dimensions={0} | all-to-all | bytes 7340032 | tf_op jit(solution)/shard_map/all_to_all | solution.py:27
  378.8 20.5 %reshape.334 = bf16[128,1,14336]{2,1,0:T(2,128)(2,1)} reshape(bf16[128,2,7168]{2,1,0:T(2,128)(2,1)} %all_to_all.59) | data formatting | bytes 7340032
  399.2 23.1 %reduce.14 = bf16[128,14336]{1,0:T(8,128)(2,1)} reduce(bf16[128,1,14336]{2,1,0:T(2,128)(2,1)} %reshape.334, bf16[]{:T(256)} %constant.86), dimensions={1}, to_apply=%all_to_all.45.reduce_sub_computation | reduce | bytes 7340034 | tf_op jit(solution)/shard_map/all_to_all | solution.py:27
  422.4 6.7 %reshape.315 = bf16[512,3584,1]{1,0,2:T(8,128)(2,1)} reshape(bf16[128,14336]{1,0:T(8,128)(2,1)} %reduce.14) | data formatting | bytes 7340032 | tf_op jit(solution)/shard_map/reshape | solution.py:162
  429.1 3.3 convolution_bitcast_fusion
  432.4 3.1 convolution_convert_fusion
  435.5 17.5 %all_to_all.50 = bf16[128,1,14336]{2,1,0:T(2,128)(2,1)} reshape(bf16[512,3584]{1,0:T(8,128)(2,1)} %convolution_convert_fusion) | data formatting | bytes 7340032 | tf_op jit(solution)/shard_map/all_to_all | solution.py:31
  453.0 23.8 %reduce.21 = bf16[128,14336]{1,0:T(8,128)(2,1)} reduce(bf16[128,1,14336]{2,1,0:T(2,128)(2,1)} %all_to_all.50, bf16[]{:T(256)} %broadcast.156), dimensions={1}, to_apply=%all_to_all.50.reduce_sub_computation | reduce | bytes 7340034 | tf_op jit(solution)/shard_map/all_to_all | solution.py:31
  476.7 8.8 %reshape.335 = bf16[128,2,7168]{2,1,0:T(2,128)(2,1)} reshape(bf16[128,14336]{1,0:T(8,128)(2,1)} %reduce.21) | data formatting | bytes 7340032
  485.6 52.9 %all_to_all.60 = bf16[128,2,7168]{2,1,0:T(2,128)(2,1)} all-to-all(bf16[128,2,7168]{2,1,0:T(2,128)(2,1)} %reshape.335), channel_id=1, replica_groups=mesh['req'=4,'wide'=32] {'req','wide'}, dimensions={0} | all-to-all | bytes 7340032 | tf_op jit(solution)/shard_map/all_to_all | solution.py:31
  538.5 20.6 %reshape.336 = bf16[128,1,14336]{2,1,0:T(2,128)(2,1)} reshape(bf16[128,2,7168]{2,1,0:T(2,128)(2,1)} %all_to_all.60) | data formatting | bytes 7340032
  559.1 7.8 %reduce_sum.93 = bf16[14336]{0:T(1024)(128)(2,1)S(1)} reduce(bf16[128,1,14336]{2,1,0:T(2,128)(2,1)} %reshape.336, bf16[]{:T(256)} %constant.74.clone.1), dimensions={0,1}, to_apply=%region_13.14 | reduce | flops 1820672 | bytes 3698690 | tf_op jit(solution)/shard_map/reduce_sum | solution.py:167
  (63 shorter events, 6.9 us)
Async XLA Ops:
  0.6 249.1 %copy-start = (bf16[224,3584]{1,0:T(8,128)(2,1)S(1)}, bf16[224,3584]{1,0:T(8,128)(2,1)}, u32[]{:S(2)}) copy-start(bf16[224,3584]{1,0:T(8,128)(2,1)} %param.23) | copy-start | bytes 4816900
  23.8 34.1 %all-to-all-start = ((bf16[32,2,14336]{2,1,0:T(2,128)(2,1)}), bf16[32,2,14336]{2,1,0:T(2,128)(2,1)S(1)}, u32[]{:S(2)}, u32[]{:S(2)}) async-start(bf16[32,2,14336]{2,1,0:T(2,128)(2,1)} %reshape.325), calls=%async_computation | async-start | bytes 3670016 | tf_op jit(solution)/shard_map/all_to_all | solution.py:27
  82.3 13.4 %all-to-all-start.1 = ((f32[32,1,1536]{2,1,0:T(1,128)}), f32[32,1,1536]{2,1,0:T(1,128)}, u32[]{:S(2)}, u32[]{:S(2)}) async-start(f32[32,1,1536]{2,1,0:T(1,128)} %all_to_all.48), calls=%async_computation.1 | async-start | bytes 393216 | tf_op jit(solution)/shard_map/all_to_all | solution.py:31
  98.7 11.8 %all-to-all-start.2 = ((bf16[32,2,768]{2,1,0:T(2,128)(2,1)}), bf16[32,2,768]{2,1,0:T(2,128)(2,1)S(1)}, u32[]{:S(2)}, u32[]{:S(2)}) async-start(bf16[32,2,768]{2,1,0:T(2,128)(2,1)} %reshape.327), calls=%async_computation.2 | async-start | bytes 196608 | tf_op jit(solution)/shard_map/all_to_all | solution.py:27
  103.1 8.2 %copy-start.5 = (bf16[3,128,224]{1,2,0:T(8,128)(2,1)S(1)}, bf16[3,128,224]{1,2,0:T(8,128)(2,1)}, u32[]{:S(2)}) copy-start(bf16[3,128,224]{1,2,0:T(8,128)(2,1)} %param.22) | copy-start | bytes 516100
  111.5 0.7 copy-start.4
  132.9 31.5 %all-to-all-start.3 = ((bf16[32,2,14336]{2,1,0:T(2,128)(2,1)}), bf16[32,2,14336]{2,1,0:T(2,128)(2,1)S(1)}, u32[]{:S(2)}, u32[]{:S(2)}) async-start(bf16[32,2,14336]{2,1,0:T(2,128)(2,1)} %reshape.329), calls=%async_computation.3 | async-start | bytes 3670016 | tf_op jit(solution)/shard_map/all_to_all | solution.py:27
  138.8 32.1 %copy-start.10 = (s32[1,256]{1,0:T(1,128)S(1)}, s32[1,256]{1,0:T(1,128)}, u32[]{:S(2)}) copy-start(s32[1,256]{1,0:T(1,128)} %param.30) | copy-start | bytes 3076
  197.0 1.9 copy-start.2
  217.2 30.9 %all-to-all-start.4 = ((bf16[32,128,228]{1,2,0:T(8,128)(2,1)}), bf16[32,128,228]{1,2,0:T(8,128)(2,1)S(1)}, u32[]{:S(2)}, u32[]{:S(2)}) async-start(bf16[32,128,228]{1,2,0:T(8,128)(2,1)} %get-tuple-element.121), calls=%async_computation.4 | async-start | bytes 3801088 | tf_op jit(solution)/shard_map/all_to_all | solution.py:119
  223.6 0.6 copy-start.6
  249.7 11.9 %copy-start.7 = (bf16[128,224]{0,1:T(8,128)(2,1)}, bf16[128,224]{0,1:T(8,128)(2,1)S(1)}, u32[]{:S(2)}) copy-start(bf16[128,224]{0,1:T(8,128)(2,1)S(1)} %fusion.28) | copy-start | bytes 172036
  255.4 12.7 %copy-start.8 = (bf16[3584]{0:T(1024)(128)(2,1)S(1)}, bf16[3584]{0:T(1024)(128)(2,1)}, u32[]{:S(2)}) copy-start(bf16[3584]{0:T(1024)(128)(2,1)} %param.24) | copy-start | bytes 21508
  263.2 20.4 %all-to-all-start.5 = ((bf16[32,2,7168]{2,1,0:T(2,128)(2,1)}), bf16[32,2,7168]{2,1,0:T(2,128)(2,1)S(1)}, u32[]{:S(2)}, u32[]{:S(2)}) async-start(bf16[32,2,7168]{2,1,0:T(2,128)(2,1)} %reshape.331), calls=%async_computation.5 | async-start | bytes 1835008 | tf_op jit(solution)/shard_map/all_to_all | solution.py:31
  422.4 6.7 %copy-start.9 = (bf16[2,112,3584]{2,1,0:T(8,128)(2,1)S(1)}, bf16[2,112,3584]{2,1,0:T(8,128)(2,1)}, u32[]{:S(2)}) copy-start(bf16[2,112,3584]{2,1,0:T(8,128)(2,1)} %param.25) | copy-start | bytes 4816900
  429.1 3.3 copy-start.3
  538.5 29.0 %copy-start.1 = (bf16[224,3584]{1,0:T(8,128)(2,1)S(1)}, bf16[224,3584]{1,0:T(8,128)(2,1)}, u32[]{:S(2)}) copy-start(bf16[224,3584]{1,0:T(8,128)(2,1)} %param.23) | copy-start | bytes 4816900

commit v2 on v1

--- a/solution.py
+++ b/solution.py
@@ -22,13 +22,13 @@
 
 
 def gather_rows(piece, axis, count):
-    flat = piece.reshape(1, -1)
-    spread = jnp.broadcast_to(flat, (count, flat.shape[1]))
+    spread = jnp.broadcast_to(piece[None], (count,) + piece.shape)
     return lax.all_to_all(spread, axis, 0, 0, tiled=True)
 
 
 def send_rows(values, axis, count):
-    return lax.all_to_all(values.reshape(count, -1), axis, 0, 0, tiled=True)
+    blocks = values.reshape((count, values.shape[0] // count) + values.shape[1:])
+    return lax.all_to_all(blocks, axis, 0, 0, tiled=True)
 
 
 def split_pair(values):
@@ -74,7 +74,7 @@
     sliced = lax.dynamic_slice_in_dim(shard_rows, feature_start, local_width, 1)
     partial_low = jnp.dot(sliced, adapter_down, preferred_element_type=jnp.float32)
     low_parts = send_rows(partial_low, "wide", wide_size)
-    own_low = jnp.sum(low_parts, axis=0).astype(jnp.bfloat16).reshape(own_rows, 3 * RANK)
+    own_low = jnp.sum(low_parts, axis=0).astype(jnp.bfloat16)
     lowrank = gather_rows(own_low, "wide", wide_size).reshape(SPAN, 3, RANK)
     adapted = jnp.einsum("tcr,crd->tcd", lowrank, adapter_up, preferred_element_type=jnp.float32)
     projected = (base_part.reshape(SPAN, 3, local_width) + adapted).astype(jnp.bfloat16)
@@ -157,7 +157,7 @@
 
     head_out = jnp.dot(attention, out_weight, preferred_element_type=jnp.float32)
     out_parts = send_rows(head_out.astype(jnp.bfloat16), "wide", wide_size)
-    attn_out = jnp.sum(out_parts.astype(jnp.float32), axis=0).reshape(own_rows, -1)
+    attn_out = jnp.sum(out_parts.astype(jnp.float32), axis=0)
     normed_mid = rms_scale(attn_out, mlp_gain)
     every_row = gather_rows(normed_mid, ALL, all_size).reshape(all_size * own_rows, -1)
     both = jnp.einsum("td,cfd->ctf", every_row, gate_up, preferred_element_type=jnp.float32)
@@ -165,7 +165,6 @@
     ffn_part = jnp.dot(hidden, down_weight, preferred_element_type=jnp.float32)
     ffn_parts = send_rows(ffn_part.astype(jnp.bfloat16), ALL, all_size)
     hidden_out = jnp.sum(ffn_parts.astype(jnp.float32), axis=0).astype(jnp.bfloat16)
-    hidden_out = hidden_out.reshape(own_rows, -1)
     return (hidden_out, attention, new_keys, new_values)
 
 

time: 579 us -> 324 us (0.56); the launches traced: 568 us -> 322 us
  other arithmetic: 143 us -> 11.3 us
  local copies, waits for them, and re-layouts: 158 us -> 46.4 us
    unnamed x33 -> x18, local copies, waits for them, and re-layouts: 80.8 us -> 1.32 us
    all_to_all x5 -> x0, other arithmetic: 65.4 us -> none  [the longest x3 35.5 us: gather_rows(): return lax.all_to_all(spread, axis, 0, 0, tiled=True)]
    broadcast_in_dim x4 -> x0, other arithmetic: 49.7 us -> none  [gather_rows(): spread = jnp.broadcast_to(flat, (count, flat.shape[1]))]
    all_to_all x3 -> x0, local copies, waits for them, and re-layouts: 23.6 us -> none  [send_rows(): return lax.all_to_all(values.reshape(count, -1), axis, 0, 0, tiled=True)]
    another operation x3 -> x2, other arithmetic: 11.8 us -> 0.01 us
    broadcast_in_dim x6 -> x4, local copies, waits for them, and re-layouts: 16 us -> 4.82 us  [gather_rows(): spread = jnp.broadcast_to(piece[None], (count,) + piece.shape)]
  transfers between devices with their start and end apart: 6 -> 6, of which waited for: 6 -> 6; matrix products, arithmetic and copies ran while one was open for 2% -> 3% of each run, Pallas kernels for 0% -> 0%
where the time goes in v2:
time: 324 us; the launch traced here: 322 us
  blocking collectives  107 us (33%)
  waiting for transfers between devices  98.5 us (30%)
  local copies, waits for them, and re-layouts  46.4 us (14%)
  starting transfers between devices  31.8 us (10%)
  matrix products  24.9 us (8%)
  other arithmetic  11.3 us (3%)
    all_to_all x1, blocking collectives, gather_rows(): return lax.all_to_all(spread, axis, 0, 0, tiled=True)  54.1 us
    all_to_all x1, blocking collectives, send_rows(): return lax.all_to_all(blocks, axis, 0, 0, tiled=True)  52.9 us
    all_to_all x3, waiting for transfers between devices, gather_rows(): return lax.all_to_all(spread, axis, 0, 0, tiled=True)  52.1 us
    all_to_all x1, waiting for transfers between devices, body(): parts = lax.all_to_all(packed, 'wide', 0, 0, tiled=True)  23.9 us
    all_to_all x2, waiting for transfers between devices, send_rows(): return lax.all_to_all(blocks, axis, 0, 0, tiled=True)  22.6 us
    all_to_all x3, starting transfers between devices, gather_rows(): return lax.all_to_all(spread, axis, 0, 0, tiled=True)  18.2 us
    another operation x7, local copies, waits for them, and re-layouts  12.5 us
    reshape x3, local copies, waits for them, and re-layouts, send_rows(): values.reshape((count, values.shape[0] // count) + values.shape[1:])  9.8 us
  transfers between devices with their start and end apart: 6, of which 6 were waited for; matrix products, arithmetic and copies ran while one was open for 3% of the time, Pallas kernels for 0%

profile of v2, /device:TPU:1, one launch (start us, length us, event | category | flops | bytes accessed | tf_op | source)
XLA Modules:
  0.0 322.3 jit_solution(15551461872994721662)
XLA Ops:
  0.6 0.0 copy-start
  0.6 0.8 convert_element_type.82
  1.5 1.0 fusion.33
  2.5 0.9 fusion.35
  3.4 1.7 broadcast_in_dim.30
  5.1 8.6 %all-to-all-start = ((bf16[32,4,7168]{2,1,0:T(4,128)(2,1)}), bf16[32,4,7168]{2,1,0:T(4,128)(2,1)S(1)}, u32[]{:S(2)}, u32[]{:S(2)}) async-start(bf16[32,4,7168]{2,1,0:T(4,128)(2,1)} %broadcast_in_dim.30), calls=%async_computation | async-start | bytes 3670016 | tf_op jit(solution)/shard_map/all_to_all | solution.py:26
  13.7 25.5 %all-to-all-done = bf16[32,4,7168]{2,1,0:T(4,128)(2,1)S(1)} async-done(((bf16[32,4,7168]{2,1,0:T(4,128)(2,1)}), bf16[32,4,7168]{2,1,0:T(4,128)(2,1)S(1)}, u32[]{:S(2)}, u32[]{:S(2)}) %all-to-all-start) | async-done | bytes 1835040 | tf_op jit(solution)/shard_map/all_to_all | solution.py:26
  39.2 1.5 reshape.269
  40.7 1.9 fusion.39
  42.6 1.7 reshape.271
  44.2 4.9 %all-to-all-start.1 = ((f32[32,4,384]{2,1,0:T(4,128)}), f32[32,4,384]{2,1,0:T(4,128)}, u32[]{:S(2)}, u32[]{:S(2)}) async-start(f32[32,4,384]{2,1,0:T(4,128)} %reshape.271), calls=%async_computation.1 | async-start | bytes 393216 | tf_op jit(solution)/shard_map/all_to_all | solution.py:31
  49.1 1.5 reshape.280
  50.6 7.0 %all-to-all-done.1 = f32[32,4,384]{2,1,0:T(4,128)} async-done(((f32[32,4,384]{2,1,0:T(4,128)}), f32[32,4,384]{2,1,0:T(4,128)}, u32[]{:S(2)}, u32[]{:S(2)}) %all-to-all-start.1) | async-done | bytes 196640 | tf_op jit(solution)/shard_map/all_to_all | solution.py:31
  57.6 1.0 reduce_sum.87
  58.6 0.7 broadcast_in_dim.31
  59.2 3.8 %all-to-all-start.2 = ((bf16[32,4,384]{2,1,0:T(4,128)(2,1)}), bf16[32,4,384]{2,1,0:T(4,128)(2,1)S(1)}, u32[]{:S(2)}, u32[]{:S(2)}) async-start(bf16[32,4,384]{2,1,0:T(4,128)(2,1)} %broadcast_in_dim.31), calls=%async_computation.2 | async-start | bytes 196608 | tf_op jit(solution)/shard_map/all_to_all | solution.py:26
  63.0 0.0 copy-start.4
  63.1 5.9 %fusion.21 = f32[128,3,224]{0,2,1:T(8,128)S(1)} fusion(bf16[128,7168,1]{1,0,2:T(8,128)(2,1)} %reshape.280, bf16[7168,3,224]{0,2,1:T(8,128)(2,1)} %param.20), kind=kOutput, calls=%fused_computation.28 | convolution fusion | flops 1233125376 | bytes 11812864 | tf_op jit(solution)/shard_map/dot_general | solution.py:71
  68.9 0.0 copy-start.9
  68.9 1.7 all-to-all-done.2
  70.7 0.0 copy-done.4
  70.7 0.2 fusion.24
  70.9 0.0 copy-start.3
  70.9 0.7 copy-done.3
  71.6 0.7 slice_bitcast_fusion.2
  72.2 1.5 broadcast_in_dim.33
  73.7 5.8 %all-to-all-start.3 = ((bf16[32,128,224]{1,2,0:T(8,128)(2,1)}), bf16[32,128,224]{1,2,0:T(8,128)(2,1)S(1)}, u32[]{:S(2)}, u32[]{:S(2)}) async-start(bf16[32,128,224]{1,2,0:T(8,128)(2,1)} %broadcast_in_dim.33), calls=%async_computation.3 | async-start | bytes 3670016 | tf_op jit(solution)/shard_map/all_to_all | solution.py:26
  80.2 24.9 %all-to-all-done.3 = bf16[32,128,224]{1,2,0:T(8,128)(2,1)S(1)} async-done(((bf16[32,128,224]{1,2,0:T(8,128)(2,1)}), bf16[32,128,224]{1,2,0:T(8,128)(2,1)S(1)}, u32[]{:S(2)}, u32[]{:S(2)}) %all-to-all-start.3) | async-done | bytes 1835040 | tf_op jit(solution)/shard_map/all_to_all | solution.py:26
  105.1 0.0 copy-done.9
  105.1 30.2 %conditional.1 = (bf16[32,128,228]{1,2,0:T(8,128)(2,1)}) conditional(s32[]{:T(128)} %convert_element_type.80, () %tuple.18, (s32[]{:T(128)}, bf16[1,256,7168]{2,1,0:T(8,128)(2,1)}, bf16[32,128,224]{1,2,0:T(8,128)(2,1)S(1)}, bf16[1,256,7168]{2,1,0:T(8,128)(2,1)}, s32[1,256]{1,0:T(1,128)S(1)}, /*index=5*/s32[]{:T(128)}, s32[256]{0:T(256)S(1)}) %tuple.36), branch_computations={%region_2.3_spmd, %region_3.6_spmd.clone} | conditional | flops 954123264 | bytes 59018796 | solution.py:118
  105.1 0.7 compare_and_fusion
  105.8 5.9 %copy.39 = bf16[1,256,7168]{1,2,0:T(8,128)(2,1)} copy(bf16[1,256,7168]{2,1,0:T(8,128)(2,1)} %get-tuple-element.78) | data formatting | bytes 7340032 | tf_op jit(solution)/shard_map
  111.7 3.5 %fusion = (f32[32,128]{1,0:T(8,128)S(1)}, f32[32,128,256]{2,1,0:T(8,128)S(1)}) fusion(pred[256]{0:T(512)(128)(4,1)S(1)} %compare_and_fusion, bf16[32,128,224]{1,2,0:T(8,128)(2,1)S(1)} %get-tuple-element.49, bf16[256,32,224]{0,2,1:T(8,128)(2,1)} %bitcast.95), kind=kOutput, calls=%fused_computation.2 | convolution fusion | flops 472903680 | bytes 9715968 | tf_op jit(solution)/shard_map/cond/branch_1_fun/hqd,khd->hqk/dot_general | solution.py:95
  115.2 0.0 copy-start.1
  115.2 1.9 copy-done.1
  117.1 1.5 fusion.1
  118.7 5.9 %copy.40 = bf16[1,256,7168]{1,2,0:T(8,128)(2,1)} copy(bf16[1,256,7168]{2,1,0:T(8,128)(2,1)} %get-tuple-element.80) | data formatting | bytes 7340032 | tf_op jit(solution)/shard_map
  124.6 4.5 %fusion.10 = bf16[32,128,224]{1,2,0:T(8,128)(2,1)S(1)} fusion(bf16[256,32,224]{0,2,1:T(8,128)(2,1)} %bitcast.96, f32[32,128,256]{2,1,0:T(8,128)} %copy-done.1, f32[32,128]{1,0:T(8,128)S(1)} %reduce-precision_add_fusion, pred[256]{0:T(512)(128)(4,1)S(1)} %compare_and_fusion), kind=kOutput, calls=%fused_computation.11 | convolution fusion | flops 475922432 | bytes 9715968 | tf_op jit(solution)/shard_map/cond/branch_1_fun/hqk,khd->hqd/dot_general | solution.py:104
  129.2 6.1 %concatenate.7 = bf16[32,128,228]{1,2,0:T(8,128)(2,1)} concatenate(bf16[32,128,224]{1,2,0:T(8,128)(2,1)S(1)} %fusion.10, bf16[32,128,1]{1,2,0:T(2,128)(2,1)S(1)} %copy.34, bf16[32,128,1]{1,2,0:T(2,128)(2,1)S(1)} %copy.35, bf16[32,128,1]{1,2,0:T(2,128)(2,1)S(1)} %copy.36, bf16[32,128,1]{1,2,0:T(2,128)(2,1)S(1)} %copy.37), dimensions={2} | concatenate | bytes 3735552 | tf_op jit(solution)/shard_map/cond/branch_1_fun/concatenate | solution.py:112
  135.3 4.4 %all-to-all-start.4 = ((bf16[32,128,228]{1,2,0:T(8,128)(2,1)}), bf16[32,128,228]{1,2,0:T(8,128)(2,1)S(1)}, u32[]{:S(2)}, u32[]{:S(2)}) async-start(bf16[32,128,228]{1,2,0:T(8,128)(2,1)} %get-tuple-element.99), calls=%async_computation.4 | async-start | bytes 3801088 | tf_op jit(solution)/shard_map/all_to_all | solution.py:119
  140.4 1.1 fusion.59
  141.4 0.6 copy-done.5
  142.0 0.1 fusion.43
  142.2 23.9 %all-to-all-done.4 = bf16[32,128,228]{1,2,0:T(8,128)(2,1)S(1)} async-done(((bf16[32,128,228]{1,2,0:T(8,128)(2,1)}), bf16[32,128,228]{1,2,0:T(8,128)(2,1)S(1)}, u32[]{:S(2)}, u32[]{:S(2)}) %all-to-all-start.4) | async-done | bytes 1867808 | tf_op jit(solution)/shard_map/all_to_all | solution.py:119
  166.2 0.4 multiply_reduce_fusion
  166.6 0.0 copy-start.7
  166.6 1.1 fusion.28
  167.7 0.0 copy-done
  167.7 0.0 copy-start.6
  167.7 0.4 convolution_convert_fusion.1
  168.2 1.1 reshape.277
  169.3 4.4 %all-to-all-start.5 = ((bf16[32,4,3584]{2,1,0:T(4,128)(2,1)}), bf16[32,4,3584]{2,1,0:T(4,128)(2,1)S(1)}, u32[]{:S(2)}, u32[]{:S(2)}) async-start(bf16[32,4,3584]{2,1,0:T(4,128)(2,1)} %reshape.277), calls=%async_computation.5 | async-start | bytes 1835008 | tf_op jit(solution)/shard_map/all_to_all | solution.py:31
  173.7 15.6 %all-to-all-done.5 = bf16[32,4,3584]{2,1,0:T(4,128)(2,1)S(1)} async-done(((bf16[32,4,3584]{2,1,0:T(4,128)(2,1)}), bf16[32,4,3584]{2,1,0:T(4,128)(2,1)S(1)}, u32[]{:S(2)}, u32[]{:S(2)}) %all-to-all-start.5) | async-done | bytes 917536 | tf_op jit(solution)/shard_map/all_to_all | solution.py:31
  189.3 0.4 convert_reduce_fusion
  189.7 0.1 multiply_reduce_fusion.1
  189.8 0.1 multiply_convert_fusion
  189.9 0.9 broadcast_in_dim.63
  190.9 54.1 %all_to_all.40 = bf16[128,4,3584]{2,1,0:T(4,128)(2,1)} all-to-all(bf16[128,4,3584]{2,1,0:T(4,128)(2,1)S(1)} %broadcast_in_dim.63), channel_id=1, replica_groups=mesh['req'=4,'wide'=32] {'req','wide'}, dimensions={0} | all-to-all | bytes 7340032 | tf_op jit(solution)/shard_map/all_to_all | solution.py:26
  245.0 6.9 %reshape.281 = bf16[512,3584,1]{1,0,2:T(8,128)(2,1)} reshape(bf16[128,4,3584]{2,1,0:T(4,128)(2,1)} %all_to_all.40) | data formatting | bytes 7340032 | tf_op jit(solution)/shard_map/reshape | solution.py:162
  251.9 3.3 %convolution_bitcast_fusion = f32[2,512,112]{1,2,0:T(8,128)S(1)} fusion(bf16[512,3584,1]{1,0,2:T(8,128)(2,1)} %reshape.281, bf16[2,112,3584]{2,1,0:T(8,128)(2,1)S(1)} %copy-done.8), kind=kOutput, calls=%fused_computation.34 | convolution fusion | flops 822083584 | bytes 5734400 | tf_op jit(solution)/shard_map/td,cfd->ctf/dot_general | solution.py:163
  255.2 3.0 convolution_convert_fusion
  258.2 7.0 %reshape.279 = bf16[128,4,3584]{2,1,0:T(4,128)(2,1)} reshape(bf16[512,3584]{1,0:T(8,128)(2,1)} %convolution_convert_fusion) | data formatting | bytes 7340032 | tf_op jit(solution)/shard_map/reshape | solution.py:30
  265.2 52.9 %all_to_all.41 = bf16[128,4,3584]{2,1,0:T(4,128)(2,1)} all-to-all(bf16[128,4,3584]{2,1,0:T(4,128)(2,1)} %reshape.279), channel_id=1, replica_groups=mesh['req'=4,'wide'=32] {'req','wide'}, dimensions={0} | all-to-all | bytes 7340032 | tf_op jit(solution)/shard_map/all_to_all | solution.py:31
  318.1 4.1 %reduce_sum.93 = bf16[4,3584]{1,0:T(4,128)(2,1)} reduce(bf16[128,4,3584]{2,1,0:T(4,128)(2,1)} %all_to_all.41, bf16[]{:T(256)} %constant.74.clone.1), dimensions={0}, to_apply=%region_13.14 | reduce | flops 1820672 | bytes 3698690 | tf_op jit(solution)/shard_map/reduce_sum | solution.py:167
  (28 shorter events, 0.3 us)
Async XLA Ops:
  0.6 167.1 %copy-start = (bf16[224,3584]{1,0:T(8,128)(2,1)S(1)}, bf16[224,3584]{1,0:T(8,128)(2,1)}, u32[]{:S(2)}) copy-start(bf16[224,3584]{1,0:T(8,128)(2,1)} %param.23) | copy-start | bytes 4816900
  5.1 34.1 %all-to-all-start = ((bf16[32,4,7168]{2,1,0:T(4,128)(2,1)}), bf16[32,4,7168]{2,1,0:T(4,128)(2,1)S(1)}, u32[]{:S(2)}, u32[]{:S(2)}) async-start(bf16[32,4,7168]{2,1,0:T(4,128)(2,1)} %broadcast_in_dim.30), calls=%async_computation | async-start | bytes 3670016 | tf_op jit(solution)/shard_map/all_to_all | solution.py:26
  44.2 13.4 %all-to-all-start.1 = ((f32[32,4,384]{2,1,0:T(4,128)}), f32[32,4,384]{2,1,0:T(4,128)}, u32[]{:S(2)}, u32[]{:S(2)}) async-start(f32[32,4,384]{2,1,0:T(4,128)} %reshape.271), calls=%async_computation.1 | async-start | bytes 393216 | tf_op jit(solution)/shard_map/all_to_all | solution.py:31
  59.2 11.4 %all-to-all-start.2 = ((bf16[32,4,384]{2,1,0:T(4,128)(2,1)}), bf16[32,4,384]{2,1,0:T(4,128)(2,1)S(1)}, u32[]{:S(2)}, u32[]{:S(2)}) async-start(bf16[32,4,384]{2,1,0:T(4,128)(2,1)} %broadcast_in_dim.31), calls=%async_computation.2 | async-start | bytes 196608 | tf_op jit(solution)/shard_map/all_to_all | solution.py:26
  63.0 7.6 %copy-start.4 = (bf16[3,128,224]{1,2,0:T(8,128)(2,1)S(1)}, bf16[3,128,224]{1,2,0:T(8,128)(2,1)}, u32[]{:S(2)}) copy-start(bf16[3,128,224]{1,2,0:T(8,128)(2,1)} %param.22) | copy-start | bytes 516100
  68.9 36.1 %copy-start.9 = (s32[1,256]{1,0:T(1,128)S(1)}, s32[1,256]{1,0:T(1,128)}, u32[]{:S(2)}) copy-start(s32[1,256]{1,0:T(1,128)} %param.30) | copy-start | bytes 3076
  70.9 0.7 copy-start.3
  73.7 31.4 %all-to-all-start.3 = ((bf16[32,128,224]{1,2,0:T(8,128)(2,1)}), bf16[32,128,224]{1,2,0:T(8,128)(2,1)S(1)}, u32[]{:S(2)}, u32[]{:S(2)}) async-start(bf16[32,128,224]{1,2,0:T(8,128)(2,1)} %broadcast_in_dim.33), calls=%async_computation.3 | async-start | bytes 3670016 | tf_op jit(solution)/shard_map/all_to_all | solution.py:26
  115.2 1.9 copy-start.1
  135.3 30.7 %all-to-all-start.4 = ((bf16[32,128,228]{1,2,0:T(8,128)(2,1)}), bf16[32,128,228]{1,2,0:T(8,128)(2,1)S(1)}, u32[]{:S(2)}, u32[]{:S(2)}) async-start(bf16[32,128,228]{1,2,0:T(8,128)(2,1)} %get-tuple-element.99), calls=%async_computation.4 | async-start | bytes 3801088 | tf_op jit(solution)/shard_map/all_to_all | solution.py:119
  141.4 0.6 copy-start.5
  166.6 7.1 %copy-start.7 = (bf16[3584]{0:T(1024)(128)(2,1)S(1)}, bf16[3584]{0:T(1024)(128)(2,1)}, u32[]{:S(2)}) copy-start(bf16[3584]{0:T(1024)(128)(2,1)} %param.24) | copy-start | bytes 21508
  167.7 22.2 %copy-start.6 = (bf16[128,224]{0,1:T(8,128)(2,1)}, bf16[128,224]{0,1:T(8,128)(2,1)S(1)}, u32[]{:S(2)}) copy-start(bf16[128,224]{0,1:T(8,128)(2,1)S(1)} %fusion.28) | copy-start | bytes 172036
  169.3 20.0 %all-to-all-start.5 = ((bf16[32,4,3584]{2,1,0:T(4,128)(2,1)}), bf16[32,4,3584]{2,1,0:T(4,128)(2,1)S(1)}, u32[]{:S(2)}, u32[]{:S(2)}) async-start(bf16[32,4,3584]{2,1,0:T(4,128)(2,1)} %reshape.277), calls=%async_computation.5 | async-start | bytes 1835008 | tf_op jit(solution)/shard_map/all_to_all | solution.py:31
  245.0 6.9 %copy-start.8 = (bf16[2,112,3584]{2,1,0:T(8,128)(2,1)S(1)}, bf16[2,112,3584]{2,1,0:T(8,128)(2,1)}, u32[]{:S(2)}) copy-start(bf16[2,112,3584]{2,1,0:T(8,128)(2,1)} %param.25) | copy-start | bytes 4816900
  251.9 3.3 %copy-start.2 = (bf16[112,3584]{1,0:T(8,128)(2,1)S(1)}, bf16[112,3584]{1,0:T(8,128)(2,1)}, u32[]{:S(2)}) copy-start(bf16[112,3584]{1,0:T(8,128)(2,1)} %param.26) | copy-start | bytes 2408452

commit v3 on v2

--- a/solution.py
+++ b/solution.py
@@ -12,7 +12,8 @@
 
 EPSILON = 1e-05
 NEG_LARGE = -1e30
-ALL = ("req", "wide")
+WIDE = ("chip", "core")
+HALF = ("req", "chip")
 
 
 def rms_scale(values, gains):
@@ -58,31 +59,35 @@
     span_counts,
 ):
     score_scale = HD ** (-0.5)
-    wide_size = lax.psum(1, "wide")
-    all_size = lax.psum(1, ALL)
+    wide_size = lax.psum(1, WIDE)
+    half_size = lax.psum(1, HALF)
     local_width = qkv_weight.shape[2]
     local_heads = local_width // HD
     own_rows = tokens.shape[0]
-    wide_index = lax.axis_index("wide")
+    wide_index = lax.axis_index(WIDE)
     feature_start = wide_index * local_width
 
+    swap = [(0, 1), (1, 0)]
+    chip_gate = jnp.concatenate([gate_up, lax.ppermute(gate_up, "core", swap)], axis=1)
+    chip_down = jnp.concatenate([down_weight, lax.ppermute(down_weight, "core", swap)], axis=0)
+
     normed = rms_scale(tokens, attn_gain)
-    shard_rows = gather_rows(normed, "wide", wide_size).reshape(SPAN, D)
+    shard_rows = gather_rows(normed, WIDE, wide_size).reshape(SPAN, D)
     base_part = jnp.dot(
         shard_rows, qkv_weight.reshape(D, 3 * local_width), preferred_element_type=jnp.float32
     )
     sliced = lax.dynamic_slice_in_dim(shard_rows, feature_start, local_width, 1)
     partial_low = jnp.dot(sliced, adapter_down, preferred_element_type=jnp.float32)
-    low_parts = send_rows(partial_low, "wide", wide_size)
+    low_parts = send_rows(partial_low, WIDE, wide_size)
     own_low = jnp.sum(low_parts, axis=0).astype(jnp.bfloat16)
-    lowrank = gather_rows(own_low, "wide", wide_size).reshape(SPAN, 3, RANK)
+    lowrank = gather_rows(own_low, WIDE, wide_size).reshape(SPAN, 3, RANK)
     adapted = jnp.einsum("tcr,crd->tcd", lowrank, adapter_up, preferred_element_type=jnp.float32)
     projected = (base_part.reshape(SPAN, 3, local_width) + adapted).astype(jnp.bfloat16)
     query_own = projected[:, 0]
     new_keys = projected[:, 1]
     new_values = projected[:, 2]
 
-    query_heads = gather_rows(query_own, "wide", wide_size).reshape(HEADS, SPAN, HD)
+    query_heads = gather_rows(query_own, WIDE, wide_size).reshape(HEADS, SPAN, HD)
     block_len = key_cache.shape[1]
     block_start = wide_index * block_len
     length = cache_lengths[0]
@@ -116,7 +121,7 @@
         return jnp.concatenate([jnp.zeros((HEADS, SPAN, HD), jnp.bfloat16), stats], axis=-1)
 
     packed = lax.cond(block_start < length, cache_block, skipped, 0)
-    parts = lax.all_to_all(packed, "wide", 0, 0, tiled=True)
+    parts = lax.all_to_all(packed, WIDE, 0, 0, tiled=True)
     part_num = parts[..., :HD].astype(jnp.float32)
     part_max = join_pair(parts[..., HD], parts[..., HD + 1])
     part_sum = join_pair(parts[..., HD + 2], parts[..., HD + 3])
@@ -156,38 +161,42 @@
     attention = (numerator / totals[:, None]).astype(jnp.bfloat16)
 
     head_out = jnp.dot(attention, out_weight, preferred_element_type=jnp.float32)
-    out_parts = send_rows(head_out.astype(jnp.bfloat16), "wide", wide_size)
+    out_parts = send_rows(head_out.astype(jnp.bfloat16), WIDE, wide_size)
     attn_out = jnp.sum(out_parts.astype(jnp.float32), axis=0)
     normed_mid = rms_scale(attn_out, mlp_gain)
-    every_row = gather_rows(normed_mid, ALL, all_size).reshape(all_size * own_rows, -1)
-    both = jnp.einsum("td,cfd->ctf", every_row, gate_up, preferred_element_type=jnp.float32)
+    half_rows = gather_rows(normed_mid, HALF, half_size).reshape(half_size * own_rows, -1)
+    both = jnp.einsum("td,cfd->ctf", half_rows, chip_gate, preferred_element_type=jnp.float32)
     hidden = (jax.nn.silu(both[0]) * both[1]).astype(jnp.bfloat16)
-    ffn_part = jnp.dot(hidden, down_weight, preferred_element_type=jnp.float32)
-    ffn_parts = send_rows(ffn_part.astype(jnp.bfloat16), ALL, all_size)
+    ffn_part = jnp.dot(hidden, chip_down, preferred_element_type=jnp.float32)
+    ffn_parts = send_rows(ffn_part.astype(jnp.bfloat16), HALF, half_size)
     hidden_out = jnp.sum(ffn_parts.astype(jnp.float32), axis=0).astype(jnp.bfloat16)
     return (hidden_out, attention, new_keys, new_values)
 
 
 def solution(mesh):
+    chips = mesh.shape["wide"] // 2
+    split_mesh = jax.sharding.Mesh(
+        mesh.devices.reshape(mesh.shape["req"], chips, 2), ("req", "chip", "core")
+    )
     return jax.shard_map(
         body,
-        mesh=mesh,
+        mesh=split_mesh,
         in_specs=(
-            P(("req", "wide"), None),
+            P(("req",) + WIDE, None),
             P(),
-            P(None, None, "wide"),
-            P("wide", None),
-            P(None, None, "wide"),
-            P("wide", None),
+            P(None, None, WIDE),
+            P(WIDE, None),
+            P(None, None, WIDE),
+            P(WIDE, None),
             P(),
-            P(None, ("req", "wide"), None),
-            P(("req", "wide"), None),
-            P("req", "wide", None),
-            P("req", "wide", None),
+            P(None, ("req",) + WIDE, None),
+            P(("req",) + WIDE, None),
+            P("req", WIDE, None),
+            P("req", WIDE, None),
             P("req"),
-            P("req", "wide"),
+            P("req", WIDE),
             P("req"),
         ),
-        out_specs=(P(("req", "wide"), None), P("req", "wide"), P("req", "wide"), P("req", "wide")),
+        out_specs=(P(("req",) + WIDE, None), P("req", WIDE), P("req", WIDE), P("req", WIDE)),
         check_vma=False,
     )

time: 324 us -> 272 us (0.84)
  blocking collectives: 107 us -> 30.1 us
  waiting for transfers between devices: 98.5 us -> 123 us
  local copies, waits for them, and re-layouts: 46.4 us -> 37.8 us
  starting transfers between devices: 31.8 us -> 40.2 us
    all_to_all x1 -> x0, blocking collectives: 54.1 us -> none  [gather_rows(): return lax.all_to_all(spread, axis, 0, 0, tiled=True)]
    all_to_all x3 -> x4, waiting for transfers between devices: 52.1 us -> 76.6 us  [gather_rows(): return lax.all_to_all(spread, axis, 0, 0, tiled=True)]
    all_to_all x1, blocking collectives: 52.9 us -> 30.1 us  [send_rows(): return lax.all_to_all(blocks, axis, 0, 0, tiled=True)]
    all_to_all x3 -> x4, starting transfers between devices: 18.2 us -> 25.7 us  [gather_rows(): return lax.all_to_all(spread, axis, 0, 0, tiled=True)]
    reshape x4, local copies, waits for them, and re-layouts: 9.85 us -> 4.45 us  [the longest x2 2.94 us: body(): shard_rows = gather_rows(normed, WIDE, wide_size).reshape(SPAN, D)]
    reshape x3, local copies, waits for them, and re-layouts: 9.8 us -> 5.92 us  [send_rows(): values.reshape((count, values.shape[0] // count) + values.shape[1:])]
  transfers between devices with their start and end apart: 6 -> 9, of which waited for: 6 -> 7; matrix products, arithmetic and copies ran while one was open for 3% -> 5% of each run, Pallas kernels for 0% -> 0%
where the time goes in v3:
time: 272 us; the launch traced here: 269 us
  waiting for transfers between devices  123 us (45%)
  starting transfers between devices  40.2 us (15%)
  local copies, waits for them, and re-layouts  37.8 us (14%)
  blocking collectives  30.1 us (11%)
  matrix products  25.3 us (9%)
  other arithmetic  10 us (4%)
    all_to_all x4, waiting for transfers between devices, gather_rows(): return lax.all_to_all(spread, axis, 0, 0, tiled=True)  76.6 us
    all_to_all x1, blocking collectives, send_rows(): return lax.all_to_all(blocks, axis, 0, 0, tiled=True)  30.1 us
    all_to_all x4, starting transfers between devices, gather_rows(): return lax.all_to_all(spread, axis, 0, 0, tiled=True)  25.7 us
    all_to_all x1, waiting for transfers between devices, body(): parts = lax.all_to_all(packed, WIDE, 0, 0, tiled=True)  23.9 us
    all_to_all x2, waiting for transfers between devices, send_rows(): return lax.all_to_all(blocks, axis, 0, 0, tiled=True)  22.6 us
    another operation x7, local copies, waits for them, and re-layouts  12.5 us
    all_to_all x2, starting transfers between devices, send_rows(): return lax.all_to_all(blocks, axis, 0, 0, tiled=True)  9.21 us
    concatenate x1, local copies, waits for them, and re-layouts, cache_block(): return jnp.concatenate([numerator.astype(jnp.bfloat16), stats], axis=-1)  6.1 us
  transfers between devices with their start and end apart: 9, of which 7 were waited for; matrix products, arithmetic and copies ran while one was open for 5% of the time, Pallas kernels for 0%

profile of v3, /device:TPU:1, one launch (start us, length us, event | category | flops | bytes accessed | tf_op | source)
XLA Modules:
  0.0 268.8 jit_solution(1340511306483185721)
XLA Ops:
  0.6 0.0 copy-start
  0.6 0.8 convert_element_type.82
  1.5 1.0 fusion.43
  2.5 0.9 fusion.45
  3.4 1.7 broadcast_in_dim.30
  5.1 8.6 %all-to-all-start = ((bf16[32,4,7168]{2,1,0:T(4,128)(2,1)}), bf16[32,4,7168]{2,1,0:T(4,128)(2,1)S(1)}, u32[]{:S(2)}, u32[]{:S(2)}) async-start(bf16[32,4,7168]{2,1,0:T(4,128)(2,1)} %broadcast_in_dim.30), calls=%async_computation | async-start | bytes 3670016 | tf_op jit(solution)/shard_map/all_to_all | solution.py:27
  13.7 25.5 %all-to-all-done = bf16[32,4,7168]{2,1,0:T(4,128)(2,1)S(1)} async-done(((bf16[32,4,7168]{2,1,0:T(4,128)(2,1)}), bf16[32,4,7168]{2,1,0:T(4,128)(2,1)S(1)}, u32[]{:S(2)}, u32[]{:S(2)}) %all-to-all-start) | async-done | bytes 1835040 | tf_op jit(solution)/shard_map/all_to_all | solution.py:27
  39.2 1.5 reshape.269
  40.7 1.9 fusion.49
  42.6 1.7 reshape.271
  44.2 4.9 %all-to-all-start.1 = ((f32[32,4,384]{2,1,0:T(4,128)}), f32[32,4,384]{2,1,0:T(4,128)}, u32[]{:S(2)}, u32[]{:S(2)}) async-start(f32[32,4,384]{2,1,0:T(4,128)} %reshape.271), calls=%async_computation.1 | async-start | bytes 393216 | tf_op jit(solution)/shard_map/all_to_all | solution.py:32
  49.1 1.5 reshape.280
  50.6 7.0 %all-to-all-done.1 = f32[32,4,384]{2,1,0:T(4,128)} async-done(((f32[32,4,384]{2,1,0:T(4,128)}), f32[32,4,384]{2,1,0:T(4,128)}, u32[]{:S(2)}, u32[]{:S(2)}) %all-to-all-start.1) | async-done | bytes 196640 | tf_op jit(solution)/shard_map/all_to_all | solution.py:32
  57.6 1.0 reduce_sum.87
  58.6 0.7 broadcast_in_dim.31
  59.2 3.8 %all-to-all-start.2 = ((bf16[32,4,384]{2,1,0:T(4,128)(2,1)}), bf16[32,4,384]{2,1,0:T(4,128)(2,1)S(1)}, u32[]{:S(2)}, u32[]{:S(2)}) async-start(bf16[32,4,384]{2,1,0:T(4,128)(2,1)} %broadcast_in_dim.31), calls=%async_computation.2 | async-start | bytes 196608 | tf_op jit(solution)/shard_map/all_to_all | solution.py:27
  63.0 0.0 copy-start.3
  63.1 5.9 %fusion.21 = f32[128,3,224]{0,2,1:T(8,128)S(1)} fusion(bf16[128,7168,1]{1,0,2:T(8,128)(2,1)} %reshape.280, bf16[7168,3,224]{0,2,1:T(8,128)(2,1)} %param.20), kind=kOutput, calls=%fused_computation.28 | convolution fusion | flops 1233125376 | bytes 11812864 | tf_op jit(solution)/shard_map/dot_general | solution.py:76
  68.9 1.7 all-to-all-done.2
  70.7 0.0 copy-start.8
  70.7 0.2 fusion.34
  70.9 0.7 copy-done.2
  71.6 0.7 slice_bitcast_fusion.2
  72.2 1.5 broadcast_in_dim.33
  73.7 5.8 %all-to-all-start.3 = ((bf16[32,128,224]{1,2,0:T(8,128)(2,1)}), bf16[32,128,224]{1,2,0:T(8,128)(2,1)S(1)}, u32[]{:S(2)}, u32[]{:S(2)}) async-start(bf16[32,128,224]{1,2,0:T(8,128)(2,1)} %broadcast_in_dim.33), calls=%async_computation.3 | async-start | bytes 3670016 | tf_op jit(solution)/shard_map/all_to_all | solution.py:27
  80.2 24.9 %all-to-all-done.3 = bf16[32,128,224]{1,2,0:T(8,128)(2,1)S(1)} async-done(((bf16[32,128,224]{1,2,0:T(8,128)(2,1)}), bf16[32,128,224]{1,2,0:T(8,128)(2,1)S(1)}, u32[]{:S(2)}, u32[]{:S(2)}) %all-to-all-start.3) | async-done | bytes 1835040 | tf_op jit(solution)/shard_map/all_to_all | solution.py:27
  105.1 30.2 %conditional.1 = (bf16[32,128,228]{1,2,0:T(8,128)(2,1)}) conditional(s32[]{:T(128)} %convert_element_type.80, () %tuple.18, (s32[]{:T(128)}, bf16[1,256,7168]{2,1,0:T(8,128)(2,1)}, bf16[32,128,224]{1,2,0:T(8,128)(2,1)S(1)}, bf16[1,256,7168]{2,1,0:T(8,128)(2,1)}, s32[1,256]{1,0:T(1,128)S(1)}, /*index=5*/s32[]{:T(128)}, s32[256]{0:T(256)S(1)}) %tuple.36), branch_computations={%region_2.3_spmd, %region_3.6_spmd.clone} | conditional | flops 954123264 | bytes 59018796 | solution.py:123
  105.1 0.7 compare_and_fusion
  105.8 5.9 %copy.39 = bf16[1,256,7168]{1,2,0:T(8,128)(2,1)} copy(bf16[1,256,7168]{2,1,0:T(8,128)(2,1)} %get-tuple-element.78) | data formatting | bytes 7340032 | tf_op jit(solution)/shard_map
  111.7 3.5 %fusion = (f32[32,128]{1,0:T(8,128)S(1)}, f32[32,128,256]{2,1,0:T(8,128)S(1)}) fusion(pred[256]{0:T(512)(128)(4,1)S(1)} %compare_and_fusion, bf16[32,128,224]{1,2,0:T(8,128)(2,1)S(1)} %get-tuple-element.49, bf16[256,32,224]{0,2,1:T(8,128)(2,1)} %bitcast.93), kind=kOutput, calls=%fused_computation.2 | convolution fusion | flops 472903680 | bytes 9715968 | tf_op jit(solution)/shard_map/cond/branch_1_fun/hqd,khd->hqk/dot_general | solution.py:100
  115.2 1.9 copy-done.1
  117.1 1.5 fusion.1
  118.7 5.9 %copy.40 = bf16[1,256,7168]{1,2,0:T(8,128)(2,1)} copy(bf16[1,256,7168]{2,1,0:T(8,128)(2,1)} %get-tuple-element.80) | data formatting | bytes 7340032 | tf_op jit(solution)/shard_map
  124.6 4.5 %fusion.10 = bf16[32,128,224]{1,2,0:T(8,128)(2,1)S(1)} fusion(bf16[256,32,224]{0,2,1:T(8,128)(2,1)} %bitcast.94, f32[32,128,256]{2,1,0:T(8,128)} %copy-done.1, f32[32,128]{1,0:T(8,128)S(1)} %reduce-precision_add_fusion, pred[256]{0:T(512)(128)(4,1)S(1)} %compare_and_fusion), kind=kOutput, calls=%fused_computation.11 | convolution fusion | flops 475922432 | bytes 9715968 | tf_op jit(solution)/shard_map/cond/branch_1_fun/hqk,khd->hqd/dot_general | solution.py:109
  129.2 6.1 %concatenate.15 = bf16[32,128,228]{1,2,0:T(8,128)(2,1)} concatenate(bf16[32,128,224]{1,2,0:T(8,128)(2,1)S(1)} %fusion.10, bf16[32,128,1]{1,2,0:T(2,128)(2,1)S(1)} %copy.34, bf16[32,128,1]{1,2,0:T(2,128)(2,1)S(1)} %copy.35, bf16[32,128,1]{1,2,0:T(2,128)(2,1)S(1)} %copy.36, bf16[32,128,1]{1,2,0:T(2,128)(2,1)S(1)} %copy.37), dimensions={2} | concatenate | bytes 3735552 | tf_op jit(solution)/shard_map/cond/branch_1_fun/concatenate | solution.py:117
  135.3 4.4 %all-to-all-start.4 = ((bf16[32,128,228]{1,2,0:T(8,128)(2,1)}), bf16[32,128,228]{1,2,0:T(8,128)(2,1)S(1)}, u32[]{:S(2)}, u32[]{:S(2)}) async-start(bf16[32,128,228]{1,2,0:T(8,128)(2,1)} %get-tuple-element.99), calls=%async_computation.4 | async-start | bytes 3801088 | tf_op jit(solution)/shard_map/all_to_all | solution.py:124
  140.4 1.1 fusion.71
  141.4 0.6 copy-done.4
  142.0 0.1 fusion.53
  142.1 23.9 %all-to-all-done.4 = bf16[32,128,228]{1,2,0:T(8,128)(2,1)S(1)} async-done(((bf16[32,128,228]{1,2,0:T(8,128)(2,1)}), bf16[32,128,228]{1,2,0:T(8,128)(2,1)S(1)}, u32[]{:S(2)}, u32[]{:S(2)}) %all-to-all-start.4) | async-done | bytes 1867808 | tf_op jit(solution)/shard_map/all_to_all | solution.py:124
  166.2 0.4 multiply_reduce_fusion
  166.6 1.1 fusion.38
  167.7 0.0 copy-start.5
  167.7 0.0 copy-start.6
  167.7 0.4 convolution_convert_fusion.1
  168.2 1.1 reshape.277
  169.3 4.3 %all-to-all-start.5 = ((bf16[32,4,3584]{2,1,0:T(4,128)(2,1)}), bf16[32,4,3584]{2,1,0:T(4,128)(2,1)S(1)}, u32[]{:S(2)}, u32[]{:S(2)}) async-start(bf16[32,4,3584]{2,1,0:T(4,128)(2,1)} %reshape.277), calls=%async_computation.5 | async-start | bytes 1835008 | tf_op jit(solution)/shard_map/all_to_all | solution.py:32
  173.6 15.6 %all-to-all-done.5 = bf16[32,4,3584]{2,1,0:T(4,128)(2,1)S(1)} async-done(((bf16[32,4,3584]{2,1,0:T(4,128)(2,1)}), bf16[32,4,3584]{2,1,0:T(4,128)(2,1)S(1)}, u32[]{:S(2)}, u32[]{:S(2)}) %all-to-all-start.5) | async-done | bytes 917536 | tf_op jit(solution)/shard_map/all_to_all | solution.py:32
  189.3 0.4 convert_reduce_fusion
  189.6 0.1 multiply_reduce_fusion.1
  189.8 0.1 multiply_convert_fusion
  189.9 1.7 broadcast_in_dim.63
  191.6 7.5 %all-to-all-start.6 = ((bf16[64,4,3584]{2,1,0:T(4,128)(2,1)}), bf16[64,4,3584]{2,1,0:T(4,128)(2,1)S(1)}, u32[]{:S(2)}, u32[]{:S(2)}) async-start(bf16[64,4,3584]{2,1,0:T(4,128)(2,1)} %broadcast_in_dim.63), calls=%async_computation.6 | async-start | bytes 3670016 | tf_op jit(solution)/shard_map/all_to_all | solution.py:27
  199.1 0.8 collective-permute-start
  199.9 0.1 collective-permute-start.1
  200.0 24.5 %all-to-all-done.6 = bf16[64,4,3584]{2,1,0:T(4,128)(2,1)S(1)} async-done(((bf16[64,4,3584]{2,1,0:T(4,128)(2,1)}), bf16[64,4,3584]{2,1,0:T(4,128)(2,1)S(1)}, u32[]{:S(2)}, u32[]{:S(2)}) %all-to-all-start.6) | async-done | bytes 1835040 | tf_op jit(solution)/shard_map/all_to_all | solution.py:27
  224.5 1.5 reshape.281
  226.0 0.0 collective-permute-done
  226.0 3.6 %fusion.30 = f32[2,256,224]{1,2,0:T(8,128)S(1)} fusion(bf16[256,3584,1]{1,0,2:T(8,128)(2,1)} %reshape.281, bf16[2,112,3584]{2,1,0:T(8,128)(2,1)} %collective-permute-done, bf16[2,112,3584]{2,1,0:T(8,128)(2,1)} %param.25), kind=kOutput, calls=%fused_computation.41 | convolution fusion | flops 828506112 | bytes 5505024 | tf_op jit(solution)/shard_map/td,cfd->ctf/dot_general | solution.py:168
  229.6 0.0 collective-permute-done.1
  229.6 3.1 %convolution_convert_fusion = bf16[256,3584]{1,0:T(8,128)(2,1)} fusion(bf16[112,3584]{1,0:T(8,128)(2,1)} %collective-permute-done.1, bf16[112,3584]{1,0:T(8,128)(2,1)S(1)} %copy-done.7, f32[2,256,224]{1,2,0:T(8,128)S(1)} %fusion.30), kind=kOutput, calls=%fused_computation.30 | convolution fusion | flops 415514624 | bytes 3899392 | tf_op jit(solution)/shard_map/dot_general | solution.py:170
  232.7 3.1 %reshape.279 = bf16[64,4,3584]{2,1,0:T(4,128)(2,1)S(1)} reshape(bf16[256,3584]{1,0:T(8,128)(2,1)} %convolution_convert_fusion) | data formatting | bytes 3670016 | tf_op jit(solution)/shard_map/reshape | solution.py:31
  235.8 30.1 %all_to_all.40 = bf16[64,4,3584]{2,1,0:T(4,128)(2,1)} all-to-all(bf16[64,4,3584]{2,1,0:T(4,128)(2,1)S(1)} %reshape.279), channel_id=1, replica_groups=mesh['req'=4,'chip'=16,'core'=2] {'req','chip'}, dimensions={0} | all-to-all | bytes 3670016 | tf_op jit(solution)/shard_map/all_to_all | solution.py:32
  265.9 2.9 %reduce_sum.93 = bf16[4,3584]{1,0:T(4,128)(2,1)} reduce(bf16[64,4,3584]{2,1,0:T(4,128)(2,1)} %all_to_all.40, bf16[]{:T(256)} %constant.80.clone.1), dimensions={0}, to_apply=%region_13.14 | reduce | flops 903168 | bytes 1863682 | tf_op jit(solution)/shard_map/reduce_sum | solution.py:172
  (31 shorter events, 0.3 us)
Async XLA Ops:
  0.6 167.1 %copy-start = (bf16[224,3584]{1,0:T(8,128)(2,1)S(1)}, bf16[224,3584]{1,0:T(8,128)(2,1)}, u32[]{:S(2)}) copy-start(bf16[224,3584]{1,0:T(8,128)(2,1)} %param.23) | copy-start | bytes 4816900
  5.1 34.1 %all-to-all-start = ((bf16[32,4,7168]{2,1,0:T(4,128)(2,1)}), bf16[32,4,7168]{2,1,0:T(4,128)(2,1)S(1)}, u32[]{:S(2)}, u32[]{:S(2)}) async-start(bf16[32,4,7168]{2,1,0:T(4,128)(2,1)} %broadcast_in_dim.30), calls=%async_computation | async-start | bytes 3670016 | tf_op jit(solution)/shard_map/all_to_all | solution.py:27
  44.2 13.4 %all-to-all-start.1 = ((f32[32,4,384]{2,1,0:T(4,128)}), f32[32,4,384]{2,1,0:T(4,128)}, u32[]{:S(2)}, u32[]{:S(2)}) async-start(f32[32,4,384]{2,1,0:T(4,128)} %reshape.271), calls=%async_computation.1 | async-start | bytes 393216 | tf_op jit(solution)/shard_map/all_to_all | solution.py:32
  59.2 11.4 %all-to-all-start.2 = ((bf16[32,4,384]{2,1,0:T(4,128)(2,1)}), bf16[32,4,384]{2,1,0:T(4,128)(2,1)S(1)}, u32[]{:S(2)}, u32[]{:S(2)}) async-start(bf16[32,4,384]{2,1,0:T(4,128)(2,1)} %broadcast_in_dim.31), calls=%async_computation.2 | async-start | bytes 196608 | tf_op jit(solution)/shard_map/all_to_all | solution.py:27
  63.0 7.6 %copy-start.3 = (bf16[3,128,224]{1,2,0:T(8,128)(2,1)S(1)}, bf16[3,128,224]{1,2,0:T(8,128)(2,1)}, u32[]{:S(2)}) copy-start(bf16[3,128,224]{1,2,0:T(8,128)(2,1)} %param.22) | copy-start | bytes 516100
  70.7 34.4 %copy-start.8 = (s32[1,256]{1,0:T(1,128)S(1)}, s32[1,256]{1,0:T(1,128)}, u32[]{:S(2)}) copy-start(s32[1,256]{1,0:T(1,128)} %param.30) | copy-start | bytes 3076
  70.9 0.7 copy-start.2
  73.7 31.4 %all-to-all-start.3 = ((bf16[32,128,224]{1,2,0:T(8,128)(2,1)}), bf16[32,128,224]{1,2,0:T(8,128)(2,1)S(1)}, u32[]{:S(2)}, u32[]{:S(2)}) async-start(bf16[32,128,224]{1,2,0:T(8,128)(2,1)} %broadcast_in_dim.33), calls=%async_computation.3 | async-start | bytes 3670016 | tf_op jit(solution)/shard_map/all_to_all | solution.py:27
  115.2 1.9 copy-start.1
  135.3 30.7 %all-to-all-start.4 = ((bf16[32,128,228]{1,2,0:T(8,128)(2,1)}), bf16[32,128,228]{1,2,0:T(8,128)(2,1)S(1)}, u32[]{:S(2)}, u32[]{:S(2)}) async-start(bf16[32,128,228]{1,2,0:T(8,128)(2,1)} %get-tuple-element.99), calls=%async_computation.4 | async-start | bytes 3801088 | tf_op jit(solution)/shard_map/all_to_all | solution.py:124
  141.4 0.6 copy-start.4
  167.7 21.9 %copy-start.5 = (bf16[128,224]{0,1:T(8,128)(2,1)}, bf16[128,224]{0,1:T(8,128)(2,1)S(1)}, u32[]{:S(2)}) copy-start(bf16[128,224]{0,1:T(8,128)(2,1)S(1)} %fusion.38) | copy-start | bytes 172036
  167.7 5.9 %copy-start.6 = (bf16[3584]{0:T(1024)(128)(2,1)S(1)}, bf16[3584]{0:T(1024)(128)(2,1)}, u32[]{:S(2)}) copy-start(bf16[3584]{0:T(1024)(128)(2,1)} %param.24) | copy-start | bytes 21508
  169.3 20.0 %all-to-all-start.5 = ((bf16[32,4,3584]{2,1,0:T(4,128)(2,1)}), bf16[32,4,3584]{2,1,0:T(4,128)(2,1)S(1)}, u32[]{:S(2)}, u32[]{:S(2)}) async-start(bf16[32,4,3584]{2,1,0:T(4,128)(2,1)} %reshape.277), calls=%async_computation.5 | async-start | bytes 1835008 | tf_op jit(solution)/shard_map/all_to_all | solution.py:32
  191.6 32.9 %all-to-all-start.6 = ((bf16[64,4,3584]{2,1,0:T(4,128)(2,1)}), bf16[64,4,3584]{2,1,0:T(4,128)(2,1)S(1)}, u32[]{:S(2)}, u32[]{:S(2)}) async-start(bf16[64,4,3584]{2,1,0:T(4,128)(2,1)} %broadcast_in_dim.63), calls=%async_computation.6 | async-start | bytes 3670016 | tf_op jit(solution)/shard_map/all_to_all | solution.py:27
  199.1 26.9 %collective-permute-start = (bf16[2,112,3584]{2,1,0:T(8,128)(2,1)}, bf16[2,112,3584]{2,1,0:T(8,128)(2,1)}, u32[]{:S(2)}, u32[]{:S(2)}) collective-permute-start(bf16[2,112,3584]{2,1,0:T(8,128)(2,1)} %param.25), channel_id=1, source_target_pairs={{0,1},{1,0},{2,3},{3,2},{4,5},{5,4},{6,7},{7,6},{8,9},{9,8},{10,11... | collective-permute-start | bytes 4816904 | tf_op jit(solution)/shard_map/ppermute | solution.py:71
  199.9 29.7 %collective-permute-start.1 = (bf16[112,3584]{1,0:T(8,128)(2,1)}, bf16[112,3584]{1,0:T(8,128)(2,1)}, u32[]{:S(2)}, u32[]{:S(2)}) collective-permute-start(bf16[112,3584]{1,0:T(8,128)(2,1)} %param.26), channel_id=1, source_target_pairs={{0,1},{1,0},{2,3},{3,2},{4,5},{5,4},{6,7},{7,6},{8,9},{9,8},{10,11... | collective-permute-start | bytes 2408456 | tf_op jit(solution)/shard_map/ppermute | solution.py:72
  226.0 3.6 %copy-start.7 = (bf16[112,3584]{1,0:T(8,128)(2,1)S(1)}, bf16[112,3584]{1,0:T(8,128)(2,1)}, u32[]{:S(2)}) copy-start(bf16[112,3584]{1,0:T(8,128)(2,1)} %param.26) | copy-start | bytes 2408452

commit v4 on v3

--- a/solution.py
+++ b/solution.py
@@ -25,6 +25,16 @@
 def gather_rows(piece, axis, count):
     spread = jnp.broadcast_to(piece[None], (count,) + piece.shape)
     return lax.all_to_all(spread, axis, 0, 0, tiled=True)
+
+
+def gather_wide(piece, chips):
+    own = gather_rows(piece, "chip", chips)
+    other = lax.ppermute(own, "core", [(0, 1), (1, 0)])
+    first_core = lax.axis_index("core") == 0
+    even = jnp.where(first_core, own, other)
+    odd = jnp.where(first_core, other, own)
+    joined = jnp.stack([even, odd], axis=1)
+    return joined.reshape((2 * chips,) + piece.shape)
 
 
 def send_rows(values, axis, count):
@@ -61,6 +71,7 @@
     score_scale = HD ** (-0.5)
     wide_size = lax.psum(1, WIDE)
     half_size = lax.psum(1, HALF)
+    chips = lax.psum(1, "chip")
     local_width = qkv_weight.shape[2]
     local_heads = local_width // HD
     own_rows = tokens.shape[0]
@@ -72,7 +83,7 @@
     chip_down = jnp.concatenate([down_weight, lax.ppermute(down_weight, "core", swap)], axis=0)
 
     normed = rms_scale(tokens, attn_gain)
-    shard_rows = gather_rows(normed, WIDE, wide_size).reshape(SPAN, D)
+    shard_rows = gather_wide(normed, chips).reshape(SPAN, D)
     base_part = jnp.dot(
         shard_rows, qkv_weight.reshape(D, 3 * local_width), preferred_element_type=jnp.float32
     )
@@ -87,7 +98,7 @@
     new_keys = projected[:, 1]
     new_values = projected[:, 2]
 
-    query_heads = gather_rows(query_own, WIDE, wide_size).reshape(HEADS, SPAN, HD)
+    query_heads = gather_wide(query_own, chips).reshape(HEADS, SPAN, HD)
     block_len = key_cache.shape[1]
     block_start = wide_index * block_len
     length = cache_lengths[0]

time: 272 us -> 258 us (0.949)
  blocking collectives: 30.1 us -> 81.7 us
  waiting for transfers between devices: 123 us -> 73.6 us
  starting transfers between devices: 40.2 us -> 24.7 us
  local copies, waits for them, and re-layouts: 37.8 us -> 33.6 us
    all_to_all x4 -> x2, waiting for transfers between devices: 76.6 us -> 30.6 us  [gather_rows(): return lax.all_to_all(spread, axis, 0, 0, tiled=True)]
    all_to_all x0 -> x2, blocking collectives: none -> 38.6 us  [gather_rows(): return lax.all_to_all(spread, axis, 0, 0, tiled=True)]
    all_to_all x4 -> x2, starting transfers between devices: 25.7 us -> 11.3 us  [gather_rows(): return lax.all_to_all(spread, axis, 0, 0, tiled=True)]
    all_to_all x1 -> x2, blocking collectives: 30.1 us -> 43.1 us  [send_rows(): return lax.all_to_all(blocks, axis, 0, 0, tiled=True)]
    all_to_all x2 -> x1, waiting for transfers between devices: 22.6 us -> 15.6 us  [send_rows(): return lax.all_to_all(blocks, axis, 0, 0, tiled=True)]
    all_to_all x2 -> x1, starting transfers between devices: 9.21 us -> 4.34 us  [send_rows(): return lax.all_to_all(blocks, axis, 0, 0, tiled=True)]
    ppermute x0 -> x2, starting transfers between devices: none -> 4.19 us  [gather_wide(): other = lax.ppermute(own, 'core', [(0, 1), (1, 0)])]
    ppermute x0 -> x2, waiting for transfers between devices: none -> 3.54 us  [gather_wide(): other = lax.ppermute(own, 'core', [(0, 1), (1, 0)])]
  transfers between devices with their start and end apart: 9 -> 8, of which waited for: 7 -> 6; matrix products, arithmetic and copies ran while one was open for 5% -> 3% of each run, Pallas kernels for 0% -> 0%
where the time goes in v4:
time: 258 us; the launch traced here: 255 us
  blocking collectives  81.7 us (32%)
  waiting for transfers between devices  73.6 us (29%)
  local copies, waits for them, and re-layouts  33.6 us (13%)
  matrix products  26.4 us (10%)
  starting transfers between devices  24.7 us (10%)
  other arithmetic  12.2 us (5%)
    all_to_all x2, blocking collectives, send_rows(): return lax.all_to_all(blocks, axis, 0, 0, tiled=True)  43.1 us
    all_to_all x2, blocking collectives, gather_rows(): return lax.all_to_all(spread, axis, 0, 0, tiled=True)  38.6 us
    all_to_all x2, waiting for transfers between devices, gather_rows(): return lax.all_to_all(spread, axis, 0, 0, tiled=True)  30.6 us
    all_to_all x1, waiting for transfers between devices, body(): parts = lax.all_to_all(packed, WIDE, 0, 0, tiled=True)  23.9 us
    all_to_all x1, waiting for transfers between devices, send_rows(): return lax.all_to_all(blocks, axis, 0, 0, tiled=True)  15.6 us
    another operation x7, local copies, waits for them, and re-layouts  12.6 us
    all_to_all x2, starting transfers between devices, gather_rows(): return lax.all_to_all(spread, axis, 0, 0, tiled=True)  11.3 us
    dot_general x1, matrix products, body(): jnp.dot(shard_rows, qkv_weight.reshape(D, 3 * local_width), preferred_ele...  6.98 us
  transfers between devices with their start and end apart: 8, of which 6 were waited for; matrix products, arithmetic and copies ran while one was open for 3% of the time, Pallas kernels for 0%

profile of v4, /device:TPU:1, one launch (start us, length us, event | category | flops | bytes accessed | tf_op | source)
XLA Modules:
  0.0 254.6 jit_solution(2259538928654729107)
XLA Ops:
  0.6 0.8 convert_element_type.82
  1.5 1.0 fusion.47
  2.5 0.9 fusion.49
  3.4 0.2 broadcast_in_dim.30
  3.7 22.0 %all_to_all.40 = bf16[16,4,7168]{2,1,0:T(4,128)(2,1)S(1)} all-to-all(bf16[16,4,7168]{2,1,0:T(4,128)(2,1)S(1)} %broadcast_in_dim.30), channel_id=1, replica_groups=mesh['req'=4,'chip'=16,'core'=2] {'chip'}, dimensions={0} | all-to-all | bytes 1835008 | tf_op jit(solution)/shard_map/all_to_all | solution.py:27
  25.7 1.8 collective-permute-start.1
  27.4 2.1 collective-permute-done.1
  29.5 0.7 select_bitcast_fusion.3
  30.2 1.2 pad_maximum_fusion
  31.4 1.5 reshape_reshape.3
  32.9 1.9 fusion.53
  34.8 1.7 reshape.270
  36.4 13.0 %all_to_all.41 = f32[32,4,384]{2,1,0:T(4,128)} all-to-all(f32[32,4,384]{2,1,0:T(4,128)} %reshape.270), channel_id=1, replica_groups=mesh['req'=4,'chip'=16,'core'=2] {'chip','core'}, dimensions={0} | all-to-all | bytes 393216 | tf_op jit(solution)/shard_map/all_to_all | solution.py:42
  49.4 1.0 reduce_sum.87
  50.4 0.7 broadcast_in_dim.31
  51.1 3.8 %all-to-all-start.2 = ((bf16[32,4,384]{2,1,0:T(4,128)(2,1)}), bf16[32,4,384]{2,1,0:T(4,128)(2,1)S(1)}, u32[]{:S(2)}, u32[]{:S(2)}) async-start(bf16[32,4,384]{2,1,0:T(4,128)(2,1)} %broadcast_in_dim.31), calls=%async_computation.2 | async-start | bytes 196608 | tf_op jit(solution)/shard_map/all_to_all | solution.py:27
  54.9 1.5 reshape.282
  56.3 6.1 %all-to-all-done.2 = bf16[32,4,384]{2,1,0:T(4,128)(2,1)S(1)} async-done(((bf16[32,4,384]{2,1,0:T(4,128)(2,1)}), bf16[32,4,384]{2,1,0:T(4,128)(2,1)S(1)}, u32[]{:S(2)}, u32[]{:S(2)}) %all-to-all-start.2) | async-done | bytes 98336 | tf_op jit(solution)/shard_map/all_to_all | solution.py:27
  62.5 1.1 convolution_bitcast_fusion
  63.6 7.0 %fusion.36 = bf16[128,3,224]{0,2,1:T(8,128)(2,1)S(1)} fusion(f32[128,3,224]{0,2,1:T(8,128)S(1)} %convolution_bitcast_fusion, bf16[128,7168,1]{1,0,2:T(8,128)(2,1)} %reshape.282, bf16[7168,3,224]{0,2,1:T(8,128)(2,1)} %param.20), kind=kOutput, calls=%fused_computation.46 | convolution fusion | flops 1233297408 | bytes 11984896 | tf_op jit(solution)/shard_map/dot_general | solution.py:87
  70.6 0.7 slice_bitcast_fusion.2
  71.3 0.1 broadcast_in_dim.33
  71.4 16.6 %all_to_all.42 = bf16[16,128,224]{1,2,0:T(8,128)(2,1)S(1)} all-to-all(bf16[16,128,224]{1,2,0:T(8,128)(2,1)S(1)} %broadcast_in_dim.33), channel_id=1, replica_groups=mesh['req'=4,'chip'=16,'core'=2] {'chip'}, dimensions={0} | all-to-all | bytes 1835008 | tf_op jit(solution)/shard_map/all_to_all | solution.py:27
  88.0 2.4 collective-permute-start.2
  91.1 1.4 collective-permute-done.2
  92.6 0.1 select_bitcast_fusion.1
  92.7 0.2 pad_maximum_fusion.1
  92.9 0.5 copy-done.9
  93.4 28.7 %conditional.1 = (bf16[32,128,228]{1,2,0:T(8,128)(2,1)}) conditional(s32[]{:T(128)} %convert_element_type.80, () %tuple.18, (s32[]{:T(128)}, bf16[1,256,7168]{2,1,0:T(8,128)(2,1)}, bf16[16,2,128,224]{2,3,1,0:T(8,128)(2,1)S(1)}, bf16[1,256,7168]{2,1,0:T(8,128)(2,1)}, s32[1,256]{1,0:T(1,128)S(1)}, /*index=5*/s32[]{:T(128)}, ...), branch_computations={%region_2.3_spmd, %region_3.6_spmd.clone} | conditional | flops 954123264 | bytes 59018796 | solution.py:134
  93.4 0.7 compare_and_fusion
  94.0 5.9 %copy.45 = bf16[1,256,7168]{1,2,0:T(8,128)(2,1)} copy(bf16[1,256,7168]{2,1,0:T(8,128)(2,1)} %get-tuple-element.79) | data formatting | bytes 7340032 | tf_op jit(solution)/shard_map
  100.0 3.5 %fusion = (f32[32,128]{1,0:T(8,128)S(1)}, f32[32,128,256]{2,1,0:T(8,128)S(1)}) fusion(pred[256]{0:T(512)(128)(4,1)S(1)} %compare_and_fusion, bf16[32,128,224]{1,2,0:T(8,128)(2,1)S(1)} %bitcast.107, bf16[256,32,224]{0,2,1:T(8,128)(2,1)} %bitcast.106), kind=kOutput, calls=%fused_computation.2 | convolution fusion | flops 472903680 | bytes 9715968 | tf_op jit(solution)/shard_map/cond/branch_1_fun/hqd,khd->hqk/dot_general | solution.py:111
  103.5 1.5 fusion.1
  105.0 0.4 copy-done.1
  105.5 5.9 %copy.46 = bf16[1,256,7168]{1,2,0:T(8,128)(2,1)} copy(bf16[1,256,7168]{2,1,0:T(8,128)(2,1)} %get-tuple-element.81) | data formatting | bytes 7340032 | tf_op jit(solution)/shard_map
  111.4 4.5 %fusion.10 = bf16[32,128,224]{1,2,0:T(8,128)(2,1)S(1)} fusion(bf16[256,32,224]{0,2,1:T(8,128)(2,1)} %bitcast.108, f32[32,128,256]{2,1,0:T(8,128)} %copy-done.1, f32[32,128]{1,0:T(8,128)S(1)} %reduce-precision_add_fusion, pred[256]{0:T(512)(128)(4,1)S(1)} %compare_and_fusion), kind=kOutput, calls=%fused_computation.11 | convolution fusion | flops 475922432 | bytes 9715968 | tf_op jit(solution)/shard_map/cond/branch_1_fun/hqk,khd->hqd/dot_general | solution.py:120
  116.0 6.1 %concatenate.15 = bf16[32,128,228]{1,2,0:T(8,128)(2,1)} concatenate(bf16[32,128,224]{1,2,0:T(8,128)(2,1)S(1)} %fusion.10, bf16[32,128,1]{1,2,0:T(2,128)(2,1)S(1)} %copy.38, bf16[32,128,1]{1,2,0:T(2,128)(2,1)S(1)} %copy.39, bf16[32,128,1]{1,2,0:T(2,128)(2,1)S(1)} %copy.40, bf16[32,128,1]{1,2,0:T(2,128)(2,1)S(1)} %copy.41), dimensions={2} | concatenate | bytes 3735552 | tf_op jit(solution)/shard_map/cond/branch_1_fun/concatenate | solution.py:128
  122.1 4.0 %all-to-all-start.4 = ((bf16[32,128,228]{1,2,0:T(8,128)(2,1)}), bf16[32,128,228]{1,2,0:T(8,128)(2,1)S(1)}, u32[]{:S(2)}, u32[]{:S(2)}) async-start(bf16[32,128,228]{1,2,0:T(8,128)(2,1)} %get-tuple-element.104), calls=%async_computation.4 | async-start | bytes 3801088 | tf_op jit(solution)/shard_map/all_to_all | solution.py:135
  126.8 1.1 fusion.75
  127.8 0.6 copy-done.3
  128.5 0.1 fusion.57
  128.6 23.9 %all-to-all-done.4 = bf16[32,128,228]{1,2,0:T(8,128)(2,1)S(1)} async-done(((bf16[32,128,228]{1,2,0:T(8,128)(2,1)}), bf16[32,128,228]{1,2,0:T(8,128)(2,1)S(1)}, u32[]{:S(2)}, u32[]{:S(2)}) %all-to-all-start.4) | async-done | bytes 1867808 | tf_op jit(solution)/shard_map/all_to_all | solution.py:135
  152.6 0.4 multiply_reduce_fusion
  153.0 0.3 copy-done.4
  153.3 0.0 copy-done.5
  153.3 0.2 fusion.42
  153.5 0.4 convolution_convert_fusion.1
  154.0 1.1 reshape.277
  155.1 4.3 %all-to-all-start.5 = ((bf16[32,4,3584]{2,1,0:T(4,128)(2,1)}), bf16[32,4,3584]{2,1,0:T(4,128)(2,1)S(1)}, u32[]{:S(2)}, u32[]{:S(2)}) async-start(bf16[32,4,3584]{2,1,0:T(4,128)(2,1)} %reshape.277), calls=%async_computation.5 | async-start | bytes 1835008 | tf_op jit(solution)/shard_map/all_to_all | solution.py:42
  159.5 15.6 %all-to-all-done.5 = bf16[32,4,3584]{2,1,0:T(4,128)(2,1)S(1)} async-done(((bf16[32,4,3584]{2,1,0:T(4,128)(2,1)}), bf16[32,4,3584]{2,1,0:T(4,128)(2,1)S(1)}, u32[]{:S(2)}, u32[]{:S(2)}) %all-to-all-start.5) | async-done | bytes 917536 | tf_op jit(solution)/shard_map/all_to_all | solution.py:42
  175.1 0.4 convert_reduce_fusion
  175.5 0.1 multiply_reduce_fusion.1
  175.6 0.1 multiply_convert_fusion
  175.7 1.7 broadcast_in_dim.63
  177.5 7.5 %all-to-all-start.6 = ((bf16[64,4,3584]{2,1,0:T(4,128)(2,1)}), bf16[64,4,3584]{2,1,0:T(4,128)(2,1)S(1)}, u32[]{:S(2)}, u32[]{:S(2)}) async-start(bf16[64,4,3584]{2,1,0:T(4,128)(2,1)} %broadcast_in_dim.63), calls=%async_computation.6 | async-start | bytes 3670016 | tf_op jit(solution)/shard_map/all_to_all | solution.py:27
  185.0 0.8 collective-permute-start
  185.7 0.1 collective-permute-start.3
  185.8 24.5 %all-to-all-done.6 = bf16[64,4,3584]{2,1,0:T(4,128)(2,1)S(1)} async-done(((bf16[64,4,3584]{2,1,0:T(4,128)(2,1)}), bf16[64,4,3584]{2,1,0:T(4,128)(2,1)S(1)}, u32[]{:S(2)}, u32[]{:S(2)}) %all-to-all-start.6) | async-done | bytes 1835040 | tf_op jit(solution)/shard_map/all_to_all | solution.py:27
  210.4 1.5 reshape.283
  211.8 3.6 %fusion.30 = f32[2,256,224]{1,2,0:T(8,128)S(1)} fusion(bf16[256,3584,1]{1,0,2:T(8,128)(2,1)} %reshape.283, bf16[2,112,3584]{2,1,0:T(8,128)(2,1)} %collective-permute-done, bf16[2,112,3584]{2,1,0:T(8,128)(2,1)} %param.25), kind=kOutput, calls=%fused_computation.43 | convolution fusion | flops 828506112 | bytes 5505024 | tf_op jit(solution)/shard_map/td,cfd->ctf/dot_general | solution.py:179
  215.4 3.1 %convolution_convert_fusion = bf16[256,3584]{1,0:T(8,128)(2,1)} fusion(bf16[112,3584]{1,0:T(8,128)(2,1)} %collective-permute-done.3, bf16[112,3584]{1,0:T(8,128)(2,1)S(1)} %copy-done.8, f32[2,256,224]{1,2,0:T(8,128)S(1)} %fusion.30), kind=kOutput, calls=%fused_computation.30 | convolution fusion | flops 415514624 | bytes 3899392 | tf_op jit(solution)/shard_map/dot_general | solution.py:181
  218.5 3.1 %reshape.279 = bf16[64,4,3584]{2,1,0:T(4,128)(2,1)S(1)} reshape(bf16[256,3584]{1,0:T(8,128)(2,1)} %convolution_convert_fusion) | data formatting | bytes 3670016 | tf_op jit(solution)/shard_map/reshape | solution.py:41
  221.6 30.1 %all_to_all.43 = bf16[64,4,3584]{2,1,0:T(4,128)(2,1)} all-to-all(bf16[64,4,3584]{2,1,0:T(4,128)(2,1)S(1)} %reshape.279), channel_id=1, replica_groups=mesh['req'=4,'chip'=16,'core'=2] {'req','chip'}, dimensions={0} | all-to-all | bytes 3670016 | tf_op jit(solution)/shard_map/all_to_all | solution.py:42
  251.8 2.9 %reduce_sum.93 = bf16[4,3584]{1,0:T(4,128)(2,1)} reduce(bf16[64,4,3584]{2,1,0:T(4,128)(2,1)} %all_to_all.43, bf16[]{:T(256)} %constant.80.clone.1), dimensions={0}, to_apply=%region_13.14 | reduce | flops 903168 | bytes 1863682 | tf_op jit(solution)/shard_map/reduce_sum | solution.py:183
  (38 shorter events, 0.4 us)
Async XLA Ops:
  0.6 152.9 %copy-start = (bf16[224,3584]{1,0:T(8,128)(2,1)S(1)}, bf16[224,3584]{1,0:T(8,128)(2,1)}, u32[]{:S(2)}) copy-start(bf16[224,3584]{1,0:T(8,128)(2,1)} %param.23) | copy-start | bytes 4816900
  25.7 3.9 %collective-permute-start.1 = (bf16[16,4,7168]{2,1,0:T(4,128)(2,1)S(1)}, bf16[16,4,7168]{2,1,0:T(4,128)(2,1)S(1)}, u32[]{:S(2)}, u32[]{:S(2)}) collective-permute-start(bf16[16,4,7168]{2,1,0:T(4,128)(2,1)S(1)} %all_to_all.40), channel_id=1, source_target_pairs={{0,1},{1,0},{2,3},{3,2},{4,5},{5,4},{6,7},{7,6},{8,9},{9,8},{10,11... | collective-permute-start | bytes 2752520 | tf_op jit(solution)/shard_map/ppermute | solution.py:32
  51.1 11.4 %all-to-all-start.2 = ((bf16[32,4,384]{2,1,0:T(4,128)(2,1)}), bf16[32,4,384]{2,1,0:T(4,128)(2,1)S(1)}, u32[]{:S(2)}, u32[]{:S(2)}) async-start(bf16[32,4,384]{2,1,0:T(4,128)(2,1)} %broadcast_in_dim.31), calls=%async_computation.2 | async-start | bytes 196608 | tf_op jit(solution)/shard_map/all_to_all | solution.py:27
  70.6 17.4 %copy-start.2 = (bf16[128,3,224]{0,2,1:T(8,128)(2,1)}, bf16[128,3,224]{0,2,1:T(8,128)(2,1)S(1)}, u32[]{:S(2)}) copy-start(bf16[128,3,224]{0,2,1:T(8,128)(2,1)S(1)} %fusion.36) | copy-start | bytes 516100
  88.0 4.5 %collective-permute-start.2 = (bf16[16,128,224]{1,2,0:T(8,128)(2,1)S(1)}, bf16[16,128,224]{1,2,0:T(8,128)(2,1)S(1)}, u32[]{:S(2)}, u32[]{:S(2)}) collective-permute-start(bf16[16,128,224]{1,2,0:T(8,128)(2,1)S(1)} %all_to_all.42), channel_id=1, source_target_pairs={{0,1},{1,0},{2,3},{3,2},{4,5},{5,4},{6,7},{7,6},{8,9},{9,8},{10,11... | collective-permute-start | bytes 2752520 | tf_op jit(solution)/shard_map/ppermute | solution.py:32
  92.7 0.7 copy-start.9
  103.5 1.9 copy-start.1
  122.1 30.3 %all-to-all-start.4 = ((bf16[32,128,228]{1,2,0:T(8,128)(2,1)}), bf16[32,128,228]{1,2,0:T(8,128)(2,1)S(1)}, u32[]{:S(2)}, u32[]{:S(2)}) async-start(bf16[32,128,228]{1,2,0:T(8,128)(2,1)} %get-tuple-element.104), calls=%async_computation.4 | async-start | bytes 3801088 | tf_op jit(solution)/shard_map/all_to_all | solution.py:135
  127.8 0.6 copy-start.3
  152.4 0.8 copy-start.4
  152.4 0.8 copy-start.5
  153.5 1.6 copy-start.6
  154.0 5.5 %copy-start.7 = (bf16[3584]{0:T(1024)(128)(2,1)S(1)}, bf16[3584]{0:T(1024)(128)(2,1)}, u32[]{:S(2)}) copy-start(bf16[3584]{0:T(1024)(128)(2,1)} %param.24) | copy-start | bytes 21508
  155.1 20.0 %all-to-all-start.5 = ((bf16[32,4,3584]{2,1,0:T(4,128)(2,1)}), bf16[32,4,3584]{2,1,0:T(4,128)(2,1)S(1)}, u32[]{:S(2)}, u32[]{:S(2)}) async-start(bf16[32,4,3584]{2,1,0:T(4,128)(2,1)} %reshape.277), calls=%async_computation.5 | async-start | bytes 1835008 | tf_op jit(solution)/shard_map/all_to_all | solution.py:42
  177.5 32.9 %all-to-all-start.6 = ((bf16[64,4,3584]{2,1,0:T(4,128)(2,1)}), bf16[64,4,3584]{2,1,0:T(4,128)(2,1)S(1)}, u32[]{:S(2)}, u32[]{:S(2)}) async-start(bf16[64,4,3584]{2,1,0:T(4,128)(2,1)} %broadcast_in_dim.63), calls=%async_computation.6 | async-start | bytes 3670016 | tf_op jit(solution)/shard_map/all_to_all | solution.py:27
  185.0 26.9 %collective-permute-start = (bf16[2,112,3584]{2,1,0:T(8,128)(2,1)}, bf16[2,112,3584]{2,1,0:T(8,128)(2,1)}, u32[]{:S(2)}, u32[]{:S(2)}) collective-permute-start(bf16[2,112,3584]{2,1,0:T(8,128)(2,1)} %param.25), channel_id=1, source_target_pairs={{0,1},{1,0},{2,3},{3,2},{4,5},{5,4},{6,7},{7,6},{8,9},{9,8},{10,11... | collective-permute-start | bytes 4816904 | tf_op jit(solution)/shard_map/ppermute | solution.py:82
  185.7 29.7 %collective-permute-start.3 = (bf16[112,3584]{1,0:T(8,128)(2,1)}, bf16[112,3584]{1,0:T(8,128)(2,1)}, u32[]{:S(2)}, u32[]{:S(2)}) collective-permute-start(bf16[112,3584]{1,0:T(8,128)(2,1)} %param.26), channel_id=1, source_target_pairs={{0,1},{1,0},{2,3},{3,2},{4,5},{5,4},{6,7},{7,6},{8,9},{9,8},{10,11... | collective-permute-start | bytes 2408456 | tf_op jit(solution)/shard_map/ppermute | solution.py:83
  211.8 3.6 %copy-start.8 = (bf16[112,3584]{1,0:T(8,128)(2,1)S(1)}, bf16[112,3584]{1,0:T(8,128)(2,1)}, u32[]{:S(2)}) copy-start(bf16[112,3584]{1,0:T(8,128)(2,1)} %param.26) | copy-start | bytes 2408452

commit v5 on v4

--- a/solution.py
+++ b/solution.py
@@ -84,8 +84,8 @@
 
     normed = rms_scale(tokens, attn_gain)
     shard_rows = gather_wide(normed, chips).reshape(SPAN, D)
-    base_part = jnp.dot(
-        shard_rows, qkv_weight.reshape(D, 3 * local_width), preferred_element_type=jnp.float32
+    base_part = lax.optimization_barrier(
+        jnp.dot(shard_rows, qkv_weight.reshape(D, 3 * local_width), preferred_element_type=jnp.float32)
     )
     sliced = lax.dynamic_slice_in_dim(shard_rows, feature_start, local_width, 1)
     partial_low = jnp.dot(sliced, adapter_down, preferred_element_type=jnp.float32)
@@ -104,11 +104,12 @@
     length = cache_lengths[0]
     usable = (block_start + jnp.arange(block_len) < length) & (slot_mask[0] == 1)
 
+    key_heads = jnp.transpose(key_cache[0].reshape(block_len, HEADS, HD), (1, 0, 2))
+    value_heads = jnp.transpose(value_cache[0].reshape(block_len, HEADS, HD), (1, 0, 2))
+
     def cache_block(unused):
-        key_heads = key_cache[0].reshape(block_len, HEADS, HD)
-        value_heads = value_cache[0].reshape(block_len, HEADS, HD)
         scores = (
-            jnp.einsum("hqd,khd->hqk", query_heads, key_heads, preferred_element_type=jnp.float32)
+            jnp.einsum("hqd,hkd->hqk", query_heads, key_heads, preferred_element_type=jnp.float32)
             * score_scale
         )
         scores = jnp.where(usable, scores, NEG_LARGE)
@@ -118,7 +119,7 @@
         weights = jnp.where(usable, jnp.exp(scores - reference_max[..., None]), 0.0)
         totals = jnp.sum(weights, axis=-1)
         numerator = jnp.einsum(
-            "hqk,khd->hqd",
+            "hqk,hkd->hqd",
             weights.astype(jnp.bfloat16),
             value_heads,
             preferred_element_type=jnp.float32,

time: 258 us -> 254 us (0.984)
  waiting for transfers between devices: 73.6 us -> 66.4 us
  blocking collectives: 81.7 us -> 85.3 us
    another operation x7 -> x5, local copies, waits for them, and re-layouts: 12.6 us -> 0.75 us
    unnamed x18 -> x16, local copies, waits for them, and re-layouts: 1.41 us -> 12.8 us
    all_to_all x2, waiting for transfers between devices: 30.6 us -> 25 us  [gather_rows(): return lax.all_to_all(spread, axis, 0, 0, tiled=True)]
    all_to_all x2, blocking collectives: 38.6 us -> 42.2 us  [gather_rows(): return lax.all_to_all(spread, axis, 0, 0, tiled=True)]
    dot_general x2, matrix products: 8.08 us -> 5.1 us  [the longest x1 3.6 us: cache_block(): jnp.einsum('hqd,hkd->hqk', query_heads, key_heads, preferred_element_type...]
  transfers between devices with their start and end apart: 8 -> 8, of which waited for: 6 -> 5; matrix products, arithmetic and copies ran while one was open for 3% -> 10% of each run, Pallas kernels for 0% -> 0%
where the time goes in v5:
time: 254 us; the launch traced here: 250 us
  blocking collectives  85.3 us (34%)
  waiting for transfers between devices  66.4 us (26%)
  local copies, waits for them, and re-layouts  33.3 us (13%)
  matrix products  24.6 us (10%)
  starting transfers between devices  24.5 us (10%)
  other arithmetic  13.5 us (5%)
    all_to_all x2, blocking collectives, send_rows(): return lax.all_to_all(blocks, axis, 0, 0, tiled=True)  43.1 us
    all_to_all x2, blocking collectives, gather_rows(): return lax.all_to_all(spread, axis, 0, 0, tiled=True)  42.2 us
    all_to_all x2, waiting for transfers between devices, gather_rows(): return lax.all_to_all(spread, axis, 0, 0, tiled=True)  25 us
    all_to_all x1, waiting for transfers between devices, body(): parts = lax.all_to_all(packed, WIDE, 0, 0, tiled=True)  23.7 us
    all_to_all x1, waiting for transfers between devices, send_rows(): return lax.all_to_all(blocks, axis, 0, 0, tiled=True)  15.6 us
    unnamed x16, local copies, waits for them, and re-layouts  12.8 us
    all_to_all x2, starting transfers between devices, gather_rows(): return lax.all_to_all(spread, axis, 0, 0, tiled=True)  11.3 us
    dot_general x1, matrix products, body(): jnp.dot(shard_rows, qkv_weight.reshape(D, 3 * local_width), preferred_ele...  7.1 us
  transfers between devices with their start and end apart: 8, of which 5 were waited for; matrix products, arithmetic and copies ran while one was open for 10% of the time, Pallas kernels for 0%

profile of v5, /device:TPU:1, one launch (start us, length us, event | category | flops | bytes accessed | tf_op | source)
XLA Modules:
  0.0 250.0 jit_solution(12711897531453648686)
XLA Ops:
  0.6 0.0 copy-start
  0.6 0.8 convert_element_type.85
  1.5 1.0 fusion.41
  2.5 0.9 fusion.43
  3.4 0.2 broadcast_in_dim.33
  3.7 22.0 %all_to_all.40 = bf16[16,4,7168]{2,1,0:T(4,128)(2,1)S(1)} all-to-all(bf16[16,4,7168]{2,1,0:T(4,128)(2,1)S(1)} %broadcast_in_dim.33), channel_id=1, replica_groups=mesh['req'=4,'chip'=16,'core'=2] {'chip'}, dimensions={0} | all-to-all | bytes 1835008 | tf_op jit(solution)/shard_map/all_to_all | solution.py:27
  25.7 1.8 collective-permute-start.1
  27.4 2.1 collective-permute-done.1
  29.5 0.7 select_bitcast_fusion.3
  30.2 2.4 pad_maximum_fusion
  32.7 2.9 %reshape_reshape.3 = bf16[128,7168]{1,0:T(8,128)(2,1)S(1)} reshape(bf16[16,2,4,7168]{3,2,1,0:T(4,128)(2,1)} %pad_maximum_fusion) | data formatting | bytes 3670016 | tf_op jit(solution)/shard_map/reshape;reshape | solution.py:86
  35.6 1.8 fusion.47
  37.5 1.7 reshape.276
  39.1 13.0 %all_to_all.41 = f32[32,4,384]{2,1,0:T(4,128)} all-to-all(f32[32,4,384]{2,1,0:T(4,128)} %reshape.276), channel_id=1, replica_groups=mesh['req'=4,'chip'=16,'core'=2] {'chip','core'}, dimensions={0} | all-to-all | bytes 393216 | tf_op jit(solution)/shard_map/all_to_all | solution.py:42
  52.1 1.0 reduce_sum.88
  53.1 0.7 broadcast_in_dim.34
  53.8 3.8 %all-to-all-start.2 = ((bf16[32,4,384]{2,1,0:T(4,128)(2,1)}), bf16[32,4,384]{2,1,0:T(4,128)(2,1)S(1)}, u32[]{:S(2)}, u32[]{:S(2)}) async-start(bf16[32,4,384]{2,1,0:T(4,128)(2,1)} %broadcast_in_dim.34), calls=%async_computation.2 | async-start | bytes 196608 | tf_op jit(solution)/shard_map/all_to_all | solution.py:27
  57.6 7.1 %fusion.70 = f32[128,672]{0,1:T(8,128)} fusion(bf16[128,7168]{1,0:T(8,128)(2,1)S(1)} %reshape_reshape.3, bf16[7168,672]{0,1:T(8,128)(2,1)} %bitcast.106), kind=kOutput, calls=%fused_computation.107 | convolution fusion | flops 1233125376 | bytes 11812864 | tf_op jit(solution)/shard_map/dot_general | solution.py:88
  64.7 0.5 all-to-all-done.2
  65.2 1.3 fusion.32
  66.5 0.7 slice_bitcast_fusion.2
  67.2 0.1 broadcast_in_dim.63
  67.3 20.2 %all_to_all.42 = bf16[16,128,224]{1,2,0:T(8,128)(2,1)S(1)} all-to-all(bf16[16,128,224]{1,2,0:T(8,128)(2,1)S(1)} %broadcast_in_dim.63), channel_id=1, replica_groups=mesh['req'=4,'chip'=16,'core'=2] {'chip'}, dimensions={0} | all-to-all | bytes 1835008 | tf_op jit(solution)/shard_map/all_to_all | solution.py:27
  87.5 2.3 collective-permute-start.2
  89.8 5.9 %copy.39 = bf16[1,256,7168]{1,2,0:T(8,128)(2,1)} copy(bf16[1,256,7168]{2,1,0:T(8,128)(2,1)} %param.27) | data formatting | bytes 7340032 | tf_op args[9]
  95.7 5.9 %copy.40 = bf16[1,256,7168]{1,2,0:T(8,128)(2,1)} copy(bf16[1,256,7168]{2,1,0:T(8,128)(2,1)} %param.28) | data formatting | bytes 7340032 | tf_op args[10]
  102.3 0.0 copy-start.7
  102.3 0.1 select_bitcast_fusion.1
  102.5 0.2 pad_maximum_fusion.1
  102.6 0.3 copy-done.7
  103.0 14.1 %conditional.1 = (bf16[32,128,228]{1,2,0:T(8,128)(2,1)}) conditional(s32[]{:T(128)} %convert_element_type.83, () %tuple.21, (s32[]{:T(128)}, s32[256]{0:T(256)S(1)}, s32[]{:T(128)}, s32[1,256]{1,0:T(1,128)S(1)}, bf16[16,2,128,224]{2,3,1,0:T(8,128)(2,1)S(1)}, /*index=5*/bf16[32,256,224]{1,2,0:T(8,128)(2,1)}, bf16[32,256,224]{1,2,0:T(8,128)(2,1)}) %tuple.38), branch_computations={%region_2.3_spmd, %region_3.6_spmd} | conditional | flops 954123264 | bytes 42241580 | solution.py:135
  103.0 0.7 compare_and_fusion
  103.7 3.6 %fusion = (f32[32,128]{1,0:T(8,128)S(1)}, f32[32,128,256]{2,1,0:T(8,128)S(1)}) fusion(pred[256]{0:T(512)(128)(4,1)S(1)} %compare_and_fusion, bf16[32,128,224]{1,2,0:T(8,128)(2,1)S(1)} %bitcast.108, bf16[32,256,224]{1,2,0:T(8,128)(2,1)} %get-tuple-element.58), kind=kOutput, calls=%fused_computation.2 | convolution fusion | flops 472903680 | bytes 9715968 | tf_op jit(solution)/shard_map/cond/branch_1_fun/hqd,hkd->hqk/dot_general | solution.py:112
  107.3 1.5 fusion.1
  108.9 0.4 copy-done.1
  109.3 1.5 fusion.10
  110.9 6.2 %concatenate.11 = bf16[32,128,228]{1,2,0:T(8,128)(2,1)} concatenate(bf16[32,128,224]{1,2,0:T(8,128)(2,1)S(1)} %fusion.10, bf16[32,128,1]{1,2,0:T(2,128)(2,1)S(1)} %copy.32, bf16[32,128,1]{1,2,0:T(2,128)(2,1)S(1)} %copy.33, bf16[32,128,1]{1,2,0:T(2,128)(2,1)S(1)} %copy.34, bf16[32,128,1]{1,2,0:T(2,128)(2,1)S(1)} %copy.35), dimensions={2} | concatenate | bytes 3735552 | tf_op jit(solution)/shard_map/cond/branch_1_fun/concatenate | solution.py:129
  117.0 4.0 %all-to-all-start.4 = ((bf16[32,128,228]{1,2,0:T(8,128)(2,1)}), bf16[32,128,228]{1,2,0:T(8,128)(2,1)S(1)}, u32[]{:S(2)}, u32[]{:S(2)}) async-start(bf16[32,128,228]{1,2,0:T(8,128)(2,1)} %get-tuple-element.85), calls=%async_computation.4 | async-start | bytes 3801088 | tf_op jit(solution)/shard_map/all_to_all | solution.py:136
  121.7 1.1 fusion.69
  122.7 0.6 copy-done.3
  123.4 0.1 fusion.51
  123.5 23.7 %all-to-all-done.4 = bf16[32,128,228]{1,2,0:T(8,128)(2,1)S(1)} async-done(((bf16[32,128,228]{1,2,0:T(8,128)(2,1)}), bf16[32,128,228]{1,2,0:T(8,128)(2,1)S(1)}, u32[]{:S(2)}, u32[]{:S(2)}) %all-to-all-start.4) | async-done | bytes 1867808 | tf_op jit(solution)/shard_map/all_to_all | solution.py:136
  147.3 0.4 multiply_reduce_fusion
  147.8 1.1 fusion.36
  148.9 0.0 copy-start.4
  148.9 0.0 copy-start.5
  148.9 0.4 convolution_convert_fusion.1
  149.3 1.1 reshape.282
  150.5 4.3 %all-to-all-start.5 = ((bf16[32,4,3584]{2,1,0:T(4,128)(2,1)}), bf16[32,4,3584]{2,1,0:T(4,128)(2,1)S(1)}, u32[]{:S(2)}, u32[]{:S(2)}) async-start(bf16[32,4,3584]{2,1,0:T(4,128)(2,1)} %reshape.282), calls=%async_computation.5 | async-start | bytes 1835008 | tf_op jit(solution)/shard_map/all_to_all | solution.py:42
  154.8 15.6 %all-to-all-done.5 = bf16[32,4,3584]{2,1,0:T(4,128)(2,1)S(1)} async-done(((bf16[32,4,3584]{2,1,0:T(4,128)(2,1)}), bf16[32,4,3584]{2,1,0:T(4,128)(2,1)S(1)}, u32[]{:S(2)}, u32[]{:S(2)}) %all-to-all-start.5) | async-done | bytes 917536 | tf_op jit(solution)/shard_map/all_to_all | solution.py:42
  170.4 0.4 convert_reduce_fusion
  170.8 0.1 multiply_reduce_fusion.1
  171.0 0.1 multiply_convert_fusion
  171.1 1.7 broadcast_in_dim.66
  172.8 7.5 %all-to-all-start.6 = ((bf16[64,4,3584]{2,1,0:T(4,128)(2,1)}), bf16[64,4,3584]{2,1,0:T(4,128)(2,1)S(1)}, u32[]{:S(2)}, u32[]{:S(2)}) async-start(bf16[64,4,3584]{2,1,0:T(4,128)(2,1)} %broadcast_in_dim.66), calls=%async_computation.6 | async-start | bytes 3670016 | tf_op jit(solution)/shard_map/all_to_all | solution.py:27
  180.3 0.8 collective-permute-start
  181.1 0.1 collective-permute-start.3
  181.2 24.5 %all-to-all-done.6 = bf16[64,4,3584]{2,1,0:T(4,128)(2,1)S(1)} async-done(((bf16[64,4,3584]{2,1,0:T(4,128)(2,1)}), bf16[64,4,3584]{2,1,0:T(4,128)(2,1)S(1)}, u32[]{:S(2)}, u32[]{:S(2)}) %all-to-all-start.6) | async-done | bytes 1835040 | tf_op jit(solution)/shard_map/all_to_all | solution.py:27
  205.7 1.5 reshape.285
  207.2 3.6 %fusion.28 = f32[2,256,224]{1,2,0:T(8,128)S(1)} fusion(bf16[256,3584,1]{1,0,2:T(8,128)(2,1)} %reshape.285, bf16[2,112,3584]{2,1,0:T(8,128)(2,1)} %collective-permute-done, bf16[2,112,3584]{2,1,0:T(8,128)(2,1)} %param.25), kind=kOutput, calls=%fused_computation.41 | convolution fusion | flops 828506112 | bytes 5505024 | tf_op jit(solution)/shard_map/td,cfd->ctf/dot_general | solution.py:180
  210.8 3.1 %convolution_convert_fusion = bf16[256,3584]{1,0:T(8,128)(2,1)} fusion(bf16[112,3584]{1,0:T(8,128)(2,1)} %collective-permute-done.3, bf16[112,3584]{1,0:T(8,128)(2,1)S(1)} %copy-done.6, f32[2,256,224]{1,2,0:T(8,128)S(1)} %fusion.28), kind=kOutput, calls=%fused_computation.28 | convolution fusion | flops 415514624 | bytes 3899392 | tf_op jit(solution)/shard_map/dot_general | solution.py:182
  213.9 3.1 %reshape.284 = bf16[64,4,3584]{2,1,0:T(4,128)(2,1)S(1)} reshape(bf16[256,3584]{1,0:T(8,128)(2,1)} %convolution_convert_fusion) | data formatting | bytes 3670016 | tf_op jit(solution)/shard_map/reshape | solution.py:41
  217.0 30.1 %all_to_all.43 = bf16[64,4,3584]{2,1,0:T(4,128)(2,1)} all-to-all(bf16[64,4,3584]{2,1,0:T(4,128)(2,1)S(1)} %reshape.284), channel_id=1, replica_groups=mesh['req'=4,'chip'=16,'core'=2] {'req','chip'}, dimensions={0} | all-to-all | bytes 3670016 | tf_op jit(solution)/shard_map/all_to_all | solution.py:42
  247.1 2.9 %reduce_sum.94 = bf16[4,3584]{1,0:T(4,128)(2,1)} reduce(bf16[64,4,3584]{2,1,0:T(4,128)(2,1)} %all_to_all.43, bf16[]{:T(256)} %constant.86.clone.1), dimensions={0}, to_apply=%region_13.14 | reduce | flops 903168 | bytes 1863682 | tf_op jit(solution)/shard_map/reduce_sum | solution.py:184
  (33 shorter events, 0.3 us)
Async XLA Ops:
  0.6 148.2 %copy-start = (bf16[224,3584]{1,0:T(8,128)(2,1)S(1)}, bf16[224,3584]{1,0:T(8,128)(2,1)}, u32[]{:S(2)}) copy-start(bf16[224,3584]{1,0:T(8,128)(2,1)} %param.23) | copy-start | bytes 4816900
  25.7 3.9 %collective-permute-start.1 = (bf16[16,4,7168]{2,1,0:T(4,128)(2,1)S(1)}, bf16[16,4,7168]{2,1,0:T(4,128)(2,1)S(1)}, u32[]{:S(2)}, u32[]{:S(2)}) collective-permute-start(bf16[16,4,7168]{2,1,0:T(4,128)(2,1)S(1)} %all_to_all.40), channel_id=1, source_target_pairs={{0,1},{1,0},{2,3},{3,2},{4,5},{5,4},{6,7},{7,6},{8,9},{9,8},{10,11... | collective-permute-start | bytes 2752520 | tf_op jit(solution)/shard_map/ppermute | solution.py:32
  53.8 11.4 %all-to-all-start.2 = ((bf16[32,4,384]{2,1,0:T(4,128)(2,1)}), bf16[32,4,384]{2,1,0:T(4,128)(2,1)S(1)}, u32[]{:S(2)}, u32[]{:S(2)}) async-start(bf16[32,4,384]{2,1,0:T(4,128)(2,1)} %broadcast_in_dim.34), calls=%async_computation.2 | async-start | bytes 196608 | tf_op jit(solution)/shard_map/all_to_all | solution.py:27
  66.5 0.7 copy-start.2
  87.5 14.8 %collective-permute-start.2 = (bf16[16,128,224]{1,2,0:T(8,128)(2,1)S(1)}, bf16[16,128,224]{1,2,0:T(8,128)(2,1)S(1)}, u32[]{:S(2)}, u32[]{:S(2)}) collective-permute-start(bf16[16,128,224]{1,2,0:T(8,128)(2,1)S(1)} %all_to_all.42), channel_id=1, source_target_pairs={{0,1},{1,0},{2,3},{3,2},{4,5},{5,4},{6,7},{7,6},{8,9},{9,8},{10,11... | collective-permute-start | bytes 2752520 | tf_op jit(solution)/shard_map/ppermute | solution.py:32
  102.3 0.7 copy-start.7
  107.3 2.0 copy-start.1
  117.0 30.1 %all-to-all-start.4 = ((bf16[32,128,228]{1,2,0:T(8,128)(2,1)}), bf16[32,128,228]{1,2,0:T(8,128)(2,1)S(1)}, u32[]{:S(2)}, u32[]{:S(2)}) async-start(bf16[32,128,228]{1,2,0:T(8,128)(2,1)} %get-tuple-element.85), calls=%async_computation.4 | async-start | bytes 3801088 | tf_op jit(solution)/shard_map/all_to_all | solution.py:136
  122.7 0.6 copy-start.3
  148.9 21.9 %copy-start.4 = (bf16[128,224]{0,1:T(8,128)(2,1)}, bf16[128,224]{0,1:T(8,128)(2,1)S(1)}, u32[]{:S(2)}) copy-start(bf16[128,224]{0,1:T(8,128)(2,1)S(1)} %fusion.36) | copy-start | bytes 172036
  148.9 5.9 %copy-start.5 = (bf16[3584]{0:T(1024)(128)(2,1)S(1)}, bf16[3584]{0:T(1024)(128)(2,1)}, u32[]{:S(2)}) copy-start(bf16[3584]{0:T(1024)(128)(2,1)} %param.24) | copy-start | bytes 21508
  150.5 20.0 %all-to-all-start.5 = ((bf16[32,4,3584]{2,1,0:T(4,128)(2,1)}), bf16[32,4,3584]{2,1,0:T(4,128)(2,1)S(1)}, u32[]{:S(2)}, u32[]{:S(2)}) async-start(bf16[32,4,3584]{2,1,0:T(4,128)(2,1)} %reshape.282), calls=%async_computation.5 | async-start | bytes 1835008 | tf_op jit(solution)/shard_map/all_to_all | solution.py:42
  172.8 32.9 %all-to-all-start.6 = ((bf16[64,4,3584]{2,1,0:T(4,128)(2,1)}), bf16[64,4,3584]{2,1,0:T(4,128)(2,1)S(1)}, u32[]{:S(2)}, u32[]{:S(2)}) async-start(bf16[64,4,3584]{2,1,0:T(4,128)(2,1)} %broadcast_in_dim.66), calls=%async_computation.6 | async-start | bytes 3670016 | tf_op jit(solution)/shard_map/all_to_all | solution.py:27
  180.3 26.9 %collective-permute-start = (bf16[2,112,3584]{2,1,0:T(8,128)(2,1)}, bf16[2,112,3584]{2,1,0:T(8,128)(2,1)}, u32[]{:S(2)}, u32[]{:S(2)}) collective-permute-start(bf16[2,112,3584]{2,1,0:T(8,128)(2,1)} %param.25), channel_id=1, source_target_pairs={{0,1},{1,0},{2,3},{3,2},{4,5},{5,4},{6,7},{7,6},{8,9},{9,8},{10,11... | collective-permute-start | bytes 4816904 | tf_op jit(solution)/shard_map/ppermute | solution.py:82
  181.1 29.7 %collective-permute-start.3 = (bf16[112,3584]{1,0:T(8,128)(2,1)}, bf16[112,3584]{1,0:T(8,128)(2,1)}, u32[]{:S(2)}, u32[]{:S(2)}) collective-permute-start(bf16[112,3584]{1,0:T(8,128)(2,1)} %param.26), channel_id=1, source_target_pairs={{0,1},{1,0},{2,3},{3,2},{4,5},{5,4},{6,7},{7,6},{8,9},{9,8},{10,11... | collective-permute-start | bytes 2408456 | tf_op jit(solution)/shard_map/ppermute | solution.py:83
  207.2 3.6 %copy-start.6 = (bf16[112,3584]{1,0:T(8,128)(2,1)S(1)}, bf16[112,3584]{1,0:T(8,128)(2,1)}, u32[]{:S(2)}) copy-start(bf16[112,3584]{1,0:T(8,128)(2,1)} %param.26) | copy-start | bytes 2408452

commit v6 on v5

--- a/solution.py
+++ b/solution.py
@@ -28,12 +28,12 @@
 
 
 def gather_wide(piece, chips):
-    own = gather_rows(piece, "chip", chips)
+    own = gather_rows(piece, "chip", chips)[:, None]
     other = lax.ppermute(own, "core", [(0, 1), (1, 0)])
-    first_core = lax.axis_index("core") == 0
-    even = jnp.where(first_core, own, other)
-    odd = jnp.where(first_core, other, own)
-    joined = jnp.stack([even, odd], axis=1)
+    core = lax.axis_index("core")
+    joined = jnp.zeros((chips, 2) + piece.shape, piece.dtype)
+    joined = lax.dynamic_update_slice_in_dim(joined, own, core, axis=1)
+    joined = lax.dynamic_update_slice_in_dim(joined, other, 1 - core, axis=1)
     return joined.reshape((2 * chips,) + piece.shape)
 
 
@@ -84,13 +84,17 @@
 
     normed = rms_scale(tokens, attn_gain)
     shard_rows = gather_wide(normed, chips).reshape(SPAN, D)
+    block_len = key_cache.shape[1]
+    key_heads = jnp.transpose(key_cache[0].reshape(block_len, HEADS, HD), (1, 0, 2))
+    value_heads = jnp.transpose(value_cache[0].reshape(block_len, HEADS, HD), (1, 0, 2))
+    shard_rows, key_heads, value_heads = lax.optimization_barrier((shard_rows, key_heads, value_heads))
     base_part = lax.optimization_barrier(
         jnp.dot(shard_rows, qkv_weight.reshape(D, 3 * local_width), preferred_element_type=jnp.float32)
     )
     sliced = lax.dynamic_slice_in_dim(shard_rows, feature_start, local_width, 1)
     partial_low = jnp.dot(sliced, adapter_down, preferred_element_type=jnp.float32)
-    low_parts = send_rows(partial_low, WIDE, wide_size)
-    own_low = jnp.sum(low_parts, axis=0).astype(jnp.bfloat16)
+    low_parts = send_rows(partial_low.astype(jnp.bfloat16), WIDE, wide_size)
+    own_low = jnp.sum(low_parts.astype(jnp.float32), axis=0).astype(jnp.bfloat16)
     lowrank = gather_rows(own_low, WIDE, wide_size).reshape(SPAN, 3, RANK)
     adapted = jnp.einsum("tcr,crd->tcd", lowrank, adapter_up, preferred_element_type=jnp.float32)
     projected = (base_part.reshape(SPAN, 3, local_width) + adapted).astype(jnp.bfloat16)
@@ -99,13 +103,10 @@
     new_values = projected[:, 2]
 
     query_heads = gather_wide(query_own, chips).reshape(HEADS, SPAN, HD)
-    block_len = key_cache.shape[1]
     block_start = wide_index * block_len
     length = cache_lengths[0]
     usable = (block_start + jnp.arange(block_len) < length) & (slot_mask[0] == 1)
 
-    key_heads = jnp.transpose(key_cache[0].reshape(block_len, HEADS, HD), (1, 0, 2))
-    value_heads = jnp.transpose(value_cache[0].reshape(block_len, HEADS, HD), (1, 0, 2))
 
     def cache_block(unused):
         scores = (

time: 254 us -> 241 us (0.949)
  blocking collectives: 85.3 us -> 61.2 us
  starting transfers between devices: 24.5 us -> 33.4 us
  local copies, waits for them, and re-layouts: 33.3 us -> 40.5 us
  other arithmetic: 13.5 us -> 10.1 us
  matrix products: 24.6 us -> 21.6 us
    all_to_all x2 -> x1, blocking collectives: 42.2 us -> 20.2 us  [gather_rows(): return lax.all_to_all(spread, axis, 0, 0, tiled=True)]
    all_to_all x2 -> x3, starting transfers between devices: 11.3 us -> 19 us  [gather_rows(): return lax.all_to_all(spread, axis, 0, 0, tiled=True)]
    another operation x6 -> x2, other arithmetic: 3.47 us -> 0.01 us  [the longest x4 3.45 us: gather_wide(): joined = jnp.stack([even, odd], axis=1)]
    dynamic_update_slice x0 -> x4, local copies, waits for them, and re-layouts: none -> 2.88 us  [the longest x2 1.48 us: gather_wide(): joined = lax.dynamic_update_slice_in_dim(joined, own, core, axis=1)]
    all_to_all x2 -> x3, waiting for transfers between devices: 25 us -> 27.3 us  [gather_rows(): return lax.all_to_all(spread, axis, 0, 0, tiled=True)]
    unnamed x16 -> x20, local copies, waits for them, and re-layouts: 12.8 us -> 12.8 us
  transfers between devices with their start and end apart: 8 -> 9, of which waited for: 5 -> 6; matrix products, arithmetic and copies ran while one was open for 10% -> 12% of each run, Pallas kernels for 0% -> 0%
where the time goes in v6:
time: 241 us; the launch traced here: 237 us
  waiting for transfers between devices  68.2 us (28%)
  blocking collectives  61.2 us (25%)
  local copies, waits for them, and re-layouts  40.5 us (17%)
  starting transfers between devices  33.4 us (14%)
  matrix products  21.6 us (9%)
  other arithmetic  10.1 us (4%)
    all_to_all x2, blocking collectives, send_rows(): return lax.all_to_all(blocks, axis, 0, 0, tiled=True)  41 us
    all_to_all x3, waiting for transfers between devices, gather_rows(): return lax.all_to_all(spread, axis, 0, 0, tiled=True)  27.3 us
    all_to_all x1, waiting for transfers between devices, body(): parts = lax.all_to_all(packed, WIDE, 0, 0, tiled=True)  23.9 us
    all_to_all x1, blocking collectives, gather_rows(): return lax.all_to_all(spread, axis, 0, 0, tiled=True)  20.2 us
    all_to_all x3, starting transfers between devices, gather_rows(): return lax.all_to_all(spread, axis, 0, 0, tiled=True)  19 us
    all_to_all x1, waiting for transfers between devices, send_rows(): return lax.all_to_all(blocks, axis, 0, 0, tiled=True)  15.6 us
    unnamed x20, local copies, waits for them, and re-layouts  12.8 us
    dot_general x1, matrix products, body(): jnp.dot(shard_rows, qkv_weight.reshape(D, 3 * local_width), preferred_ele...  7.12 us
  transfers between devices with their start and end apart: 9, of which 6 were waited for; matrix products, arithmetic and copies ran while one was open for 12% of the time, Pallas kernels for 0%

profile of v6, /device:TPU:1, one launch (start us, length us, event | category | flops | bytes accessed | tf_op | source)
XLA Modules:
  0.0 237.3 jit_solution(38751555760100412)
XLA Ops:
  0.6 0.8 convert_element_type.86
  1.5 1.0 fusion.41
  2.5 0.9 fusion.43
  3.4 1.2 broadcast_in_dim.79
  4.6 7.6 %all-to-all-start = ((bf16[16,4,7168]{2,1,0:T(4,128)(2,1)}), bf16[16,4,7168]{2,1,0:T(4,128)(2,1)S(1)}, u32[]{:S(2)}, u32[]{:S(2)}) async-start(bf16[16,4,7168]{2,1,0:T(4,128)(2,1)} %broadcast_in_dim.79), calls=%async_computation | async-start | bytes 1835008 | tf_op jit(solution)/shard_map/all_to_all | solution.py:27
  12.2 5.9 %copy.33 = bf16[1,256,7168]{1,2,0:T(8,128)(2,1)} copy(bf16[1,256,7168]{2,1,0:T(8,128)(2,1)} %param.27) | data formatting | bytes 7340032 | tf_op args[9]
  18.1 5.9 %copy.34 = bf16[1,256,7168]{1,2,0:T(8,128)(2,1)} copy(bf16[1,256,7168]{2,1,0:T(8,128)(2,1)} %param.28) | data formatting | bytes 7340032 | tf_op args[10]
  24.0 2.3 all-to-all-done
  26.3 2.8 %collective-permute-start.1 = (bf16[16,1,4,7168]{3,2,1,0:T(4,128)(2,1)S(1)}, bf16[16,1,4,7168]{3,2,1,0:T(4,128)(2,1)S(1)}, u32[]{:S(2)}, u32[]{:S(2)}) collective-permute-start(bf16[16,1,4,7168]{3,2,1,0:T(4,128)(2,1)S(1)} %bitcast.103), channel_id=1, source_target_pairs={{0,1},{1,0},{2,3},{3,2},{4,5},{5,4},{6,7},{7,6},{8,9},{9,8},{10,11... | collective-permute-start | bytes 2752520 | tf_op jit(solution)/shard_map/ppermute | solution.py:32
  29.2 2.0 broadcast_in_dim.78
  31.2 1.4 constant_dynamic-update-slice_fusion.3
  32.6 1.3 constant_dynamic-update-slice_fusion.2
  33.9 2.9 %reshape_reshape.3 = bf16[128,7168]{1,0:T(8,128)(2,1)S(1)} reshape(bf16[16,2,4,7168]{3,2,1,0:T(4,128)(2,1)} %constant_dynamic-update-slice_fusion.2) | data formatting | bytes 3670016 | tf_op jit(solution)/shard_map/reshape;reshape | solution.py:86
  36.8 1.8 convolution_convert_fusion.2
  38.6 0.9 reshape.279
  39.5 10.9 %all_to_all.40 = bf16[32,4,384]{2,1,0:T(4,128)(2,1)} all-to-all(bf16[32,4,384]{2,1,0:T(4,128)(2,1)S(1)} %reshape.279), channel_id=1, replica_groups=mesh['req'=4,'chip'=16,'core'=2] {'chip','core'}, dimensions={0} | all-to-all | bytes 196608 | tf_op jit(solution)/shard_map/all_to_all | solution.py:42
  50.4 1.0 reduce_sum.92
  51.4 0.7 broadcast_in_dim.81
  52.0 3.9 %all-to-all-start.2 = ((bf16[32,4,384]{2,1,0:T(4,128)(2,1)}), bf16[32,4,384]{2,1,0:T(4,128)(2,1)S(1)}, u32[]{:S(2)}, u32[]{:S(2)}) async-start(bf16[32,4,384]{2,1,0:T(4,128)(2,1)} %broadcast_in_dim.81), calls=%async_computation.2 | async-start | bytes 196608 | tf_op jit(solution)/shard_map/all_to_all | solution.py:27
  55.9 7.1 %fusion.69 = f32[128,672]{0,1:T(8,128)} fusion(bf16[128,7168]{1,0:T(8,128)(2,1)S(1)} %reshape_reshape.3, bf16[7168,672]{0,1:T(8,128)(2,1)} %bitcast.97), kind=kOutput, calls=%fused_computation.105 | convolution fusion | flops 1233125376 | bytes 11812864 | tf_op jit(solution)/shard_map/dot_general | solution.py:92
  63.1 0.4 all-to-all-done.2
  63.6 1.3 fusion.32
  64.9 0.7 slice_bitcast_fusion.2
  65.6 0.1 broadcast_in_dim.83
  65.7 20.2 %all_to_all.41 = bf16[16,128,224]{1,2,0:T(8,128)(2,1)S(1)} all-to-all(bf16[16,128,224]{1,2,0:T(8,128)(2,1)S(1)} %broadcast_in_dim.83), channel_id=1, replica_groups=mesh['req'=4,'chip'=16,'core'=2] {'chip'}, dimensions={0} | all-to-all | bytes 1835008 | tf_op jit(solution)/shard_map/all_to_all | solution.py:27
  85.9 2.3 collective-permute-start.2
  88.9 1.4 collective-permute-done.2
  90.3 14.4 %conditional.1 = (bf16[32,128,228]{1,2,0:T(8,128)(2,1)}) conditional(s32[]{:T(128)} %convert_element_type.84, () %tuple.23, (s32[]{:T(128)}, s32[256]{0:T(256)S(1)}, s32[]{:T(128)}, s32[1,256]{1,0:T(1,128)S(1)}, bf16[16,1,128,224]{2,3,1,0:T(8,128)(2,1)S(1)}, /*index=5*/s32[]{:T(128)}, bf16[16,1,128,224]{2,3,1,0:T(8,128)(2,1)S(1)}, s32[]{:T(128)}, ...), branch_computations={%region_2.3_spmd, %region_3.6_spmd} | conditional | flops 954123264 | bytes 62426704 | solution.py:136
  90.3 0.7 compare_and_fusion
  91.0 0.3 broadcast_in_dim.34
  91.4 0.1 constant_dynamic-update-slice_fusion.1
  91.5 0.1 constant_dynamic-update-slice_fusion
  91.6 1.8 copy-done.1
  93.4 1.6 fusion
  95.0 1.5 fusion.1
  96.6 0.4 copy-done.2
  97.0 1.5 fusion.10
  98.6 6.2 %concatenate.12 = bf16[32,128,228]{1,2,0:T(8,128)(2,1)} concatenate(bf16[32,128,224]{1,2,0:T(8,128)(2,1)S(1)} %fusion.10, bf16[32,128,1]{1,2,0:T(2,128)(2,1)S(1)} %copy.29, bf16[32,128,1]{1,2,0:T(2,128)(2,1)S(1)} %copy.30, bf16[32,128,1]{1,2,0:T(2,128)(2,1)S(1)} %copy.31, bf16[32,128,1]{1,2,0:T(2,128)(2,1)S(1)} %copy.32), dimensions={2} | concatenate | bytes 3735552 | tf_op jit(solution)/shard_map/cond/branch_1_fun/concatenate | solution.py:130
  104.7 4.0 %all-to-all-start.4 = ((bf16[32,128,228]{1,2,0:T(8,128)(2,1)}), bf16[32,128,228]{1,2,0:T(8,128)(2,1)S(1)}, u32[]{:S(2)}, u32[]{:S(2)}) async-start(bf16[32,128,228]{1,2,0:T(8,128)(2,1)} %get-tuple-element.139), calls=%async_computation.4 | async-start | bytes 3801088 | tf_op jit(solution)/shard_map/all_to_all | solution.py:137
  109.4 1.1 fusion.68
  110.5 0.6 copy-done.4
  111.1 0.1 fusion.50
  111.2 23.9 %all-to-all-done.4 = bf16[32,128,228]{1,2,0:T(8,128)(2,1)S(1)} async-done(((bf16[32,128,228]{1,2,0:T(8,128)(2,1)}), bf16[32,128,228]{1,2,0:T(8,128)(2,1)S(1)}, u32[]{:S(2)}, u32[]{:S(2)}) %all-to-all-start.4) | async-done | bytes 1867808 | tf_op jit(solution)/shard_map/all_to_all | solution.py:137
  135.2 0.4 multiply_reduce_fusion
  135.7 0.3 copy-done.5
  135.9 0.2 fusion.36
  136.2 0.4 convolution_convert_fusion.1
  136.6 1.1 reshape.285
  137.8 4.3 %all-to-all-start.5 = ((bf16[32,4,3584]{2,1,0:T(4,128)(2,1)}), bf16[32,4,3584]{2,1,0:T(4,128)(2,1)S(1)}, u32[]{:S(2)}, u32[]{:S(2)}) async-start(bf16[32,4,3584]{2,1,0:T(4,128)(2,1)} %reshape.285), calls=%async_computation.5 | async-start | bytes 1835008 | tf_op jit(solution)/shard_map/all_to_all | solution.py:42
  142.1 15.6 %all-to-all-done.5 = bf16[32,4,3584]{2,1,0:T(4,128)(2,1)S(1)} async-done(((bf16[32,4,3584]{2,1,0:T(4,128)(2,1)}), bf16[32,4,3584]{2,1,0:T(4,128)(2,1)S(1)}, u32[]{:S(2)}, u32[]{:S(2)}) %all-to-all-start.5) | async-done | bytes 917536 | tf_op jit(solution)/shard_map/all_to_all | solution.py:42
  157.8 0.4 convert_reduce_fusion
  158.1 0.1 multiply_reduce_fusion.1
  158.3 0.1 multiply_convert_fusion
  158.4 1.7 broadcast_in_dim.87
  160.1 7.5 %all-to-all-start.6 = ((bf16[64,4,3584]{2,1,0:T(4,128)(2,1)}), bf16[64,4,3584]{2,1,0:T(4,128)(2,1)S(1)}, u32[]{:S(2)}, u32[]{:S(2)}) async-start(bf16[64,4,3584]{2,1,0:T(4,128)(2,1)} %broadcast_in_dim.87), calls=%async_computation.6 | async-start | bytes 3670016 | tf_op jit(solution)/shard_map/all_to_all | solution.py:27
  167.6 0.8 collective-permute-start
  168.4 0.1 collective-permute-start.3
  168.5 24.5 %all-to-all-done.6 = bf16[64,4,3584]{2,1,0:T(4,128)(2,1)S(1)} async-done(((bf16[64,4,3584]{2,1,0:T(4,128)(2,1)}), bf16[64,4,3584]{2,1,0:T(4,128)(2,1)S(1)}, u32[]{:S(2)}, u32[]{:S(2)}) %all-to-all-start.6) | async-done | bytes 1835040 | tf_op jit(solution)/shard_map/all_to_all | solution.py:27
  193.0 1.5 reshape.288
  194.5 3.6 %fusion.28 = f32[2,256,224]{1,2,0:T(8,128)S(1)} fusion(bf16[256,3584,1]{1,0,2:T(8,128)(2,1)} %reshape.288, bf16[2,112,3584]{2,1,0:T(8,128)(2,1)} %collective-permute-done, bf16[2,112,3584]{2,1,0:T(8,128)(2,1)} %param.25), kind=kOutput, calls=%fused_computation.41 | convolution fusion | flops 828506112 | bytes 5505024 | tf_op jit(solution)/shard_map/td,cfd->ctf/dot_general | solution.py:181
  198.1 3.1 %convolution_convert_fusion = bf16[256,3584]{1,0:T(8,128)(2,1)} fusion(bf16[112,3584]{1,0:T(8,128)(2,1)} %collective-permute-done.3, bf16[112,3584]{1,0:T(8,128)(2,1)S(1)} %copy-done.9, f32[2,256,224]{1,2,0:T(8,128)S(1)} %fusion.28), kind=kOutput, calls=%fused_computation.30 | convolution fusion | flops 415514624 | bytes 3899392 | tf_op jit(solution)/shard_map/dot_general | solution.py:183
  201.2 3.1 %reshape.287 = bf16[64,4,3584]{2,1,0:T(4,128)(2,1)S(1)} reshape(bf16[256,3584]{1,0:T(8,128)(2,1)} %convolution_convert_fusion) | data formatting | bytes 3670016 | tf_op jit(solution)/shard_map/reshape | solution.py:41
  204.3 30.1 %all_to_all.42 = bf16[64,4,3584]{2,1,0:T(4,128)(2,1)} all-to-all(bf16[64,4,3584]{2,1,0:T(4,128)(2,1)S(1)} %reshape.287), channel_id=1, replica_groups=mesh['req'=4,'chip'=16,'core'=2] {'req','chip'}, dimensions={0} | all-to-all | bytes 3670016 | tf_op jit(solution)/shard_map/all_to_all | solution.py:42
  234.4 2.9 %reduce_sum.98 = bf16[4,3584]{1,0:T(4,128)(2,1)} reduce(bf16[64,4,3584]{2,1,0:T(4,128)(2,1)} %all_to_all.42, bf16[]{:T(256)} %constant.90.clone.1), dimensions={0}, to_apply=%region_13.14 | reduce | flops 903168 | bytes 1863682 | tf_op jit(solution)/shard_map/reduce_sum | solution.py:185
  (42 shorter events, 0.4 us)
Async XLA Ops:
  0.6 135.5 %copy-start = (bf16[224,3584]{1,0:T(8,128)(2,1)S(1)}, bf16[224,3584]{1,0:T(8,128)(2,1)}, u32[]{:S(2)}) copy-start(bf16[224,3584]{1,0:T(8,128)(2,1)} %param.23) | copy-start | bytes 4816900
  4.6 21.8 %all-to-all-start = ((bf16[16,4,7168]{2,1,0:T(4,128)(2,1)}), bf16[16,4,7168]{2,1,0:T(4,128)(2,1)S(1)}, u32[]{:S(2)}, u32[]{:S(2)}) async-start(bf16[16,4,7168]{2,1,0:T(4,128)(2,1)} %broadcast_in_dim.79), calls=%async_computation | async-start | bytes 1835008 | tf_op jit(solution)/shard_map/all_to_all | solution.py:27
  26.3 6.2 %collective-permute-start.1 = (bf16[16,1,4,7168]{3,2,1,0:T(4,128)(2,1)S(1)}, bf16[16,1,4,7168]{3,2,1,0:T(4,128)(2,1)S(1)}, u32[]{:S(2)}, u32[]{:S(2)}) collective-permute-start(bf16[16,1,4,7168]{3,2,1,0:T(4,128)(2,1)S(1)} %bitcast.103), channel_id=1, source_target_pairs={{0,1},{1,0},{2,3},{3,2},{4,5},{5,4},{6,7},{7,6},{8,9},{9,8},{10,11... | collective-permute-start | bytes 2752520 | tf_op jit(solution)/shard_map/ppermute | solution.py:32
  52.0 11.5 %all-to-all-start.2 = ((bf16[32,4,384]{2,1,0:T(4,128)(2,1)}), bf16[32,4,384]{2,1,0:T(4,128)(2,1)S(1)}, u32[]{:S(2)}, u32[]{:S(2)}) async-start(bf16[32,4,384]{2,1,0:T(4,128)(2,1)} %broadcast_in_dim.81), calls=%async_computation.2 | async-start | bytes 196608 | tf_op jit(solution)/shard_map/all_to_all | solution.py:27
  63.5 26.8 %copy-start.10 = (s32[1,256]{1,0:T(1,128)S(1)}, s32[1,256]{1,0:T(1,128)}, u32[]{:S(2)}) copy-start(s32[1,256]{1,0:T(1,128)} %param.30) | copy-start | bytes 3076
  64.8 0.7 copy-start.3
  85.9 4.4 %collective-permute-start.2 = (bf16[16,1,128,224]{2,3,1,0:T(8,128)(2,1)S(1)}, bf16[16,1,128,224]{2,3,1,0:T(8,128)(2,1)S(1)}, u32[]{:S(2)}, u32[]{:S(2)}) collective-permute-start(bf16[16,1,128,224]{2,3,1,0:T(8,128)(2,1)S(1)} %bitcast.101), channel_id=1, source_target_pairs={{0,1},{1,0},{2,3},{3,2},{4,5},{5,4},{6,7},{7,6},{8,9},{9,8},{10,11... | collective-permute-start | bytes 2752520 | tf_op jit(solution)/shard_map/ppermute | solution.py:32
  91.4 2.0 copy-start.1
  95.0 2.0 copy-start.2
  104.7 30.3 %all-to-all-start.4 = ((bf16[32,128,228]{1,2,0:T(8,128)(2,1)}), bf16[32,128,228]{1,2,0:T(8,128)(2,1)S(1)}, u32[]{:S(2)}, u32[]{:S(2)}) async-start(bf16[32,128,228]{1,2,0:T(8,128)(2,1)} %get-tuple-element.139), calls=%async_computation.4 | async-start | bytes 3801088 | tf_op jit(solution)/shard_map/all_to_all | solution.py:137
  110.5 0.6 copy-start.4
  135.1 0.8 copy-start.5
  135.1 0.8 copy-start.6
  136.2 1.6 copy-start.7
  136.6 5.5 %copy-start.8 = (bf16[3584]{0:T(1024)(128)(2,1)S(1)}, bf16[3584]{0:T(1024)(128)(2,1)}, u32[]{:S(2)}) copy-start(bf16[3584]{0:T(1024)(128)(2,1)} %param.24) | copy-start | bytes 21508
  137.8 20.0 %all-to-all-start.5 = ((bf16[32,4,3584]{2,1,0:T(4,128)(2,1)}), bf16[32,4,3584]{2,1,0:T(4,128)(2,1)S(1)}, u32[]{:S(2)}, u32[]{:S(2)}) async-start(bf16[32,4,3584]{2,1,0:T(4,128)(2,1)} %reshape.285), calls=%async_computation.5 | async-start | bytes 1835008 | tf_op jit(solution)/shard_map/all_to_all | solution.py:42
  160.1 32.9 %all-to-all-start.6 = ((bf16[64,4,3584]{2,1,0:T(4,128)(2,1)}), bf16[64,4,3584]{2,1,0:T(4,128)(2,1)S(1)}, u32[]{:S(2)}, u32[]{:S(2)}) async-start(bf16[64,4,3584]{2,1,0:T(4,128)(2,1)} %broadcast_in_dim.87), calls=%async_computation.6 | async-start | bytes 3670016 | tf_op jit(solution)/shard_map/all_to_all | solution.py:27
  167.6 26.9 %collective-permute-start = (bf16[2,112,3584]{2,1,0:T(8,128)(2,1)}, bf16[2,112,3584]{2,1,0:T(8,128)(2,1)}, u32[]{:S(2)}, u32[]{:S(2)}) collective-permute-start(bf16[2,112,3584]{2,1,0:T(8,128)(2,1)} %param.25), channel_id=1, source_target_pairs={{0,1},{1,0},{2,3},{3,2},{4,5},{5,4},{6,7},{7,6},{8,9},{9,8},{10,11... | collective-permute-start | bytes 4816904 | tf_op jit(solution)/shard_map/ppermute | solution.py:82
  168.4 29.7 %collective-permute-start.3 = (bf16[112,3584]{1,0:T(8,128)(2,1)}, bf16[112,3584]{1,0:T(8,128)(2,1)}, u32[]{:S(2)}, u32[]{:S(2)}) collective-permute-start(bf16[112,3584]{1,0:T(8,128)(2,1)} %param.26), channel_id=1, source_target_pairs={{0,1},{1,0},{2,3},{3,2},{4,5},{5,4},{6,7},{7,6},{8,9},{9,8},{10,11... | collective-permute-start | bytes 2408456 | tf_op jit(solution)/shard_map/ppermute | solution.py:83
  194.5 3.6 %copy-start.9 = (bf16[112,3584]{1,0:T(8,128)(2,1)S(1)}, bf16[112,3584]{1,0:T(8,128)(2,1)}, u32[]{:S(2)}) copy-start(bf16[112,3584]{1,0:T(8,128)(2,1)} %param.26) | copy-start | bytes 2408452

commit v7 on v6

--- a/solution.py
+++ b/solution.py
@@ -86,15 +86,18 @@
     shard_rows = gather_wide(normed, chips).reshape(SPAN, D)
     block_len = key_cache.shape[1]
     key_heads = jnp.transpose(key_cache[0].reshape(block_len, HEADS, HD), (1, 0, 2))
-    value_heads = jnp.transpose(value_cache[0].reshape(block_len, HEADS, HD), (1, 0, 2))
+    value_heads = jnp.pad(
+        jnp.transpose(value_cache[0].reshape(block_len, HEADS, HD), (1, 0, 2)),
+        ((0, 0), (0, 0), (0, 4)),
+    )
     shard_rows, key_heads, value_heads = lax.optimization_barrier((shard_rows, key_heads, value_heads))
     base_part = lax.optimization_barrier(
         jnp.dot(shard_rows, qkv_weight.reshape(D, 3 * local_width), preferred_element_type=jnp.float32)
     )
     sliced = lax.dynamic_slice_in_dim(shard_rows, feature_start, local_width, 1)
     partial_low = jnp.dot(sliced, adapter_down, preferred_element_type=jnp.float32)
-    low_parts = send_rows(partial_low.astype(jnp.bfloat16), WIDE, wide_size)
-    own_low = jnp.sum(low_parts.astype(jnp.float32), axis=0).astype(jnp.bfloat16)
+    low_parts = send_rows(partial_low, WIDE, wide_size)
+    own_low = jnp.sum(low_parts, axis=0).astype(jnp.bfloat16)
     lowrank = gather_rows(own_low, WIDE, wide_size).reshape(SPAN, 3, RANK)
     adapted = jnp.einsum("tcr,crd->tcd", lowrank, adapter_up, preferred_element_type=jnp.float32)
     projected = (base_part.reshape(SPAN, 3, local_width) + adapted).astype(jnp.bfloat16)
@@ -127,7 +130,7 @@
         )
         total_high, total_low = split_pair(totals)
         stats = jnp.stack([high, low, total_high, total_low], axis=-1).astype(jnp.bfloat16)
-        return jnp.concatenate([numerator.astype(jnp.bfloat16), stats], axis=-1)
+        return lax.dynamic_update_slice(numerator.astype(jnp.bfloat16), stats, (0, 0, HD))
 
     def skipped(unused):
         stats = jnp.zeros((HEADS, SPAN, 4), jnp.bfloat16).at[..., 0].set(NEG_LARGE)

time: 241 us -> 242 us (level)
  blocking collectives: 61.2 us -> 66 us
    concatenate x1 -> x0, local copies, waits for them, and re-layouts: 6.17 us -> none  [cache_block(): return jnp.concatenate([numerator.astype(jnp.bfloat16), stats], axis=-1)]
    all_to_all x2, blocking collectives: 41 us -> 45.8 us  [send_rows(): return lax.all_to_all(blocks, axis, 0, 0, tiled=True)]
    pad x0 -> x1, local copies, waits for them, and re-layouts: none -> 4.11 us  [body(): jnp.pad(jnp.transpose(value_cache[0].reshape(block_len, HEADS, HD), (1, 0...]
  transfers between devices with their start and end apart: 9 -> 9, of which waited for: 6 -> 5; matrix products, arithmetic and copies ran while one was open for 12% -> 14% of each run, Pallas kernels for 0% -> 0%
where the time goes in v7:
time: 242 us; the launch traced here: 238 us
  blocking collectives  66 us (27%)
  waiting for transfers between devices  65.9 us (27%)
  local copies, waits for them, and re-layouts  39.7 us (16%)
  starting transfers between devices  31.5 us (13%)
  matrix products  22.8 us (9%)
  other arithmetic  10.1 us (4%)
    all_to_all x2, blocking collectives, send_rows(): return lax.all_to_all(blocks, axis, 0, 0, tiled=True)  45.8 us
    all_to_all x3, waiting for transfers between devices, gather_rows(): return lax.all_to_all(spread, axis, 0, 0, tiled=True)  25 us
    all_to_all x1, waiting for transfers between devices, body(): parts = lax.all_to_all(packed, WIDE, 0, 0, tiled=True)  23.9 us
    all_to_all x1, blocking collectives, gather_rows(): return lax.all_to_all(spread, axis, 0, 0, tiled=True)  20.2 us
    all_to_all x3, starting transfers between devices, gather_rows(): return lax.all_to_all(spread, axis, 0, 0, tiled=True)  18.9 us
    all_to_all x1, waiting for transfers between devices, send_rows(): return lax.all_to_all(blocks, axis, 0, 0, tiled=True)  15.6 us
    unnamed x20, local copies, waits for them, and re-layouts  12.8 us
    dot_general x1, matrix products, body(): jnp.dot(shard_rows, qkv_weight.reshape(D, 3 * local_width), preferred_ele...  7.09 us
  transfers between devices with their start and end apart: 9, of which 5 were waited for; matrix products, arithmetic and copies ran while one was open for 14% of the time, Pallas kernels for 0%

profile of v7, /device:TPU:1, one launch (start us, length us, event | category | flops | bytes accessed | tf_op | source)
XLA Modules:
  0.0 238.3 jit_solution(2378952777815842022)
XLA Ops:
  0.6 0.8 convert_element_type.90
  1.5 1.0 fusion.41
  2.5 0.9 fusion.43
  3.4 1.1 broadcast_in_dim.79
  4.6 7.6 %all-to-all-start = ((bf16[16,4,7168]{2,1,0:T(4,128)(2,1)}), bf16[16,4,7168]{2,1,0:T(4,128)(2,1)S(1)}, u32[]{:S(2)}, u32[]{:S(2)}) async-start(bf16[16,4,7168]{2,1,0:T(4,128)(2,1)} %broadcast_in_dim.79), calls=%async_computation | async-start | bytes 1835008 | tf_op jit(solution)/shard_map/all_to_all | solution.py:27
  12.1 5.9 %copy.31 = bf16[1,256,7168]{1,2,0:T(8,128)(2,1)} copy(bf16[1,256,7168]{2,1,0:T(8,128)(2,1)} %param.28) | data formatting | bytes 7340032 | tf_op args[10]
  18.1 5.9 %copy.30 = bf16[1,256,7168]{1,2,0:T(8,128)(2,1)} copy(bf16[1,256,7168]{2,1,0:T(8,128)(2,1)} %param.27) | data formatting | bytes 7340032 | tf_op args[9]
  24.0 4.1 %pad.7 = bf16[32,256,228]{1,2,0:T(8,128)(2,1)} pad(bf16[32,256,224]{1,2,0:T(8,128)(2,1)} %bitcast.99, bf16[]{:T(256)} %constant.97.clone.1), padding=0_0x0_0x0_4 | pad | bytes 7405570 | tf_op jit(solution)/shard_map/jit(_pad)/pad | solution.py:89
  28.1 1.1 collective-permute-start.1
  29.2 2.0 broadcast_in_dim.78
  31.2 1.3 constant_dynamic-update-slice_fusion.3
  32.5 1.3 constant_dynamic-update-slice_fusion.2
  33.8 2.9 %reshape_reshape.3 = bf16[128,7168]{1,0:T(8,128)(2,1)S(1)} reshape(bf16[16,2,4,7168]{3,2,1,0:T(4,128)(2,1)} %constant_dynamic-update-slice_fusion.2) | data formatting | bytes 3670016 | tf_op jit(solution)/shard_map/reshape;reshape | solution.py:86
  36.7 1.8 fusion.47
  38.6 1.7 reshape.281
  40.2 15.7 %all_to_all.40 = f32[32,4,384]{2,1,0:T(4,128)} all-to-all(f32[32,4,384]{2,1,0:T(4,128)} %reshape.281), channel_id=1, replica_groups=mesh['req'=4,'chip'=16,'core'=2] {'chip','core'}, dimensions={0} | all-to-all | bytes 393216 | tf_op jit(solution)/shard_map/all_to_all | solution.py:42
  55.9 1.0 reduce_sum.89
  56.9 0.7 broadcast_in_dim.81
  57.5 3.8 %all-to-all-start.2 = ((bf16[32,4,384]{2,1,0:T(4,128)(2,1)}), bf16[32,4,384]{2,1,0:T(4,128)(2,1)S(1)}, u32[]{:S(2)}, u32[]{:S(2)}) async-start(bf16[32,4,384]{2,1,0:T(4,128)(2,1)} %broadcast_in_dim.81), calls=%async_computation.2 | async-start | bytes 196608 | tf_op jit(solution)/shard_map/all_to_all | solution.py:27
  61.3 7.1 %fusion.70 = f32[128,672]{0,1:T(8,128)} fusion(bf16[128,7168]{1,0:T(8,128)(2,1)S(1)} %reshape_reshape.3, bf16[7168,672]{0,1:T(8,128)(2,1)} %bitcast.97), kind=kOutput, calls=%fused_computation.107 | convolution fusion | flops 1233125376 | bytes 11812864 | tf_op jit(solution)/shard_map/dot_general | solution.py:95
  68.4 0.5 all-to-all-done.2
  69.0 1.3 fusion.32
  70.3 0.7 slice_bitcast_fusion.2
  71.0 0.1 broadcast_in_dim.83
  71.1 20.2 %all_to_all.41 = bf16[16,128,224]{1,2,0:T(8,128)(2,1)S(1)} all-to-all(bf16[16,128,224]{1,2,0:T(8,128)(2,1)S(1)} %broadcast_in_dim.83), channel_id=1, replica_groups=mesh['req'=4,'chip'=16,'core'=2] {'chip'}, dimensions={0} | all-to-all | bytes 1835008 | tf_op jit(solution)/shard_map/all_to_all | solution.py:27
  91.3 2.3 collective-permute-start.2
  94.2 1.4 collective-permute-done.2
  95.7 10.0 %conditional.1 = (bf16[32,128,228]{1,2,0:T(8,128)(2,1)}) conditional(s32[]{:T(128)} %convert_element_type.88, () %tuple.23, (s32[]{:T(128)}, s32[256]{0:T(256)S(1)}, s32[]{:T(128)}, s32[1,256]{1,0:T(1,128)S(1)}, bf16[16,1,128,224]{2,3,1,0:T(8,128)(2,1)S(1)}, /*index=5*/s32[]{:T(128)}, bf16[16,1,128,224]{2,3,1,0:T(8,128)(2,1)S(1)}, s32[]{:T(128)}, ...), branch_computations={%region_2.3_spmd, %region_3.6_spmd} | conditional | flops 962577408 | bytes 59117136 | solution.py:139
  95.7 0.7 compare_and_fusion
  96.4 0.3 broadcast_in_dim.34
  96.7 0.1 constant_dynamic-update-slice_fusion.1
  96.9 0.1 constant_dynamic-update-slice_fusion
  97.0 1.8 copy-done.1
  98.8 1.6 fusion
  100.4 1.5 fusion.1
  102.0 0.5 copy-done.2
  102.4 2.7 %fusion.10 = bf16[32,128,228]{1,2,0:T(8,128)(2,1)} fusion(bf16[32,256,228]{1,2,0:T(8,128)(2,1)S(1)} %copy-done.2, f32[32,128,256]{2,1,0:T(8,128)S(1)} %get-tuple-element.131, f32[32,128]{1,0:T(8,128)S(1)} %reduce-precision_add_fusion, pred[256]{0:T(512)(128)(4,1)S(1)} %compare_and_fusion), kind=kOutput, calls=%fused_computation.11 | convolution fusion | flops 484327424 | bytes 9814272 | tf_op jit(solution)/shard_map/cond/branch_1_fun/hqk,hkd->hqd/dot_general | solution.py:125
  105.1 0.6 copy_dynamic-update-slice_fusion
  105.7 4.0 %all-to-all-start.4 = ((bf16[32,128,228]{1,2,0:T(8,128)(2,1)}), bf16[32,128,228]{1,2,0:T(8,128)(2,1)S(1)}, u32[]{:S(2)}, u32[]{:S(2)}) async-start(bf16[32,128,228]{1,2,0:T(8,128)(2,1)} %get-tuple-element.141), calls=%async_computation.4 | async-start | bytes 3801088 | tf_op jit(solution)/shard_map/all_to_all | solution.py:140
  110.4 1.1 fusion.69
  111.5 0.6 copy-done.4
  112.1 0.1 fusion.51
  112.2 23.9 %all-to-all-done.4 = bf16[32,128,228]{1,2,0:T(8,128)(2,1)S(1)} async-done(((bf16[32,128,228]{1,2,0:T(8,128)(2,1)}), bf16[32,128,228]{1,2,0:T(8,128)(2,1)S(1)}, u32[]{:S(2)}, u32[]{:S(2)}) %all-to-all-start.4) | async-done | bytes 1867808 | tf_op jit(solution)/shard_map/all_to_all | solution.py:140
  136.2 0.4 multiply_reduce_fusion
  136.7 0.3 copy-done.5
  136.9 0.2 fusion.36
  137.2 0.4 convolution_convert_fusion.1
  137.6 1.1 reshape.287
  138.8 4.3 %all-to-all-start.5 = ((bf16[32,4,3584]{2,1,0:T(4,128)(2,1)}), bf16[32,4,3584]{2,1,0:T(4,128)(2,1)S(1)}, u32[]{:S(2)}, u32[]{:S(2)}) async-start(bf16[32,4,3584]{2,1,0:T(4,128)(2,1)} %reshape.287), calls=%async_computation.5 | async-start | bytes 1835008 | tf_op jit(solution)/shard_map/all_to_all | solution.py:42
  143.1 15.6 %all-to-all-done.5 = bf16[32,4,3584]{2,1,0:T(4,128)(2,1)S(1)} async-done(((bf16[32,4,3584]{2,1,0:T(4,128)(2,1)}), bf16[32,4,3584]{2,1,0:T(4,128)(2,1)S(1)}, u32[]{:S(2)}, u32[]{:S(2)}) %all-to-all-start.5) | async-done | bytes 917536 | tf_op jit(solution)/shard_map/all_to_all | solution.py:42
  158.7 0.4 convert_reduce_fusion
  159.1 0.1 multiply_reduce_fusion.1
  159.3 0.1 multiply_convert_fusion
  159.4 1.7 broadcast_in_dim.87
  161.1 7.5 %all-to-all-start.6 = ((bf16[64,4,3584]{2,1,0:T(4,128)(2,1)}), bf16[64,4,3584]{2,1,0:T(4,128)(2,1)S(1)}, u32[]{:S(2)}, u32[]{:S(2)}) async-start(bf16[64,4,3584]{2,1,0:T(4,128)(2,1)} %broadcast_in_dim.87), calls=%async_computation.6 | async-start | bytes 3670016 | tf_op jit(solution)/shard_map/all_to_all | solution.py:27
  168.7 0.8 collective-permute-start
  169.4 0.1 collective-permute-start.3
  169.5 24.5 %all-to-all-done.6 = bf16[64,4,3584]{2,1,0:T(4,128)(2,1)S(1)} async-done(((bf16[64,4,3584]{2,1,0:T(4,128)(2,1)}), bf16[64,4,3584]{2,1,0:T(4,128)(2,1)S(1)}, u32[]{:S(2)}, u32[]{:S(2)}) %all-to-all-start.6) | async-done | bytes 1835040 | tf_op jit(solution)/shard_map/all_to_all | solution.py:27
  194.0 1.5 reshape.290
  195.5 3.6 %fusion.28 = f32[2,256,224]{1,2,0:T(8,128)S(1)} fusion(bf16[256,3584,1]{1,0,2:T(8,128)(2,1)} %reshape.290, bf16[2,112,3584]{2,1,0:T(8,128)(2,1)} %collective-permute-done, bf16[2,112,3584]{2,1,0:T(8,128)(2,1)} %param.25), kind=kOutput, calls=%fused_computation.43 | convolution fusion | flops 828506112 | bytes 5505024 | tf_op jit(solution)/shard_map/td,cfd->ctf/dot_general | solution.py:184
  199.1 3.1 %convolution_convert_fusion = bf16[256,3584]{1,0:T(8,128)(2,1)} fusion(bf16[112,3584]{1,0:T(8,128)(2,1)} %collective-permute-done.3, bf16[112,3584]{1,0:T(8,128)(2,1)S(1)} %copy-done.9, f32[2,256,224]{1,2,0:T(8,128)S(1)} %fusion.28), kind=kOutput, calls=%fused_computation.32 | convolution fusion | flops 415514624 | bytes 3899392 | tf_op jit(solution)/shard_map/dot_general | solution.py:186
  202.2 3.1 %reshape.289 = bf16[64,4,3584]{2,1,0:T(4,128)(2,1)S(1)} reshape(bf16[256,3584]{1,0:T(8,128)(2,1)} %convolution_convert_fusion) | data formatting | bytes 3670016 | tf_op jit(solution)/shard_map/reshape | solution.py:41
  205.3 30.1 %all_to_all.42 = bf16[64,4,3584]{2,1,0:T(4,128)(2,1)} all-to-all(bf16[64,4,3584]{2,1,0:T(4,128)(2,1)S(1)} %reshape.289), channel_id=1, replica_groups=mesh['req'=4,'chip'=16,'core'=2] {'req','chip'}, dimensions={0} | all-to-all | bytes 3670016 | tf_op jit(solution)/shard_map/all_to_all | solution.py:42
  235.4 2.9 %reduce_sum.95 = bf16[4,3584]{1,0:T(4,128)(2,1)} reduce(bf16[64,4,3584]{2,1,0:T(4,128)(2,1)} %all_to_all.42, bf16[]{:T(256)} %constant.97.clone.1), dimensions={0}, to_apply=%region_13.14 | reduce | flops 903168 | bytes 1863682 | tf_op jit(solution)/shard_map/reduce_sum | solution.py:188
  (39 shorter events, 0.3 us)
Async XLA Ops:
  0.6 136.5 %copy-start = (bf16[224,3584]{1,0:T(8,128)(2,1)S(1)}, bf16[224,3584]{1,0:T(8,128)(2,1)}, u32[]{:S(2)}) copy-start(bf16[224,3584]{1,0:T(8,128)(2,1)} %param.23) | copy-start | bytes 4816900
  4.6 23.6 %all-to-all-start = ((bf16[16,4,7168]{2,1,0:T(4,128)(2,1)}), bf16[16,4,7168]{2,1,0:T(4,128)(2,1)S(1)}, u32[]{:S(2)}, u32[]{:S(2)}) async-start(bf16[16,4,7168]{2,1,0:T(4,128)(2,1)} %broadcast_in_dim.79), calls=%async_computation | async-start | bytes 1835008 | tf_op jit(solution)/shard_map/all_to_all | solution.py:27
  28.1 4.4 %collective-permute-start.1 = (bf16[16,1,4,7168]{3,2,1,0:T(4,128)(2,1)S(1)}, bf16[16,1,4,7168]{3,2,1,0:T(4,128)(2,1)S(1)}, u32[]{:S(2)}, u32[]{:S(2)}) collective-permute-start(bf16[16,1,4,7168]{3,2,1,0:T(4,128)(2,1)S(1)} %bitcast.103), channel_id=1, source_target_pairs={{0,1},{1,0},{2,3},{3,2},{4,5},{5,4},{6,7},{7,6},{8,9},{9,8},{10,11... | collective-permute-start | bytes 2752520 | tf_op jit(solution)/shard_map/ppermute | solution.py:32
  57.5 11.4 %all-to-all-start.2 = ((bf16[32,4,384]{2,1,0:T(4,128)(2,1)}), bf16[32,4,384]{2,1,0:T(4,128)(2,1)S(1)}, u32[]{:S(2)}, u32[]{:S(2)}) async-start(bf16[32,4,384]{2,1,0:T(4,128)(2,1)} %broadcast_in_dim.81), calls=%async_computation.2 | async-start | bytes 196608 | tf_op jit(solution)/shard_map/all_to_all | solution.py:27
  69.0 26.7 %copy-start.10 = (s32[1,256]{1,0:T(1,128)S(1)}, s32[1,256]{1,0:T(1,128)}, u32[]{:S(2)}) copy-start(s32[1,256]{1,0:T(1,128)} %param.30) | copy-start | bytes 3076
  70.3 0.7 copy-start.3
  91.3 4.4 %collective-permute-start.2 = (bf16[16,1,128,224]{2,3,1,0:T(8,128)(2,1)S(1)}, bf16[16,1,128,224]{2,3,1,0:T(8,128)(2,1)S(1)}, u32[]{:S(2)}, u32[]{:S(2)}) collective-permute-start(bf16[16,1,128,224]{2,3,1,0:T(8,128)(2,1)S(1)} %bitcast.101), channel_id=1, source_target_pairs={{0,1},{1,0},{2,3},{3,2},{4,5},{5,4},{6,7},{7,6},{8,9},{9,8},{10,11... | collective-permute-start | bytes 2752520 | tf_op jit(solution)/shard_map/ppermute | solution.py:32
  96.7 2.0 copy-start.1
  100.4 2.1 copy-start.2
  105.7 30.3 %all-to-all-start.4 = ((bf16[32,128,228]{1,2,0:T(8,128)(2,1)}), bf16[32,128,228]{1,2,0:T(8,128)(2,1)S(1)}, u32[]{:S(2)}, u32[]{:S(2)}) async-start(bf16[32,128,228]{1,2,0:T(8,128)(2,1)} %get-tuple-element.141), calls=%async_computation.4 | async-start | bytes 3801088 | tf_op jit(solution)/shard_map/all_to_all | solution.py:140
  111.5 0.6 copy-start.4
  136.1 0.8 copy-start.5
  136.1 0.8 copy-start.6
  137.2 1.6 copy-start.7
  137.6 5.5 %copy-start.8 = (bf16[3584]{0:T(1024)(128)(2,1)S(1)}, bf16[3584]{0:T(1024)(128)(2,1)}, u32[]{:S(2)}) copy-start(bf16[3584]{0:T(1024)(128)(2,1)} %param.24) | copy-start | bytes 21508
  138.8 20.0 %all-to-all-start.5 = ((bf16[32,4,3584]{2,1,0:T(4,128)(2,1)}), bf16[32,4,3584]{2,1,0:T(4,128)(2,1)S(1)}, u32[]{:S(2)}, u32[]{:S(2)}) async-start(bf16[32,4,3584]{2,1,0:T(4,128)(2,1)} %reshape.287), calls=%async_computation.5 | async-start | bytes 1835008 | tf_op jit(solution)/shard_map/all_to_all | solution.py:42
  161.1 32.9 %all-to-all-start.6 = ((bf16[64,4,3584]{2,1,0:T(4,128)(2,1)}), bf16[64,4,3584]{2,1,0:T(4,128)(2,1)S(1)}, u32[]{:S(2)}, u32[]{:S(2)}) async-start(bf16[64,4,3584]{2,1,0:T(4,128)(2,1)} %broadcast_in_dim.87), calls=%async_computation.6 | async-start | bytes 3670016 | tf_op jit(solution)/shard_map/all_to_all | solution.py:27
  168.7 26.9 %collective-permute-start = (bf16[2,112,3584]{2,1,0:T(8,128)(2,1)}, bf16[2,112,3584]{2,1,0:T(8,128)(2,1)}, u32[]{:S(2)}, u32[]{:S(2)}) collective-permute-start(bf16[2,112,3584]{2,1,0:T(8,128)(2,1)} %param.25), channel_id=1, source_target_pairs={{0,1},{1,0},{2,3},{3,2},{4,5},{5,4},{6,7},{7,6},{8,9},{9,8},{10,11... | collective-permute-start | bytes 4816904 | tf_op jit(solution)/shard_map/ppermute | solution.py:82
  169.4 29.7 %collective-permute-start.3 = (bf16[112,3584]{1,0:T(8,128)(2,1)}, bf16[112,3584]{1,0:T(8,128)(2,1)}, u32[]{:S(2)}, u32[]{:S(2)}) collective-permute-start(bf16[112,3584]{1,0:T(8,128)(2,1)} %param.26), channel_id=1, source_target_pairs={{0,1},{1,0},{2,3},{3,2},{4,5},{5,4},{6,7},{7,6},{8,9},{9,8},{10,11... | collective-permute-start | bytes 2408456 | tf_op jit(solution)/shard_map/ppermute | solution.py:83
  195.5 3.6 %copy-start.9 = (bf16[112,3584]{1,0:T(8,128)(2,1)S(1)}, bf16[112,3584]{1,0:T(8,128)(2,1)}, u32[]{:S(2)}) copy-start(bf16[112,3584]{1,0:T(8,128)(2,1)} %param.26) | copy-start | bytes 2408452

commit v8 on v7

--- a/solution.py
+++ b/solution.py
@@ -27,13 +27,20 @@
     return lax.all_to_all(spread, axis, 0, 0, tiled=True)
 
 
-def gather_wide(piece, chips):
-    own = gather_rows(piece, "chip", chips)[:, None]
+def gather_wide(piece, chips, along_rows):
+    own = gather_rows(piece, "chip", chips)
     other = lax.ppermute(own, "core", [(0, 1), (1, 0)])
     core = lax.axis_index("core")
-    joined = jnp.zeros((chips, 2) + piece.shape, piece.dtype)
-    joined = lax.dynamic_update_slice_in_dim(joined, own, core, axis=1)
-    joined = lax.dynamic_update_slice_in_dim(joined, other, 1 - core, axis=1)
+    if along_rows:
+        rows = piece.shape[0]
+        joined = jnp.zeros((chips, 2 * rows) + piece.shape[1:], piece.dtype)
+        own_at, other_at = core * rows, (1 - core) * rows
+    else:
+        own, other = own[:, None], other[:, None]
+        joined = jnp.zeros((chips, 2) + piece.shape, piece.dtype)
+        own_at, other_at = core, 1 - core
+    joined = lax.dynamic_update_slice_in_dim(joined, own, own_at, axis=1)
+    joined = lax.dynamic_update_slice_in_dim(joined, other, other_at, axis=1)
     return joined.reshape((2 * chips,) + piece.shape)
 
 
@@ -83,7 +90,7 @@
     chip_down = jnp.concatenate([down_weight, lax.ppermute(down_weight, "core", swap)], axis=0)
 
     normed = rms_scale(tokens, attn_gain)
-    shard_rows = gather_wide(normed, chips).reshape(SPAN, D)
+    shard_rows = gather_wide(normed, chips, True).reshape(SPAN, D)
     block_len = key_cache.shape[1]
     key_heads = jnp.transpose(key_cache[0].reshape(block_len, HEADS, HD), (1, 0, 2))
     value_heads = jnp.pad(
@@ -105,7 +112,7 @@
     new_keys = projected[:, 1]
     new_values = projected[:, 2]
 
-    query_heads = gather_wide(query_own, chips).reshape(HEADS, SPAN, HD)
+    query_heads = gather_wide(query_own, chips, False).reshape(HEADS, SPAN, HD)
     block_start = wide_index * block_len
     length = cache_lengths[0]
     usable = (block_start + jnp.arange(block_len) < length) & (slot_mask[0] == 1)
@@ -180,11 +187,11 @@
     out_parts = send_rows(head_out.astype(jnp.bfloat16), WIDE, wide_size)
     attn_out = jnp.sum(out_parts.astype(jnp.float32), axis=0)
     normed_mid = rms_scale(attn_out, mlp_gain)
-    half_rows = gather_rows(normed_mid, HALF, half_size).reshape(half_size * own_rows, -1)
-    both = jnp.einsum("td,cfd->ctf", half_rows, chip_gate, preferred_element_type=jnp.float32)
+    half_rows = gather_rows(normed_mid, HALF, half_size)
+    both = jnp.einsum("gtd,cfd->cgtf", half_rows, chip_gate, preferred_element_type=jnp.float32)
     hidden = (jax.nn.silu(both[0]) * both[1]).astype(jnp.bfloat16)
-    ffn_part = jnp.dot(hidden, chip_down, preferred_element_type=jnp.float32)
-    ffn_parts = send_rows(ffn_part.astype(jnp.bfloat16), HALF, half_size)
+    ffn_part = jnp.einsum("gtf,fd->gtd", hidden, chip_down, preferred_element_type=jnp.float32)
+    ffn_parts = lax.all_to_all(ffn_part.astype(jnp.bfloat16), HALF, 0, 0, tiled=True)
     hidden_out = jnp.sum(ffn_parts.astype(jnp.float32), axis=0).astype(jnp.bfloat16)
     return (hidden_out, attention, new_keys, new_values)
 

time: 242 us -> 244 us (level)
  blocking collectives: 66 us -> 84.9 us
  local copies, waits for them, and re-layouts: 39.7 us -> 32.1 us
  starting transfers between devices: 31.5 us -> 24.6 us
    all_to_all x2 -> x1, blocking collectives: 45.8 us -> 12.6 us  [send_rows(): return lax.all_to_all(blocks, axis, 0, 0, tiled=True)]
    all_to_all x0 -> x1, blocking collectives: none -> 30 us  [body(): lax.all_to_all(ffn_part.astype(jnp.bfloat16), HALF, 0, 0, tiled=True)]
    all_to_all x1 -> x2, blocking collectives: 20.2 us -> 42.3 us  [gather_rows(): return lax.all_to_all(spread, axis, 0, 0, tiled=True)]
    all_to_all x3 -> x2, starting transfers between devices: 18.9 us -> 11.3 us  [gather_rows(): return lax.all_to_all(spread, axis, 0, 0, tiled=True)]
    all_to_all x3 -> x2, waiting for transfers between devices: 25 us -> 21.7 us  [gather_rows(): return lax.all_to_all(spread, axis, 0, 0, tiled=True)]
    ppermute x1, waiting for transfers between devices: 0.01 us -> 3.33 us  [body(): lax.ppermute(gate_up, 'core', swap)]
    reshape x3 -> x2, local copies, waits for them, and re-layouts: 5.91 us -> 2.79 us  [send_rows(): values.reshape((count, values.shape[0] // count) + values.shape[1:])]
    another operation x2 -> x1, local copies, waits for them, and re-layouts: 3.63 us -> 0.69 us  [the longest x1 2.94 us: body(): shard_rows = gather_wide(normed, chips).reshape(SPAN, D)]
  transfers between devices with their start and end apart: 9 -> 8, of which waited for: 5 -> 6; matrix products, arithmetic and copies ran while one was open for 14% -> 12% of each run, Pallas kernels for 0% -> 0%
where the time goes in v8:
time: 244 us; the launch traced here: 241 us
  blocking collectives  84.9 us (35%)
  waiting for transfers between devices  65.9 us (27%)
  local copies, waits for them, and re-layouts  32.1 us (13%)
  starting transfers between devices  24.6 us (10%)
  matrix products  22.2 us (9%)
  other arithmetic  8.6 us (4%)
    all_to_all x2, blocking collectives, gather_rows(): return lax.all_to_all(spread, axis, 0, 0, tiled=True)  42.3 us
    all_to_all x1, blocking collectives, body(): lax.all_to_all(ffn_part.astype(jnp.bfloat16), HALF, 0, 0, tiled=True)  30 us
    all_to_all x1, waiting for transfers between devices, body(): parts = lax.all_to_all(packed, WIDE, 0, 0, tiled=True)  23.9 us
    all_to_all x2, waiting for transfers between devices, gather_rows(): return lax.all_to_all(spread, axis, 0, 0, tiled=True)  21.7 us
    all_to_all x1, waiting for transfers between devices, send_rows(): return lax.all_to_all(blocks, axis, 0, 0, tiled=True)  15.6 us
    unnamed x22, local copies, waits for them, and re-layouts  12.8 us
    all_to_all x1, blocking collectives, send_rows(): return lax.all_to_all(blocks, axis, 0, 0, tiled=True)  12.6 us
    all_to_all x2, starting transfers between devices, gather_rows(): return lax.all_to_all(spread, axis, 0, 0, tiled=True)  11.3 us
  transfers between devices with their start and end apart: 8, of which 6 were waited for; matrix products, arithmetic and copies ran while one was open for 12% of the time, Pallas kernels for 0%

profile of v8, /device:TPU:1, one launch (start us, length us, event | category | flops | bytes accessed | tf_op | source)
XLA Modules:
  0.0 240.6 jit_solution(18095867306407863823)
XLA Ops:
  0.6 0.8 convert_element_type.87
  1.5 1.0 fusion.43
  2.5 0.9 fusion.45
  3.4 0.2 broadcast_in_dim.79
  3.7 22.1 %all_to_all.40 = bf16[16,4,7168]{2,1,0:T(4,128)(2,1)} all-to-all(bf16[16,4,7168]{2,1,0:T(4,128)(2,1)S(1)} %broadcast_in_dim.79), channel_id=1, replica_groups=mesh['req'=4,'chip'=16,'core'=2] {'chip'}, dimensions={0} | all-to-all | bytes 1835008 | tf_op jit(solution)/shard_map/all_to_all | solution.py:27
  25.8 1.8 collective-permute-start.1
  27.5 5.9 %copy.46 = bf16[1,256,7168]{1,2,0:T(8,128)(2,1)} copy(bf16[1,256,7168]{2,1,0:T(8,128)(2,1)} %param.28) | data formatting | bytes 7340032 | tf_op args[10]
  33.5 5.9 %copy.45 = bf16[1,256,7168]{1,2,0:T(8,128)(2,1)} copy(bf16[1,256,7168]{2,1,0:T(8,128)(2,1)} %param.27) | data formatting | bytes 7340032 | tf_op args[9]
  39.4 4.1 %pad.7 = bf16[32,256,228]{1,2,0:T(8,128)(2,1)} pad(bf16[32,256,224]{1,2,0:T(8,128)(2,1)} %bitcast.117, bf16[]{:T(256)} %constant.96.clone.1), padding=0_0x0_0x0_4 | pad | bytes 7405570 | tf_op jit(solution)/shard_map/jit(_pad)/pad | solution.py:96
  43.5 0.2 broadcast_in_dim.78
  43.7 1.9 constant_dynamic-update-slice_fusion.1
  45.5 1.8 constant_dynamic-update-slice_fusion
  47.4 0.9 fusion.47
  48.3 1.7 reshape.270
  49.9 12.6 %all_to_all.41 = f32[32,4,384]{2,1,0:T(4,128)} all-to-all(f32[32,4,384]{2,1,0:T(4,128)} %reshape.270), channel_id=1, replica_groups=mesh['req'=4,'chip'=16,'core'=2] {'chip','core'}, dimensions={0} | all-to-all | bytes 393216 | tf_op jit(solution)/shard_map/all_to_all | solution.py:49
  62.6 1.0 reduce_sum.88
  63.5 0.7 broadcast_in_dim.80
  64.2 3.8 %all-to-all-start.2 = ((bf16[32,4,384]{2,1,0:T(4,128)(2,1)}), bf16[32,4,384]{2,1,0:T(4,128)(2,1)S(1)}, u32[]{:S(2)}, u32[]{:S(2)}) async-start(bf16[32,4,384]{2,1,0:T(4,128)(2,1)} %broadcast_in_dim.80), calls=%async_computation.2 | async-start | bytes 196608 | tf_op jit(solution)/shard_map/all_to_all | solution.py:27
  68.0 7.1 %fusion.70 = f32[128,672]{0,1:T(8,128)} fusion(bf16[128,7168]{1,0:T(8,128)(2,1)S(1)} %bitcast.119, bf16[7168,672]{0,1:T(8,128)(2,1)} %bitcast.115), kind=kOutput, calls=%fused_computation.109 | convolution fusion | flops 1233125376 | bytes 11812864 | tf_op jit(solution)/shard_map/dot_general | solution.py:102
  75.1 0.5 all-to-all-done.2
  75.6 1.3 fusion.32
  76.9 0.7 slice_bitcast_fusion.2
  77.6 0.1 broadcast_in_dim.82
  77.8 20.2 %all_to_all.42 = bf16[16,128,224]{1,2,0:T(8,128)(2,1)S(1)} all-to-all(bf16[16,128,224]{1,2,0:T(8,128)(2,1)S(1)} %broadcast_in_dim.82), channel_id=1, replica_groups=mesh['req'=4,'chip'=16,'core'=2] {'chip'}, dimensions={0} | all-to-all | bytes 1835008 | tf_op jit(solution)/shard_map/all_to_all | solution.py:27
  97.9 2.3 collective-permute-start.2
  100.9 1.4 collective-permute-done.2
  102.4 12.2 %conditional.1 = (bf16[32,128,228]{1,2,0:T(8,128)(2,1)}) conditional(s32[]{:T(128)} %convert_element_type.85, () %tuple.22, (s32[]{:T(128)}, s32[256]{0:T(256)S(1)}, s32[]{:T(128)}, s32[1,256]{1,0:T(1,128)S(1)}, bf16[16,128,224]{1,2,0:T(8,128)(2,1)S(1)}, /*index=5*/s32[]{:T(128)}, bf16[16,128,224]{1,2,0:T(8,128)(2,1)S(1)}, s32[]{:T(128)}, ...), branch_computations={%region_2.3_spmd, %region_3.6_spmd} | conditional | flops 962577408 | bytes 51777172 | solution.py:146
  102.4 0.2 broadcast_in_dim.34
  102.6 0.7 copy-done.2
  103.3 0.1 bitcast_dynamic-update-slice_fusion.1
  103.4 0.2 copy.42
  103.6 1.3 bitcast_dynamic-update-slice_fusion
  104.9 0.7 compare_and_fusion
  105.6 3.6 %fusion = (f32[32,128]{1,0:T(8,128)S(1)}, f32[32,128,256]{2,1,0:T(8,128)S(1)}) fusion(pred[256]{0:T(512)(128)(4,1)S(1)} %compare_and_fusion, bf16[32,128,224]{1,2,0:T(8,128)(2,1)S(1)} %bitcast.120, bf16[32,256,224]{1,2,0:T(8,128)(2,1)} %get-tuple-element.113), kind=kOutput, calls=%fused_computation.2 | convolution fusion | flops 472903680 | bytes 9715968 | tf_op jit(solution)/shard_map/cond/branch_1_fun/hqd,hkd->hqk/dot_general | solution.py:123
  109.2 1.5 fusion.1
  110.8 0.5 copy-done.1
  111.3 2.7 %fusion.10 = bf16[32,128,228]{1,2,0:T(8,128)(2,1)} fusion(bf16[32,256,228]{1,2,0:T(8,128)(2,1)S(1)} %copy-done.1, f32[32,128,256]{2,1,0:T(8,128)S(1)} %get-tuple-element.134, f32[32,128]{1,0:T(8,128)S(1)} %reduce-precision_add_fusion, pred[256]{0:T(512)(128)(4,1)S(1)} %compare_and_fusion), kind=kOutput, calls=%fused_computation.11 | convolution fusion | flops 484327424 | bytes 9814272 | tf_op jit(solution)/shard_map/cond/branch_1_fun/hqk,hkd->hqd/dot_general | solution.py:132
  114.0 0.6 copy_dynamic-update-slice_fusion
  114.6 4.0 %all-to-all-start.4 = ((bf16[32,128,228]{1,2,0:T(8,128)(2,1)}), bf16[32,128,228]{1,2,0:T(8,128)(2,1)S(1)}, u32[]{:S(2)}, u32[]{:S(2)}) async-start(bf16[32,128,228]{1,2,0:T(8,128)(2,1)} %get-tuple-element.144), calls=%async_computation.4 | async-start | bytes 3801088 | tf_op jit(solution)/shard_map/all_to_all | solution.py:147
  119.3 1.1 fusion.69
  120.4 0.6 copy-done.5
  121.0 0.1 fusion.51
  121.1 23.9 %all-to-all-done.4 = bf16[32,128,228]{1,2,0:T(8,128)(2,1)S(1)} async-done(((bf16[32,128,228]{1,2,0:T(8,128)(2,1)}), bf16[32,128,228]{1,2,0:T(8,128)(2,1)S(1)}, u32[]{:S(2)}, u32[]{:S(2)}) %all-to-all-start.4) | async-done | bytes 1867808 | tf_op jit(solution)/shard_map/all_to_all | solution.py:147
  145.1 0.4 multiply_reduce_fusion
  145.5 0.3 copy-done.6
  145.8 0.2 fusion.36
  146.0 0.4 convolution_convert_fusion.1
  146.5 1.1 reshape.276
  147.6 4.3 %all-to-all-start.5 = ((bf16[32,4,3584]{2,1,0:T(4,128)(2,1)}), bf16[32,4,3584]{2,1,0:T(4,128)(2,1)S(1)}, u32[]{:S(2)}, u32[]{:S(2)}) async-start(bf16[32,4,3584]{2,1,0:T(4,128)(2,1)} %reshape.276), calls=%async_computation.5 | async-start | bytes 1835008 | tf_op jit(solution)/shard_map/all_to_all | solution.py:49
  152.0 15.6 %all-to-all-done.5 = bf16[32,4,3584]{2,1,0:T(4,128)(2,1)S(1)} async-done(((bf16[32,4,3584]{2,1,0:T(4,128)(2,1)}), bf16[32,4,3584]{2,1,0:T(4,128)(2,1)S(1)}, u32[]{:S(2)}, u32[]{:S(2)}) %all-to-all-start.5) | async-done | bytes 917536 | tf_op jit(solution)/shard_map/all_to_all | solution.py:49
  167.6 0.4 convert_reduce_fusion
  168.0 0.1 multiply_reduce_fusion.1
  168.1 0.1 multiply_convert_fusion
  168.2 1.7 broadcast_in_dim.85
  170.0 7.5 %all-to-all-start.6 = ((bf16[64,4,3584]{2,1,0:T(4,128)(2,1)}), bf16[64,4,3584]{2,1,0:T(4,128)(2,1)S(1)}, u32[]{:S(2)}, u32[]{:S(2)}) async-start(bf16[64,4,3584]{2,1,0:T(4,128)(2,1)} %broadcast_in_dim.85), calls=%async_computation.6 | async-start | bytes 3670016 | tf_op jit(solution)/shard_map/all_to_all | solution.py:27
  177.5 0.8 collective-permute-start
  178.2 0.1 collective-permute-start.3
  178.3 3.3 %collective-permute-done = bf16[2,112,3584]{2,1,0:T(8,128)(2,1)} collective-permute-done((bf16[2,112,3584]{2,1,0:T(8,128)(2,1)}, bf16[2,112,3584]{2,1,0:T(8,128)(2,1)}, u32[]{:S(2)}, u32[]{:S(2)}) %collective-permute-start) | collective-permute-done | bytes 1605664 | tf_op jit(solution)/shard_map/ppermute | solution.py:89
  181.7 21.2 %all-to-all-done.6 = bf16[64,4,3584]{2,1,0:T(4,128)(2,1)S(1)} async-done(((bf16[64,4,3584]{2,1,0:T(4,128)(2,1)}), bf16[64,4,3584]{2,1,0:T(4,128)(2,1)S(1)}, u32[]{:S(2)}, u32[]{:S(2)}) %all-to-all-start.6) | async-done | bytes 1835040 | tf_op jit(solution)/shard_map/all_to_all | solution.py:27
  202.9 3.1 %fusion.28 = f32[2,64,4,224]{3,1,2,0:T(8,128)S(1)} fusion(bf16[64,4,3584]{2,1,0:T(4,128)(2,1)S(1)} %all-to-all-done.6, bf16[2,112,3584]{2,1,0:T(8,128)(2,1)} %collective-permute-done, bf16[2,112,3584]{2,1,0:T(8,128)(2,1)} %param.25), kind=kOutput, calls=%fused_computation.45 | convolution fusion | flops 828506112 | bytes 5505024 | tf_op jit(solution)/shard_map/gtd,cfd->cgtf/dot_general | solution.py:191
  206.0 1.8 convolution_convert_fusion
  207.8 1.4 copy.51
  209.2 30.0 %all_to_all.43 = bf16[64,4,3584]{2,1,0:T(4,128)(2,1)S(1)} all-to-all(bf16[64,4,3584]{2,1,0:T(4,128)(2,1)S(1)} %copy.51), channel_id=1, replica_groups=mesh['req'=4,'chip'=16,'core'=2] {'req','chip'}, dimensions={0} | all-to-all | bytes 3670016 | tf_op jit(solution)/shard_map/all_to_all | solution.py:194
  239.2 1.4 reduce_sum.94
  (39 shorter events, 0.3 us)
Async XLA Ops:
  0.6 145.4 %copy-start = (bf16[224,3584]{1,0:T(8,128)(2,1)S(1)}, bf16[224,3584]{1,0:T(8,128)(2,1)}, u32[]{:S(2)}) copy-start(bf16[224,3584]{1,0:T(8,128)(2,1)} %param.23) | copy-start | bytes 4816900
  25.8 19.8 %collective-permute-start.1 = (bf16[16,4,7168]{2,1,0:T(4,128)(2,1)}, bf16[16,4,7168]{2,1,0:T(4,128)(2,1)}, u32[]{:S(2)}, u32[]{:S(2)}) collective-permute-start(bf16[16,4,7168]{2,1,0:T(4,128)(2,1)} %all_to_all.40), channel_id=1, source_target_pairs={{0,1},{1,0},{2,3},{3,2},{4,5},{5,4},{6,7},{7,6},{8,9},{9,8},{10,11... | collective-permute-start | bytes 2752520 | tf_op jit(solution)/shard_map/ppermute | solution.py:32
  43.7 3.7 %copy-start.4 = (bf16[224,384]{1,0:T(8,128)(2,1)S(1)}, bf16[224,384]{1,0:T(8,128)(2,1)}, u32[]{:S(2)}) copy-start(bf16[224,384]{1,0:T(8,128)(2,1)} %param.21) | copy-start | bytes 516100
  64.2 11.4 %all-to-all-start.2 = ((bf16[32,4,384]{2,1,0:T(4,128)(2,1)}), bf16[32,4,384]{2,1,0:T(4,128)(2,1)S(1)}, u32[]{:S(2)}, u32[]{:S(2)}) async-start(bf16[32,4,384]{2,1,0:T(4,128)(2,1)} %broadcast_in_dim.80), calls=%async_computation.2 | async-start | bytes 196608 | tf_op jit(solution)/shard_map/all_to_all | solution.py:27
  75.6 26.7 %copy-start.11 = (s32[1,256]{1,0:T(1,128)S(1)}, s32[1,256]{1,0:T(1,128)}, u32[]{:S(2)}) copy-start(s32[1,256]{1,0:T(1,128)} %param.30) | copy-start | bytes 3076
  76.9 0.7 copy-start.3
  97.9 4.4 %collective-permute-start.2 = (bf16[16,128,224]{1,2,0:T(8,128)(2,1)S(1)}, bf16[16,128,224]{1,2,0:T(8,128)(2,1)S(1)}, u32[]{:S(2)}, u32[]{:S(2)}) collective-permute-start(bf16[16,128,224]{1,2,0:T(8,128)(2,1)S(1)} %all_to_all.42), channel_id=1, source_target_pairs={{0,1},{1,0},{2,3},{3,2},{4,5},{5,4},{6,7},{7,6},{8,9},{9,8},{10,11... | collective-permute-start | bytes 2752520 | tf_op jit(solution)/shard_map/ppermute | solution.py:32
  102.4 0.9 copy-start.2
  109.2 2.1 copy-start.1
  114.6 30.3 %all-to-all-start.4 = ((bf16[32,128,228]{1,2,0:T(8,128)(2,1)}), bf16[32,128,228]{1,2,0:T(8,128)(2,1)S(1)}, u32[]{:S(2)}, u32[]{:S(2)}) async-start(bf16[32,128,228]{1,2,0:T(8,128)(2,1)} %get-tuple-element.144), calls=%async_computation.4 | async-start | bytes 3801088 | tf_op jit(solution)/shard_map/all_to_all | solution.py:147
  120.4 0.6 copy-start.5
  144.9 0.8 copy-start.6
  144.9 0.8 copy-start.7
  146.0 1.6 copy-start.8
  146.5 5.5 %copy-start.9 = (bf16[3584]{0:T(1024)(128)(2,1)S(1)}, bf16[3584]{0:T(1024)(128)(2,1)}, u32[]{:S(2)}) copy-start(bf16[3584]{0:T(1024)(128)(2,1)} %param.24) | copy-start | bytes 21508
  147.6 20.0 %all-to-all-start.5 = ((bf16[32,4,3584]{2,1,0:T(4,128)(2,1)}), bf16[32,4,3584]{2,1,0:T(4,128)(2,1)S(1)}, u32[]{:S(2)}, u32[]{:S(2)}) async-start(bf16[32,4,3584]{2,1,0:T(4,128)(2,1)} %reshape.276), calls=%async_computation.5 | async-start | bytes 1835008 | tf_op jit(solution)/shard_map/all_to_all | solution.py:49
  170.0 32.9 %all-to-all-start.6 = ((bf16[64,4,3584]{2,1,0:T(4,128)(2,1)}), bf16[64,4,3584]{2,1,0:T(4,128)(2,1)S(1)}, u32[]{:S(2)}, u32[]{:S(2)}) async-start(bf16[64,4,3584]{2,1,0:T(4,128)(2,1)} %broadcast_in_dim.85), calls=%async_computation.6 | async-start | bytes 3670016 | tf_op jit(solution)/shard_map/all_to_all | solution.py:27
  177.5 4.2 %collective-permute-start = (bf16[2,112,3584]{2,1,0:T(8,128)(2,1)}, bf16[2,112,3584]{2,1,0:T(8,128)(2,1)}, u32[]{:S(2)}, u32[]{:S(2)}) collective-permute-start(bf16[2,112,3584]{2,1,0:T(8,128)(2,1)} %param.25), channel_id=1, source_target_pairs={{0,1},{1,0},{2,3},{3,2},{4,5},{5,4},{6,7},{7,6},{8,9},{9,8},{10,11... | collective-permute-start | bytes 4816904 | tf_op jit(solution)/shard_map/ppermute | solution.py:89
  178.2 27.7 %collective-permute-start.3 = (bf16[112,3584]{1,0:T(8,128)(2,1)}, bf16[112,3584]{1,0:T(8,128)(2,1)}, u32[]{:S(2)}, u32[]{:S(2)}) collective-permute-start(bf16[112,3584]{1,0:T(8,128)(2,1)} %param.26), channel_id=1, source_target_pairs={{0,1},{1,0},{2,3},{3,2},{4,5},{5,4},{6,7},{7,6},{8,9},{9,8},{10,11... | collective-permute-start | bytes 2408456 | tf_op jit(solution)/shard_map/ppermute | solution.py:90
  202.9 3.1 %copy-start.10 = (bf16[112,3584]{1,0:T(8,128)(2,1)S(1)}, bf16[112,3584]{1,0:T(8,128)(2,1)}, u32[]{:S(2)}) copy-start(bf16[112,3584]{1,0:T(8,128)(2,1)} %param.26) | copy-start | bytes 2408452

commit v9 on v7

--- a/solution.py
+++ b/solution.py
@@ -180,11 +180,11 @@
     out_parts = send_rows(head_out.astype(jnp.bfloat16), WIDE, wide_size)
     attn_out = jnp.sum(out_parts.astype(jnp.float32), axis=0)
     normed_mid = rms_scale(attn_out, mlp_gain)
-    half_rows = gather_rows(normed_mid, HALF, half_size).reshape(half_size * own_rows, -1)
-    both = jnp.einsum("td,cfd->ctf", half_rows, chip_gate, preferred_element_type=jnp.float32)
+    half_rows = gather_rows(normed_mid, HALF, half_size)
+    both = jnp.einsum("gtd,cfd->cgtf", half_rows, chip_gate, preferred_element_type=jnp.float32)
     hidden = (jax.nn.silu(both[0]) * both[1]).astype(jnp.bfloat16)
-    ffn_part = jnp.dot(hidden, chip_down, preferred_element_type=jnp.float32)
-    ffn_parts = send_rows(ffn_part.astype(jnp.bfloat16), HALF, half_size)
+    ffn_part = jnp.einsum("gtf,fd->gtd", hidden, chip_down, preferred_element_type=jnp.float32)
+    ffn_parts = lax.all_to_all(ffn_part.astype(jnp.bfloat16), HALF, 0, 0, tiled=True)
     hidden_out = jnp.sum(ffn_parts.astype(jnp.float32), axis=0).astype(jnp.bfloat16)
     return (hidden_out, attention, new_keys, new_values)
 

time: 242 us -> 235 us (0.971)
  local copies, waits for them, and re-layouts: 39.7 us -> 36.5 us
    all_to_all x2 -> x1, blocking collectives: 45.8 us -> 15.7 us  [send_rows(): return lax.all_to_all(blocks, axis, 0, 0, tiled=True)]
    all_to_all x0 -> x1, blocking collectives: none -> 30 us  [body(): lax.all_to_all(ffn_part.astype(jnp.bfloat16), HALF, 0, 0, tiled=True)]
    all_to_all x3, waiting for transfers between devices: 25 us -> 21.7 us  [gather_rows(): return lax.all_to_all(spread, axis, 0, 0, tiled=True)]
    ppermute x1, waiting for transfers between devices: 0.01 us -> 3.33 us  [body(): lax.ppermute(gate_up, 'core', swap)]
    reshape x3 -> x2, local copies, waits for them, and re-layouts: 5.91 us -> 2.79 us  [send_rows(): values.reshape((count, values.shape[0] // count) + values.shape[1:])]
  transfers between devices with their start and end apart: 9 -> 9, of which waited for: 5 -> 6; matrix products, arithmetic and copies ran while one was open for 14% -> 13% of each run, Pallas kernels for 0% -> 0%
where the time goes in v9:
time: 235 us; the launch traced here: 232 us
  blocking collectives  65.9 us (28%)
  waiting for transfers between devices  65.8 us (28%)
  local copies, waits for them, and re-layouts  36.5 us (16%)
  starting transfers between devices  31.6 us (13%)
  matrix products  21.1 us (9%)
  other arithmetic  8.6 us (4%)
    all_to_all x1, blocking collectives, body(): lax.all_to_all(ffn_part.astype(jnp.bfloat16), HALF, 0, 0, tiled=True)  30 us
    all_to_all x1, waiting for transfers between devices, body(): parts = lax.all_to_all(packed, WIDE, 0, 0, tiled=True)  23.8 us
    all_to_all x3, waiting for transfers between devices, gather_rows(): return lax.all_to_all(spread, axis, 0, 0, tiled=True)  21.7 us
    all_to_all x1, blocking collectives, gather_rows(): return lax.all_to_all(spread, axis, 0, 0, tiled=True)  20.2 us
    all_to_all x3, starting transfers between devices, gather_rows(): return lax.all_to_all(spread, axis, 0, 0, tiled=True)  18.8 us
    all_to_all x1, blocking collectives, send_rows(): return lax.all_to_all(blocks, axis, 0, 0, tiled=True)  15.7 us
    all_to_all x1, waiting for transfers between devices, send_rows(): return lax.all_to_all(blocks, axis, 0, 0, tiled=True)  15.6 us
    unnamed x20, local copies, waits for them, and re-layouts  12.8 us
  transfers between devices with their start and end apart: 9, of which 6 were waited for; matrix products, arithmetic and copies ran while one was open for 13% of the time, Pallas kernels for 0%

profile of v9, /device:TPU:1, one launch (start us, length us, event | category | flops | bytes accessed | tf_op | source)
XLA Modules:
  0.0 231.7 jit_solution(6029824895000130881)
XLA Ops:
  0.6 0.8 convert_element_type.90
  1.5 1.0 fusion.43
  2.5 0.9 fusion.45
  3.4 1.1 broadcast_in_dim.79
  4.6 7.6 %all-to-all-start = ((bf16[16,4,7168]{2,1,0:T(4,128)(2,1)}), bf16[16,4,7168]{2,1,0:T(4,128)(2,1)S(1)}, u32[]{:S(2)}, u32[]{:S(2)}) async-start(bf16[16,4,7168]{2,1,0:T(4,128)(2,1)} %broadcast_in_dim.79), calls=%async_computation | async-start | bytes 1835008 | tf_op jit(solution)/shard_map/all_to_all | solution.py:27
  12.1 5.9 %copy.38 = bf16[1,256,7168]{1,2,0:T(8,128)(2,1)} copy(bf16[1,256,7168]{2,1,0:T(8,128)(2,1)} %param.28) | data formatting | bytes 7340032 | tf_op args[10]
  18.1 5.9 %copy.37 = bf16[1,256,7168]{1,2,0:T(8,128)(2,1)} copy(bf16[1,256,7168]{2,1,0:T(8,128)(2,1)} %param.27) | data formatting | bytes 7340032 | tf_op args[9]
  24.0 4.1 %pad.7 = bf16[32,256,228]{1,2,0:T(8,128)(2,1)} pad(bf16[32,256,224]{1,2,0:T(8,128)(2,1)} %bitcast.113, bf16[]{:T(256)} %constant.97.clone.1), padding=0_0x0_0x0_4 | pad | bytes 7405570 | tf_op jit(solution)/shard_map/jit(_pad)/pad | solution.py:89
  28.1 1.1 collective-permute-start.1
  29.2 2.0 broadcast_in_dim.78
  31.2 1.3 constant_dynamic-update-slice_fusion.3
  32.5 1.3 constant_dynamic-update-slice_fusion.2
  33.8 2.9 %reshape_reshape.3 = bf16[128,7168]{1,0:T(8,128)(2,1)S(1)} reshape(bf16[16,2,4,7168]{3,2,1,0:T(4,128)(2,1)} %constant_dynamic-update-slice_fusion.2) | data formatting | bytes 3670016 | tf_op jit(solution)/shard_map/reshape;reshape | solution.py:86
  36.7 1.8 fusion.47
  38.6 1.7 reshape.275
  40.2 15.7 %all_to_all.40 = f32[32,4,384]{2,1,0:T(4,128)} all-to-all(f32[32,4,384]{2,1,0:T(4,128)} %reshape.275), channel_id=1, replica_groups=mesh['req'=4,'chip'=16,'core'=2] {'chip','core'}, dimensions={0} | all-to-all | bytes 393216 | tf_op jit(solution)/shard_map/all_to_all | solution.py:42
  55.9 1.0 reduce_sum.89
  56.9 0.7 broadcast_in_dim.81
  57.5 3.8 %all-to-all-start.2 = ((bf16[32,4,384]{2,1,0:T(4,128)(2,1)}), bf16[32,4,384]{2,1,0:T(4,128)(2,1)S(1)}, u32[]{:S(2)}, u32[]{:S(2)}) async-start(bf16[32,4,384]{2,1,0:T(4,128)(2,1)} %broadcast_in_dim.81), calls=%async_computation.2 | async-start | bytes 196608 | tf_op jit(solution)/shard_map/all_to_all | solution.py:27
  61.3 7.1 %fusion.70 = f32[128,672]{0,1:T(8,128)} fusion(bf16[128,7168]{1,0:T(8,128)(2,1)S(1)} %reshape_reshape.3, bf16[7168,672]{0,1:T(8,128)(2,1)} %bitcast.111), kind=kOutput, calls=%fused_computation.109 | convolution fusion | flops 1233125376 | bytes 11812864 | tf_op jit(solution)/shard_map/dot_general | solution.py:95
  68.4 0.5 all-to-all-done.2
  69.0 1.3 fusion.32
  70.3 0.7 slice_bitcast_fusion.2
  71.0 0.1 broadcast_in_dim.83
  71.1 20.2 %all_to_all.41 = bf16[16,128,224]{1,2,0:T(8,128)(2,1)S(1)} all-to-all(bf16[16,128,224]{1,2,0:T(8,128)(2,1)S(1)} %broadcast_in_dim.83), channel_id=1, replica_groups=mesh['req'=4,'chip'=16,'core'=2] {'chip'}, dimensions={0} | all-to-all | bytes 1835008 | tf_op jit(solution)/shard_map/all_to_all | solution.py:27
  91.3 2.3 collective-permute-start.2
  94.2 1.4 collective-permute-done.2
  95.7 10.0 %conditional.1 = (bf16[32,128,228]{1,2,0:T(8,128)(2,1)}) conditional(s32[]{:T(128)} %convert_element_type.88, () %tuple.23, (s32[]{:T(128)}, s32[256]{0:T(256)S(1)}, s32[]{:T(128)}, s32[1,256]{1,0:T(1,128)S(1)}, bf16[16,1,128,224]{2,3,1,0:T(8,128)(2,1)S(1)}, /*index=5*/s32[]{:T(128)}, bf16[16,1,128,224]{2,3,1,0:T(8,128)(2,1)S(1)}, s32[]{:T(128)}, ...), branch_computations={%region_2.3_spmd, %region_3.6_spmd} | conditional | flops 962577408 | bytes 59117136 | solution.py:139
  95.7 0.7 compare_and_fusion
  96.4 0.3 broadcast_in_dim.34
  96.7 0.1 constant_dynamic-update-slice_fusion.1
  96.9 0.1 constant_dynamic-update-slice_fusion
  97.0 1.8 copy-done.1
  98.8 1.6 fusion
  100.4 1.5 fusion.1
  102.0 0.5 copy-done.2
  102.4 2.7 %fusion.10 = bf16[32,128,228]{1,2,0:T(8,128)(2,1)} fusion(bf16[32,256,228]{1,2,0:T(8,128)(2,1)S(1)} %copy-done.2, f32[32,128,256]{2,1,0:T(8,128)S(1)} %get-tuple-element.131, f32[32,128]{1,0:T(8,128)S(1)} %reduce-precision_add_fusion, pred[256]{0:T(512)(128)(4,1)S(1)} %compare_and_fusion), kind=kOutput, calls=%fused_computation.11 | convolution fusion | flops 484327424 | bytes 9814272 | tf_op jit(solution)/shard_map/cond/branch_1_fun/hqk,hkd->hqd/dot_general | solution.py:125
  105.1 0.6 copy_dynamic-update-slice_fusion
  105.7 4.1 %all-to-all-start.4 = ((bf16[32,128,228]{1,2,0:T(8,128)(2,1)}), bf16[32,128,228]{1,2,0:T(8,128)(2,1)S(1)}, u32[]{:S(2)}, u32[]{:S(2)}) async-start(bf16[32,128,228]{1,2,0:T(8,128)(2,1)} %get-tuple-element.141), calls=%async_computation.4 | async-start | bytes 3801088 | tf_op jit(solution)/shard_map/all_to_all | solution.py:140
  110.5 1.1 fusion.69
  111.6 0.6 copy-done.4
  112.2 0.1 fusion.51
  112.3 23.8 %all-to-all-done.4 = bf16[32,128,228]{1,2,0:T(8,128)(2,1)S(1)} async-done(((bf16[32,128,228]{1,2,0:T(8,128)(2,1)}), bf16[32,128,228]{1,2,0:T(8,128)(2,1)S(1)}, u32[]{:S(2)}, u32[]{:S(2)}) %all-to-all-start.4) | async-done | bytes 1867808 | tf_op jit(solution)/shard_map/all_to_all | solution.py:140
  136.3 0.4 multiply_reduce_fusion
  136.7 0.3 copy-done.5
  137.0 0.2 fusion.36
  137.2 0.4 convolution_convert_fusion.1
  137.6 1.1 reshape.281
  138.8 4.3 %all-to-all-start.5 = ((bf16[32,4,3584]{2,1,0:T(4,128)(2,1)}), bf16[32,4,3584]{2,1,0:T(4,128)(2,1)S(1)}, u32[]{:S(2)}, u32[]{:S(2)}) async-start(bf16[32,4,3584]{2,1,0:T(4,128)(2,1)} %reshape.281), calls=%async_computation.5 | async-start | bytes 1835008 | tf_op jit(solution)/shard_map/all_to_all | solution.py:42
  143.2 15.6 %all-to-all-done.5 = bf16[32,4,3584]{2,1,0:T(4,128)(2,1)S(1)} async-done(((bf16[32,4,3584]{2,1,0:T(4,128)(2,1)}), bf16[32,4,3584]{2,1,0:T(4,128)(2,1)S(1)}, u32[]{:S(2)}, u32[]{:S(2)}) %all-to-all-start.5) | async-done | bytes 917536 | tf_op jit(solution)/shard_map/all_to_all | solution.py:42
  158.8 0.4 convert_reduce_fusion
  159.2 0.1 multiply_reduce_fusion.1
  159.3 0.1 multiply_convert_fusion
  159.4 1.7 broadcast_in_dim.87
  161.1 7.5 %all-to-all-start.6 = ((bf16[64,4,3584]{2,1,0:T(4,128)(2,1)}), bf16[64,4,3584]{2,1,0:T(4,128)(2,1)S(1)}, u32[]{:S(2)}, u32[]{:S(2)}) async-start(bf16[64,4,3584]{2,1,0:T(4,128)(2,1)} %broadcast_in_dim.87), calls=%async_computation.6 | async-start | bytes 3670016 | tf_op jit(solution)/shard_map/all_to_all | solution.py:27
  168.6 0.8 collective-permute-start
  169.4 0.1 collective-permute-start.3
  169.5 3.3 %collective-permute-done = bf16[2,112,3584]{2,1,0:T(8,128)(2,1)} collective-permute-done((bf16[2,112,3584]{2,1,0:T(8,128)(2,1)}, bf16[2,112,3584]{2,1,0:T(8,128)(2,1)}, u32[]{:S(2)}, u32[]{:S(2)}) %collective-permute-start) | collective-permute-done | bytes 1605664 | tf_op jit(solution)/shard_map/ppermute | solution.py:82
  172.8 21.2 %all-to-all-done.6 = bf16[64,4,3584]{2,1,0:T(4,128)(2,1)S(1)} async-done(((bf16[64,4,3584]{2,1,0:T(4,128)(2,1)}), bf16[64,4,3584]{2,1,0:T(4,128)(2,1)S(1)}, u32[]{:S(2)}, u32[]{:S(2)}) %all-to-all-start.6) | async-done | bytes 1835040 | tf_op jit(solution)/shard_map/all_to_all | solution.py:27
  194.0 3.1 %fusion.28 = f32[2,64,4,224]{3,1,2,0:T(8,128)S(1)} fusion(bf16[64,4,3584]{2,1,0:T(4,128)(2,1)S(1)} %all-to-all-done.6, bf16[2,112,3584]{2,1,0:T(8,128)(2,1)} %collective-permute-done, bf16[2,112,3584]{2,1,0:T(8,128)(2,1)} %param.25), kind=kOutput, calls=%fused_computation.45 | convolution fusion | flops 828506112 | bytes 5505024 | tf_op jit(solution)/shard_map/gtd,cfd->cgtf/dot_general | solution.py:184
  197.1 1.8 convolution_convert_fusion
  198.9 1.4 copy.43
  200.4 30.0 %all_to_all.42 = bf16[64,4,3584]{2,1,0:T(4,128)(2,1)S(1)} all-to-all(bf16[64,4,3584]{2,1,0:T(4,128)(2,1)S(1)} %copy.43), channel_id=1, replica_groups=mesh['req'=4,'chip'=16,'core'=2] {'req','chip'}, dimensions={0} | all-to-all | bytes 3670016 | tf_op jit(solution)/shard_map/all_to_all | solution.py:187
  230.4 1.4 reduce_sum.95
  (38 shorter events, 0.3 us)
Async XLA Ops:
  0.6 136.6 %copy-start = (bf16[224,3584]{1,0:T(8,128)(2,1)S(1)}, bf16[224,3584]{1,0:T(8,128)(2,1)}, u32[]{:S(2)}) copy-start(bf16[224,3584]{1,0:T(8,128)(2,1)} %param.23) | copy-start | bytes 4816900
  4.6 23.6 %all-to-all-start = ((bf16[16,4,7168]{2,1,0:T(4,128)(2,1)}), bf16[16,4,7168]{2,1,0:T(4,128)(2,1)S(1)}, u32[]{:S(2)}, u32[]{:S(2)}) async-start(bf16[16,4,7168]{2,1,0:T(4,128)(2,1)} %broadcast_in_dim.79), calls=%async_computation | async-start | bytes 1835008 | tf_op jit(solution)/shard_map/all_to_all | solution.py:27
  28.1 4.4 %collective-permute-start.1 = (bf16[16,1,4,7168]{3,2,1,0:T(4,128)(2,1)S(1)}, bf16[16,1,4,7168]{3,2,1,0:T(4,128)(2,1)S(1)}, u32[]{:S(2)}, u32[]{:S(2)}) collective-permute-start(bf16[16,1,4,7168]{3,2,1,0:T(4,128)(2,1)S(1)} %bitcast.117), channel_id=1, source_target_pairs={{0,1},{1,0},{2,3},{3,2},{4,5},{5,4},{6,7},{7,6},{8,9},{9,8},{10,11... | collective-permute-start | bytes 2752520 | tf_op jit(solution)/shard_map/ppermute | solution.py:32
  57.5 11.4 %all-to-all-start.2 = ((bf16[32,4,384]{2,1,0:T(4,128)(2,1)}), bf16[32,4,384]{2,1,0:T(4,128)(2,1)S(1)}, u32[]{:S(2)}, u32[]{:S(2)}) async-start(bf16[32,4,384]{2,1,0:T(4,128)(2,1)} %broadcast_in_dim.81), calls=%async_computation.2 | async-start | bytes 196608 | tf_op jit(solution)/shard_map/all_to_all | solution.py:27
  69.0 26.7 %copy-start.10 = (s32[1,256]{1,0:T(1,128)S(1)}, s32[1,256]{1,0:T(1,128)}, u32[]{:S(2)}) copy-start(s32[1,256]{1,0:T(1,128)} %param.30) | copy-start | bytes 3076
  70.3 0.7 copy-start.3
  91.3 4.4 %collective-permute-start.2 = (bf16[16,1,128,224]{2,3,1,0:T(8,128)(2,1)S(1)}, bf16[16,1,128,224]{2,3,1,0:T(8,128)(2,1)S(1)}, u32[]{:S(2)}, u32[]{:S(2)}) collective-permute-start(bf16[16,1,128,224]{2,3,1,0:T(8,128)(2,1)S(1)} %bitcast.115), channel_id=1, source_target_pairs={{0,1},{1,0},{2,3},{3,2},{4,5},{5,4},{6,7},{7,6},{8,9},{9,8},{10,11... | collective-permute-start | bytes 2752520 | tf_op jit(solution)/shard_map/ppermute | solution.py:32
  96.7 2.0 copy-start.1
  100.4 2.1 copy-start.2
  105.7 30.4 %all-to-all-start.4 = ((bf16[32,128,228]{1,2,0:T(8,128)(2,1)}), bf16[32,128,228]{1,2,0:T(8,128)(2,1)S(1)}, u32[]{:S(2)}, u32[]{:S(2)}) async-start(bf16[32,128,228]{1,2,0:T(8,128)(2,1)} %get-tuple-element.141), calls=%async_computation.4 | async-start | bytes 3801088 | tf_op jit(solution)/shard_map/all_to_all | solution.py:140
  111.6 0.6 copy-start.4
  136.1 0.8 copy-start.5
  136.1 0.8 copy-start.6
  137.2 1.6 copy-start.7
  137.6 5.5 %copy-start.8 = (bf16[3584]{0:T(1024)(128)(2,1)S(1)}, bf16[3584]{0:T(1024)(128)(2,1)}, u32[]{:S(2)}) copy-start(bf16[3584]{0:T(1024)(128)(2,1)} %param.24) | copy-start | bytes 21508
  138.8 20.0 %all-to-all-start.5 = ((bf16[32,4,3584]{2,1,0:T(4,128)(2,1)}), bf16[32,4,3584]{2,1,0:T(4,128)(2,1)S(1)}, u32[]{:S(2)}, u32[]{:S(2)}) async-start(bf16[32,4,3584]{2,1,0:T(4,128)(2,1)} %reshape.281), calls=%async_computation.5 | async-start | bytes 1835008 | tf_op jit(solution)/shard_map/all_to_all | solution.py:42
  161.1 32.9 %all-to-all-start.6 = ((bf16[64,4,3584]{2,1,0:T(4,128)(2,1)}), bf16[64,4,3584]{2,1,0:T(4,128)(2,1)S(1)}, u32[]{:S(2)}, u32[]{:S(2)}) async-start(bf16[64,4,3584]{2,1,0:T(4,128)(2,1)} %broadcast_in_dim.87), calls=%async_computation.6 | async-start | bytes 3670016 | tf_op jit(solution)/shard_map/all_to_all | solution.py:27
  168.6 4.2 %collective-permute-start = (bf16[2,112,3584]{2,1,0:T(8,128)(2,1)}, bf16[2,112,3584]{2,1,0:T(8,128)(2,1)}, u32[]{:S(2)}, u32[]{:S(2)}) collective-permute-start(bf16[2,112,3584]{2,1,0:T(8,128)(2,1)} %param.25), channel_id=1, source_target_pairs={{0,1},{1,0},{2,3},{3,2},{4,5},{5,4},{6,7},{7,6},{8,9},{9,8},{10,11... | collective-permute-start | bytes 4816904 | tf_op jit(solution)/shard_map/ppermute | solution.py:82
  169.4 27.8 %collective-permute-start.3 = (bf16[112,3584]{1,0:T(8,128)(2,1)}, bf16[112,3584]{1,0:T(8,128)(2,1)}, u32[]{:S(2)}, u32[]{:S(2)}) collective-permute-start(bf16[112,3584]{1,0:T(8,128)(2,1)} %param.26), channel_id=1, source_target_pairs={{0,1},{1,0},{2,3},{3,2},{4,5},{5,4},{6,7},{7,6},{8,9},{9,8},{10,11... | collective-permute-start | bytes 2408456 | tf_op jit(solution)/shard_map/ppermute | solution.py:83
  194.0 3.1 %copy-start.9 = (bf16[112,3584]{1,0:T(8,128)(2,1)S(1)}, bf16[112,3584]{1,0:T(8,128)(2,1)}, u32[]{:S(2)}) copy-start(bf16[112,3584]{1,0:T(8,128)(2,1)} %param.26) | copy-start | bytes 2408452

commit v10 on v9

--- a/solution.py
+++ b/solution.py
@@ -50,6 +50,26 @@
 
 def join_pair(high, low):
     return high.astype(jnp.float32) + low.astype(jnp.float32)
+
+
+def join_partials(first, second):
+    first_max = join_pair(first[..., HD], first[..., HD + 1])
+    second_max = join_pair(second[..., HD], second[..., HD + 1])
+    highest = jnp.maximum(first_max, second_max)
+    first_factor = jnp.exp(first_max - highest)
+    second_factor = jnp.exp(second_max - highest)
+    numerator = (
+        first[..., :HD].astype(jnp.float32) * first_factor[..., None]
+        + second[..., :HD].astype(jnp.float32) * second_factor[..., None]
+    )
+    totals = join_pair(first[..., HD + 2], first[..., HD + 3]) * first_factor + join_pair(
+        second[..., HD + 2], second[..., HD + 3]
+    ) * second_factor
+    high, low = split_pair(highest)
+    shift = jnp.exp(highest - (high + low))
+    total_high, total_low = split_pair(totals * shift)
+    stats = jnp.stack([high, low, total_high, total_low], axis=-1).astype(jnp.bfloat16)
+    return jnp.concatenate([(numerator * shift[..., None]).astype(jnp.bfloat16), stats], axis=-1)
 
 
 def body(
@@ -137,7 +157,13 @@
         return jnp.concatenate([jnp.zeros((HEADS, SPAN, HD), jnp.bfloat16), stats], axis=-1)
 
     packed = lax.cond(block_start < length, cache_block, skipped, 0)
-    parts = lax.all_to_all(packed, WIDE, 0, 0, tiled=True)
+    core = lax.axis_index("core")
+    by_side = packed.reshape(HEADS // 2, 2, SPAN, HD + 4)
+    kept = lax.dynamic_index_in_dim(by_side, core, axis=1, keepdims=False)
+    given = lax.dynamic_index_in_dim(by_side, 1 - core, axis=1, keepdims=False)
+    taken = lax.ppermute(given, "core", [(0, 1), (1, 0)])
+    joined = join_partials(kept, taken)
+    parts = lax.all_to_all(joined, "chip", 0, 0, tiled=True)
     part_num = parts[..., :HD].astype(jnp.float32)
     part_max = join_pair(parts[..., HD], parts[..., HD + 1])
     part_sum = join_pair(parts[..., HD + 2], parts[..., HD + 3])

time: 235 us -> 232 us (0.987)
  starting transfers between devices: 31.6 us -> 41.2 us
  waiting for transfers between devices: 65.8 us -> 57.3 us
  matrix products: 21.1 us -> 16.8 us
    all_to_all x1, waiting for transfers between devices: 23.8 us -> 13.2 us  [body(): parts = lax.all_to_all(joined, 'chip', 0, 0, tiled=True)]
    ppermute x0 -> x1, starting transfers between devices: none -> 8.38 us  [body(): taken = lax.ppermute(given, 'core', [(0, 1), (1, 0)])]
    dot_general x2 -> x0, matrix products: 4.23 us -> none  [the longest x1 2.67 us: cache_block(): jnp.einsum('hqk,hkd->hqd', weights.astype(jnp.bfloat16), value_heads, pre...]
    unnamed x20 -> x16, local copies, waits for them, and re-layouts: 12.8 us -> 12.5 us
  transfers between devices with their start and end apart: 9 -> 10, of which waited for: 6 -> 7; matrix products, arithmetic and copies ran while one was open for 13% -> 13% of each run, Pallas kernels for 0% -> 0%
where the time goes in v10:
time: 232 us; the launch traced here: 228 us
  blocking collectives  65.9 us (28%)
  waiting for transfers between devices  57.3 us (25%)
  starting transfers between devices  41.2 us (18%)
  local copies, waits for them, and re-layouts  38.1 us (16%)
  matrix products  16.8 us (7%)
  other arithmetic  6.62 us (3%)
    all_to_all x1, blocking collectives, body(): lax.all_to_all(ffn_part.astype(jnp.bfloat16), HALF, 0, 0, tiled=True)  30 us
    all_to_all x3, waiting for transfers between devices, gather_rows(): return lax.all_to_all(spread, axis, 0, 0, tiled=True)  21.7 us
    all_to_all x1, blocking collectives, gather_rows(): return lax.all_to_all(spread, axis, 0, 0, tiled=True)  20.2 us
    all_to_all x3, starting transfers between devices, gather_rows(): return lax.all_to_all(spread, axis, 0, 0, tiled=True)  18.9 us
    all_to_all x1, blocking collectives, send_rows(): return lax.all_to_all(blocks, axis, 0, 0, tiled=True)  15.7 us
    all_to_all x1, waiting for transfers between devices, send_rows(): return lax.all_to_all(blocks, axis, 0, 0, tiled=True)  15.6 us
    all_to_all x1, waiting for transfers between devices, body(): parts = lax.all_to_all(joined, 'chip', 0, 0, tiled=True)  13.2 us
    unnamed x16, local copies, waits for them, and re-layouts  12.5 us
  transfers between devices with their start and end apart: 10, of which 7 were waited for; matrix products, arithmetic and copies ran while one was open for 13% of the time, Pallas kernels for 0%

profile of v10, /device:TPU:1, one launch (start us, length us, event | category | flops | bytes accessed | tf_op | source)
XLA Modules:
  0.0 228.1 jit_solution(16318191172737886983)
XLA Ops:
  0.6 0.0 copy-start
  0.6 0.8 convert_element_type.160
  1.5 1.0 fusion.44
  2.5 0.9 fusion.46
  3.4 1.1 broadcast_in_dim.82
  4.6 7.6 %all-to-all-start = ((bf16[16,4,7168]{2,1,0:T(4,128)(2,1)}), bf16[16,4,7168]{2,1,0:T(4,128)(2,1)S(1)}, u32[]{:S(2)}, u32[]{:S(2)}) async-start(bf16[16,4,7168]{2,1,0:T(4,128)(2,1)} %broadcast_in_dim.82), calls=%async_computation | async-start | bytes 1835008 | tf_op jit(solution)/shard_map/all_to_all | solution.py:27
  12.1 5.9 %copy.47 = bf16[1,256,7168]{1,2,0:T(8,128)(2,1)} copy(bf16[1,256,7168]{2,1,0:T(8,128)(2,1)} %param.28) | data formatting | bytes 7340032 | tf_op args[10]
  18.1 5.9 %copy.46 = bf16[1,256,7168]{1,2,0:T(8,128)(2,1)} copy(bf16[1,256,7168]{2,1,0:T(8,128)(2,1)} %param.27) | data formatting | bytes 7340032 | tf_op args[9]
  24.0 4.1 %pad.7 = bf16[32,256,228]{1,2,0:T(8,128)(2,1)} pad(bf16[32,256,224]{1,2,0:T(8,128)(2,1)} %bitcast.126, bf16[]{:T(256)} %constant.103.clone.1), padding=0_0x0_0x0_4 | pad | bytes 7405570 | tf_op jit(solution)/shard_map/jit(_pad)/pad | solution.py:109
  28.1 0.0 all-to-all-done
  28.1 1.1 collective-permute-start.1
  29.2 2.0 broadcast_in_dim.81
  31.2 1.3 constant_dynamic-update-slice_fusion.7
  32.5 1.3 constant_dynamic-update-slice_fusion.6
  33.8 2.9 %reshape_reshape.3 = bf16[128,7168]{1,0:T(8,128)(2,1)S(1)} reshape(bf16[16,2,4,7168]{3,2,1,0:T(4,128)(2,1)} %constant_dynamic-update-slice_fusion.6) | data formatting | bytes 3670016 | tf_op jit(solution)/shard_map/reshape;reshape | solution.py:106
  36.7 1.8 fusion.48
  38.6 1.7 reshape.278
  40.2 15.7 %all_to_all.40 = f32[32,4,384]{2,1,0:T(4,128)} all-to-all(f32[32,4,384]{2,1,0:T(4,128)} %reshape.278), channel_id=1, replica_groups=mesh['req'=4,'chip'=16,'core'=2] {'chip','core'}, dimensions={0} | all-to-all | bytes 393216 | tf_op jit(solution)/shard_map/all_to_all | solution.py:42
  55.9 1.0 reduce_sum.89
  56.9 0.7 broadcast_in_dim.84
  57.5 3.8 %all-to-all-start.2 = ((bf16[32,4,384]{2,1,0:T(4,128)(2,1)}), bf16[32,4,384]{2,1,0:T(4,128)(2,1)S(1)}, u32[]{:S(2)}, u32[]{:S(2)}) async-start(bf16[32,4,384]{2,1,0:T(4,128)(2,1)} %broadcast_in_dim.84), calls=%async_computation.2 | async-start | bytes 196608 | tf_op jit(solution)/shard_map/all_to_all | solution.py:27
  61.3 7.1 %fusion.82 = f32[128,672]{0,1:T(8,128)} fusion(bf16[128,7168]{1,0:T(8,128)(2,1)S(1)} %reshape_reshape.3, bf16[7168,672]{0,1:T(8,128)(2,1)} %bitcast.124), kind=kOutput, calls=%fused_computation.139 | convolution fusion | flops 1233125376 | bytes 11812864 | tf_op jit(solution)/shard_map/dot_general | solution.py:115
  68.4 0.5 all-to-all-done.2
  69.0 1.3 fusion.32
  70.3 0.6 copy-done.3
  70.9 0.1 broadcast_in_dim.86
  71.0 20.2 %all_to_all.41 = bf16[16,128,224]{1,2,0:T(8,128)(2,1)S(1)} all-to-all(bf16[16,128,224]{1,2,0:T(8,128)(2,1)S(1)} %broadcast_in_dim.86), channel_id=1, replica_groups=mesh['req'=4,'chip'=16,'core'=2] {'chip'}, dimensions={0} | all-to-all | bytes 1835008 | tf_op jit(solution)/shard_map/all_to_all | solution.py:27
  91.2 2.3 %collective-permute-start.2 = (bf16[16,1,128,224]{2,3,1,0:T(8,128)(2,1)S(1)}, bf16[16,1,128,224]{2,3,1,0:T(8,128)(2,1)S(1)}, u32[]{:S(2)}, u32[]{:S(2)}) collective-permute-start(bf16[16,1,128,224]{2,3,1,0:T(8,128)(2,1)S(1)} %bitcast.131), channel_id=1, source_target_pairs={{0,1},{1,0},{2,3},{3,2},{4,5},{5,4},{6,7},{7,6},{8,9},{9,8},{10,11... | collective-permute-start | bytes 2752520 | tf_op jit(solution)/shard_map/ppermute | solution.py:32
  94.2 1.4 collective-permute-done.2
  95.7 3.0 %conditional.1 = (bf16[16,2,128,228]{2,3,1,0:T(8,128)(2,1)}) conditional(s32[]{:T(128)} %convert_element_type.158, () %tuple.23, (s32[]{:T(128)}, s32[256]{0:T(256)S(1)}, s32[]{:T(128)}, s32[1,256]{1,0:T(1,128)}, bf16[16,1,128,224]{2,3,1,0:T(8,128)(2,1)S(1)}, /*index=5*/s32[]{:T(128)}, bf16[16,1,128,224]{2,3,1,0:T(8,128)(2,1)S(1)}, s32[]{:T(128)}, ...), branch_computations={%region_2.3_spmd, %region_3.6_spmd} | conditional | flops 962577408 | bytes 59117136 | solution.py:159
  95.7 3.0 %copy.92 = bf16[16,2,128,228]{2,3,1,0:T(8,128)(2,1)} copy(bf16[16,2,128,228]{2,3,1,0:T(8,128)(2,1)} %constant.127) | data formatting | bytes 3735552 | tf_op jit(solution)/shard_map/cond
  98.6 1.6 constant_dynamic-slice_fusion.1
  100.2 0.1 copy.76
  100.4 8.4 %collective-permute-start.3 = (bf16[16,128,228]{1,0,2:T(8,128)(2,1)S(1)}, bf16[16,128,228]{1,0,2:T(8,128)(2,1)S(1)}, u32[]{:S(2)}, u32[]{:S(2)}) collective-permute-start(bf16[16,128,228]{1,0,2:T(8,128)(2,1)S(1)} %bitcast.135), channel_id=1, source_target_pairs={{0,1},{1,0},{2,3},{3,2},{4,5},{5,4},{6,7},{7,6},{8,9},{9,8},{10,11... | collective-permute-start | bytes 2801672 | tf_op jit(solution)/shard_map/ppermute | solution.py:164
  108.7 0.1 copy.77
  108.9 2.0 collective-permute-done.3
  110.9 0.4 fusion.39
  111.4 1.2 copy.51
  112.6 3.6 %all-to-all-start.4 = ((bf16[16,128,228]{1,2,0:T(8,128)(2,1)}), bf16[16,128,228]{1,2,0:T(8,128)(2,1)S(1)}, u32[]{:S(2)}, u32[]{:S(2)}) async-start(bf16[16,128,228]{1,2,0:T(8,128)(2,1)} %copy.51), calls=%async_computation.4 | async-start | bytes 1900544 | tf_op jit(solution)/shard_map/all_to_all | solution.py:166
  116.9 1.0 fusion.81
  117.9 0.1 fusion.52
  118.0 13.2 %all-to-all-done.4 = bf16[16,128,228]{1,2,0:T(8,128)(2,1)S(1)} async-done(((bf16[16,128,228]{1,2,0:T(8,128)(2,1)}), bf16[16,128,228]{1,2,0:T(8,128)(2,1)S(1)}, u32[]{:S(2)}, u32[]{:S(2)}) %all-to-all-start.4) | async-done | bytes 933920 | tf_op jit(solution)/shard_map/all_to_all | solution.py:166
  131.4 0.2 multiply_reduce_fusion
  131.6 0.2 fusion.36
  131.8 0.0 copy-start.6
  131.9 0.4 convolution_convert_fusion.1
  132.3 0.0 copy-start.7
  132.3 1.1 reshape.285
  133.4 6.1 %all-to-all-start.5 = ((bf16[32,4,3584]{2,1,0:T(4,128)(2,1)}), bf16[32,4,3584]{2,1,0:T(4,128)(2,1)S(1)}, u32[]{:S(2)}, u32[]{:S(2)}) async-start(bf16[32,4,3584]{2,1,0:T(4,128)(2,1)} %reshape.285), calls=%async_computation.5 | async-start | bytes 1835008 | tf_op jit(solution)/shard_map/all_to_all | solution.py:42
  139.5 15.6 %all-to-all-done.5 = bf16[32,4,3584]{2,1,0:T(4,128)(2,1)S(1)} async-done(((bf16[32,4,3584]{2,1,0:T(4,128)(2,1)}), bf16[32,4,3584]{2,1,0:T(4,128)(2,1)S(1)}, u32[]{:S(2)}, u32[]{:S(2)}) %all-to-all-start.5) | async-done | bytes 917536 | tf_op jit(solution)/shard_map/all_to_all | solution.py:42
  155.1 0.4 convert_reduce_fusion
  155.5 0.1 multiply_reduce_fusion.1
  155.7 0.1 multiply_convert_fusion.1
  155.8 1.7 broadcast_in_dim.90
  157.5 7.5 %all-to-all-start.6 = ((bf16[64,4,3584]{2,1,0:T(4,128)(2,1)}), bf16[64,4,3584]{2,1,0:T(4,128)(2,1)S(1)}, u32[]{:S(2)}, u32[]{:S(2)}) async-start(bf16[64,4,3584]{2,1,0:T(4,128)(2,1)} %broadcast_in_dim.90), calls=%async_computation.6 | async-start | bytes 3670016 | tf_op jit(solution)/shard_map/all_to_all | solution.py:27
  165.0 0.8 collective-permute-start
  165.8 0.1 collective-permute-start.4
  165.9 3.3 %collective-permute-done = bf16[2,112,3584]{2,1,0:T(8,128)(2,1)} collective-permute-done((bf16[2,112,3584]{2,1,0:T(8,128)(2,1)}, bf16[2,112,3584]{2,1,0:T(8,128)(2,1)}, u32[]{:S(2)}, u32[]{:S(2)}) %collective-permute-start) | collective-permute-done | bytes 1605664 | tf_op jit(solution)/shard_map/ppermute | solution.py:102
  169.2 21.2 %all-to-all-done.6 = bf16[64,4,3584]{2,1,0:T(4,128)(2,1)S(1)} async-done(((bf16[64,4,3584]{2,1,0:T(4,128)(2,1)}), bf16[64,4,3584]{2,1,0:T(4,128)(2,1)S(1)}, u32[]{:S(2)}, u32[]{:S(2)}) %all-to-all-start.6) | async-done | bytes 1835040 | tf_op jit(solution)/shard_map/all_to_all | solution.py:27
  190.4 3.1 %fusion.28 = f32[2,64,4,224]{3,1,2,0:T(8,128)S(1)} fusion(bf16[64,4,3584]{2,1,0:T(4,128)(2,1)S(1)} %all-to-all-done.6, bf16[2,112,3584]{2,1,0:T(8,128)(2,1)} %collective-permute-done, bf16[2,112,3584]{2,1,0:T(8,128)(2,1)} %param.25), kind=kOutput, calls=%fused_computation.46 | convolution fusion | flops 828506112 | bytes 5505024 | tf_op jit(solution)/shard_map/gtd,cfd->cgtf/dot_general | solution.py:210
  193.5 1.8 convolution_convert_fusion
  195.3 1.4 copy.55
  196.8 30.0 %all_to_all.42 = bf16[64,4,3584]{2,1,0:T(4,128)(2,1)S(1)} all-to-all(bf16[64,4,3584]{2,1,0:T(4,128)(2,1)S(1)} %copy.55), channel_id=1, replica_groups=mesh['req'=4,'chip'=16,'core'=2] {'req','chip'}, dimensions={0} | all-to-all | bytes 3670016 | tf_op jit(solution)/shard_map/all_to_all | solution.py:213
  226.8 1.4 reduce_sum.95
  (32 shorter events, 0.3 us)
Async XLA Ops:
  0.6 131.2 %copy-start = (bf16[224,3584]{1,0:T(8,128)(2,1)S(1)}, bf16[224,3584]{1,0:T(8,128)(2,1)}, u32[]{:S(2)}) copy-start(bf16[224,3584]{1,0:T(8,128)(2,1)} %param.23) | copy-start | bytes 4816900
  4.6 23.6 %all-to-all-start = ((bf16[16,4,7168]{2,1,0:T(4,128)(2,1)}), bf16[16,4,7168]{2,1,0:T(4,128)(2,1)S(1)}, u32[]{:S(2)}, u32[]{:S(2)}) async-start(bf16[16,4,7168]{2,1,0:T(4,128)(2,1)} %broadcast_in_dim.82), calls=%async_computation | async-start | bytes 1835008 | tf_op jit(solution)/shard_map/all_to_all | solution.py:27
  28.1 4.4 %collective-permute-start.1 = (bf16[16,1,4,7168]{3,2,1,0:T(4,128)(2,1)S(1)}, bf16[16,1,4,7168]{3,2,1,0:T(4,128)(2,1)S(1)}, u32[]{:S(2)}, u32[]{:S(2)}) collective-permute-start(bf16[16,1,4,7168]{3,2,1,0:T(4,128)(2,1)S(1)} %bitcast.133), channel_id=1, source_target_pairs={{0,1},{1,0},{2,3},{3,2},{4,5},{5,4},{6,7},{7,6},{8,9},{9,8},{10,11... | collective-permute-start | bytes 2752520 | tf_op jit(solution)/shard_map/ppermute | solution.py:32
  57.5 11.4 %all-to-all-start.2 = ((bf16[32,4,384]{2,1,0:T(4,128)(2,1)}), bf16[32,4,384]{2,1,0:T(4,128)(2,1)S(1)}, u32[]{:S(2)}, u32[]{:S(2)}) async-start(bf16[32,4,384]{2,1,0:T(4,128)(2,1)} %broadcast_in_dim.84), calls=%async_computation.2 | async-start | bytes 196608 | tf_op jit(solution)/shard_map/all_to_all | solution.py:27
  70.2 0.7 copy-start.3
  70.9 46.0 %copy-start.5 = (bf16[128,224]{0,1:T(8,128)(2,1)}, bf16[128,224]{0,1:T(8,128)(2,1)S(1)}, u32[]{:S(2)}) copy-start(bf16[128,224]{0,1:T(8,128)(2,1)S(1)} %get-tuple-element.144) | copy-start | bytes 172036
  70.9 60.7 %copy-start.4 = (bf16[128,224]{0,1:T(8,128)(2,1)}, bf16[128,224]{0,1:T(8,128)(2,1)S(1)}, u32[]{:S(2)}) copy-start(bf16[128,224]{0,1:T(8,128)(2,1)S(1)} %get-tuple-element.143) | copy-start | bytes 172036
  91.2 4.4 %collective-permute-start.2 = (bf16[16,1,128,224]{2,3,1,0:T(8,128)(2,1)S(1)}, bf16[16,1,128,224]{2,3,1,0:T(8,128)(2,1)S(1)}, u32[]{:S(2)}, u32[]{:S(2)}) collective-permute-start(bf16[16,1,128,224]{2,3,1,0:T(8,128)(2,1)S(1)} %bitcast.131), channel_id=1, source_target_pairs={{0,1},{1,0},{2,3},{3,2},{4,5},{5,4},{6,7},{7,6},{8,9},{9,8},{10,11... | collective-permute-start | bytes 2752520 | tf_op jit(solution)/shard_map/ppermute | solution.py:32
  100.4 10.5 %collective-permute-start.3 = (bf16[16,128,228]{1,0,2:T(8,128)(2,1)S(1)}, bf16[16,128,228]{1,0,2:T(8,128)(2,1)S(1)}, u32[]{:S(2)}, u32[]{:S(2)}) collective-permute-start(bf16[16,128,228]{1,0,2:T(8,128)(2,1)S(1)} %bitcast.135), channel_id=1, source_target_pairs={{0,1},{1,0},{2,3},{3,2},{4,5},{5,4},{6,7},{7,6},{8,9},{9,8},{10,11... | collective-permute-start | bytes 2801672 | tf_op jit(solution)/shard_map/ppermute | solution.py:164
  112.6 18.7 %all-to-all-start.4 = ((bf16[16,128,228]{1,2,0:T(8,128)(2,1)}), bf16[16,128,228]{1,2,0:T(8,128)(2,1)S(1)}, u32[]{:S(2)}, u32[]{:S(2)}) async-start(bf16[16,128,228]{1,2,0:T(8,128)(2,1)} %copy.51), calls=%async_computation.4 | async-start | bytes 1900544 | tf_op jit(solution)/shard_map/all_to_all | solution.py:166
  131.8 1.6 copy-start.6
  132.3 7.2 %copy-start.7 = (bf16[3584]{0:T(1024)(128)(2,1)S(1)}, bf16[3584]{0:T(1024)(128)(2,1)}, u32[]{:S(2)}) copy-start(bf16[3584]{0:T(1024)(128)(2,1)} %param.24) | copy-start | bytes 21508
  133.4 21.7 %all-to-all-start.5 = ((bf16[32,4,3584]{2,1,0:T(4,128)(2,1)}), bf16[32,4,3584]{2,1,0:T(4,128)(2,1)S(1)}, u32[]{:S(2)}, u32[]{:S(2)}) async-start(bf16[32,4,3584]{2,1,0:T(4,128)(2,1)} %reshape.285), calls=%async_computation.5 | async-start | bytes 1835008 | tf_op jit(solution)/shard_map/all_to_all | solution.py:42
  157.5 32.9 %all-to-all-start.6 = ((bf16[64,4,3584]{2,1,0:T(4,128)(2,1)}), bf16[64,4,3584]{2,1,0:T(4,128)(2,1)S(1)}, u32[]{:S(2)}, u32[]{:S(2)}) async-start(bf16[64,4,3584]{2,1,0:T(4,128)(2,1)} %broadcast_in_dim.90), calls=%async_computation.6 | async-start | bytes 3670016 | tf_op jit(solution)/shard_map/all_to_all | solution.py:27
  165.0 4.2 %collective-permute-start = (bf16[2,112,3584]{2,1,0:T(8,128)(2,1)}, bf16[2,112,3584]{2,1,0:T(8,128)(2,1)}, u32[]{:S(2)}, u32[]{:S(2)}) collective-permute-start(bf16[2,112,3584]{2,1,0:T(8,128)(2,1)} %param.25), channel_id=1, source_target_pairs={{0,1},{1,0},{2,3},{3,2},{4,5},{5,4},{6,7},{7,6},{8,9},{9,8},{10,11... | collective-permute-start | bytes 4816904 | tf_op jit(solution)/shard_map/ppermute | solution.py:102
  165.8 27.7 %collective-permute-start.4 = (bf16[112,3584]{1,0:T(8,128)(2,1)}, bf16[112,3584]{1,0:T(8,128)(2,1)}, u32[]{:S(2)}, u32[]{:S(2)}) collective-permute-start(bf16[112,3584]{1,0:T(8,128)(2,1)} %param.26), channel_id=1, source_target_pairs={{0,1},{1,0},{2,3},{3,2},{4,5},{5,4},{6,7},{7,6},{8,9},{9,8},{10,11... | collective-permute-start | bytes 2408456 | tf_op jit(solution)/shard_map/ppermute | solution.py:103
  190.4 3.1 %copy-start.8 = (bf16[112,3584]{1,0:T(8,128)(2,1)S(1)}, bf16[112,3584]{1,0:T(8,128)(2,1)}, u32[]{:S(2)}) copy-start(bf16[112,3584]{1,0:T(8,128)(2,1)} %param.26) | copy-start | bytes 2408452

commit v11 on v10

--- a/solution.py
+++ b/solution.py
@@ -116,7 +116,12 @@
     )
     sliced = lax.dynamic_slice_in_dim(shard_rows, feature_start, local_width, 1)
     partial_low = jnp.dot(sliced, adapter_down, preferred_element_type=jnp.float32)
-    low_parts = send_rows(partial_low, WIDE, wide_size)
+    low_core = lax.axis_index("core")
+    low_sides = partial_low.reshape(chips, 2, own_rows, 3 * RANK)
+    low_kept = lax.dynamic_index_in_dim(low_sides, low_core, axis=1, keepdims=False)
+    low_given = lax.dynamic_index_in_dim(low_sides, 1 - low_core, axis=1, keepdims=False)
+    low_chip = low_kept + lax.ppermute(low_given, "core", [(0, 1), (1, 0)])
+    low_parts = lax.all_to_all(low_chip, "chip", 0, 0, tiled=True)
     own_low = jnp.sum(low_parts, axis=0).astype(jnp.bfloat16)
     lowrank = gather_rows(own_low, WIDE, wide_size).reshape(SPAN, 3, RANK)
     adapted = jnp.einsum("tcr,crd->tcd", lowrank, adapter_up, preferred_element_type=jnp.float32)

time: 232 us -> 233 us (level)
  starting transfers between devices: 41.2 us -> 34.8 us
  matrix products: 16.8 us -> 21 us
  other arithmetic: 6.62 us -> 9.52 us
  blocking collectives: 65.9 us -> 63.4 us
    ppermute x1, starting transfers between devices: 8.38 us -> 0.63 us  [body(): taken = lax.ppermute(given, 'core', [(0, 1), (1, 0)])]
    dot_general x0 -> x2, matrix products: none -> 4.24 us  [the longest x1 2.68 us: cache_block(): jnp.einsum('hqk,hkd->hqd', weights.astype(jnp.bfloat16), value_heads, pre...]
    all_to_all x1, blocking collectives: 15.7 us -> 13.2 us  [body(): low_parts = lax.all_to_all(low_chip, 'chip', 0, 0, tiled=True)]
  transfers between devices with their start and end apart: 10 -> 11, of which waited for: 7 -> 8; matrix products, arithmetic and copies ran while one was open for 13% -> 13% of each run, Pallas kernels for 0% -> 0%
where the time goes in v11:
time: 233 us; the launch traced here: 229 us
  blocking collectives  63.4 us (27%)
  waiting for transfers between devices  58.5 us (25%)
  local copies, waits for them, and re-layouts  39.5 us (17%)
  starting transfers between devices  34.8 us (15%)
  matrix products  21 us (9%)
  other arithmetic  9.52 us (4%)
    all_to_all x1, blocking collectives, body(): lax.all_to_all(ffn_part.astype(jnp.bfloat16), HALF, 0, 0, tiled=True)  30 us
    all_to_all x3, waiting for transfers between devices, gather_rows(): return lax.all_to_all(spread, axis, 0, 0, tiled=True)  21.6 us
    all_to_all x3, starting transfers between devices, gather_rows(): return lax.all_to_all(spread, axis, 0, 0, tiled=True)  20.2 us
    all_to_all x1, blocking collectives, gather_rows(): return lax.all_to_all(spread, axis, 0, 0, tiled=True)  20.2 us
    all_to_all x1, waiting for transfers between devices, send_rows(): return lax.all_to_all(blocks, axis, 0, 0, tiled=True)  15.6 us
    all_to_all x1, waiting for transfers between devices, body(): parts = lax.all_to_all(joined, 'chip', 0, 0, tiled=True)  13.3 us
    all_to_all x1, blocking collectives, body(): low_parts = lax.all_to_all(low_chip, 'chip', 0, 0, tiled=True)  13.2 us
    unnamed x16, local copies, waits for them, and re-layouts  12.5 us
  transfers between devices with their start and end apart: 11, of which 8 were waited for; matrix products, arithmetic and copies ran while one was open for 13% of the time, Pallas kernels for 0%

profile of v11, /device:TPU:1, one launch (start us, length us, event | category | flops | bytes accessed | tf_op | source)
XLA Modules:
  0.0 229.2 jit_solution(8427870959119383703)
XLA Ops:
  0.6 0.8 convert_element_type.160
  1.5 1.0 fusion.44
  2.5 0.9 fusion.46
  3.4 1.1 broadcast_in_dim.82
  4.6 7.6 %all-to-all-start = ((bf16[16,4,7168]{2,1,0:T(4,128)(2,1)}), bf16[16,4,7168]{2,1,0:T(4,128)(2,1)S(1)}, u32[]{:S(2)}, u32[]{:S(2)}) async-start(bf16[16,4,7168]{2,1,0:T(4,128)(2,1)} %broadcast_in_dim.82), calls=%async_computation | async-start | bytes 1835008 | tf_op jit(solution)/shard_map/all_to_all | solution.py:27
  12.1 5.9 %copy.47 = bf16[1,256,7168]{1,2,0:T(8,128)(2,1)} copy(bf16[1,256,7168]{2,1,0:T(8,128)(2,1)} %param.28) | data formatting | bytes 7340032 | tf_op args[10]
  18.1 5.9 %copy.46 = bf16[1,256,7168]{1,2,0:T(8,128)(2,1)} copy(bf16[1,256,7168]{2,1,0:T(8,128)(2,1)} %param.27) | data formatting | bytes 7340032 | tf_op args[9]
  24.0 4.1 %pad.7 = bf16[32,256,228]{1,2,0:T(8,128)(2,1)} pad(bf16[32,256,224]{1,2,0:T(8,128)(2,1)} %bitcast.130, bf16[]{:T(256)} %constant.109.clone.1), padding=0_0x0_0x0_4 | pad | bytes 7405570 | tf_op jit(solution)/shard_map/jit(_pad)/pad | solution.py:109
  28.1 1.1 collective-permute-start.1
  29.2 2.0 broadcast_in_dim.81
  31.2 1.3 constant_dynamic-update-slice_fusion.7
  32.5 1.3 constant_dynamic-update-slice_fusion.6
  33.8 2.9 %reshape_reshape.3 = bf16[128,7168]{1,0:T(8,128)(2,1)S(1)} reshape(bf16[16,2,4,7168]{3,2,1,0:T(4,128)(2,1)} %constant_dynamic-update-slice_fusion.6) | data formatting | bytes 3670016 | tf_op jit(solution)/shard_map/reshape;reshape | solution.py:106
  36.7 1.8 fusion.48
  38.6 1.7 reshape.278
  40.2 0.9 dynamic-slice_bitcast_fusion
  41.2 1.3 collective-permute-done.2
  42.5 0.9 bitcast_add_fusion
  43.4 13.2 %all_to_all.40 = f32[16,4,384]{2,1,0:T(4,128)S(1)} all-to-all(f32[16,4,384]{2,1,0:T(4,128)S(1)} %bitcast_add_fusion), channel_id=1, replica_groups=mesh['req'=4,'chip'=16,'core'=2] {'chip'}, dimensions={0} | all-to-all | bytes 196608 | tf_op jit(solution)/shard_map/all_to_all | solution.py:124
  56.7 0.7 broadcast_in_dim.84
  57.3 5.1 %all-to-all-start.2 = ((bf16[32,4,384]{2,1,0:T(4,128)(2,1)}), bf16[32,4,384]{2,1,0:T(4,128)(2,1)S(1)}, u32[]{:S(2)}, u32[]{:S(2)}) async-start(bf16[32,4,384]{2,1,0:T(4,128)(2,1)} %broadcast_in_dim.84), calls=%async_computation.2 | async-start | bytes 196608 | tf_op jit(solution)/shard_map/all_to_all | solution.py:27
  62.5 7.1 %fusion.82 = f32[128,672]{0,1:T(8,128)} fusion(bf16[128,7168]{1,0:T(8,128)(2,1)S(1)} %reshape_reshape.3, bf16[7168,672]{0,1:T(8,128)(2,1)} %bitcast.128), kind=kOutput, calls=%fused_computation.141 | convolution fusion | flops 1233125376 | bytes 11812864 | tf_op jit(solution)/shard_map/dot_general | solution.py:115
  69.6 0.4 all-to-all-done.2
  70.1 1.3 fusion.32
  71.4 0.6 copy-done.3
  72.1 20.2 %all_to_all.41 = bf16[16,128,224]{1,2,0:T(8,128)(2,1)S(1)} all-to-all(bf16[16,128,224]{1,2,0:T(8,128)(2,1)S(1)} %broadcast_in_dim.86), channel_id=1, replica_groups=mesh['req'=4,'chip'=16,'core'=2] {'chip'}, dimensions={0} | all-to-all | bytes 1835008 | tf_op jit(solution)/shard_map/all_to_all | solution.py:27
  92.3 2.3 %collective-permute-start.3 = (bf16[16,1,128,224]{2,3,1,0:T(8,128)(2,1)S(1)}, bf16[16,1,128,224]{2,3,1,0:T(8,128)(2,1)S(1)}, u32[]{:S(2)}, u32[]{:S(2)}) collective-permute-start(bf16[16,1,128,224]{2,3,1,0:T(8,128)(2,1)S(1)} %bitcast.135), channel_id=1, source_target_pairs={{0,1},{1,0},{2,3},{3,2},{4,5},{5,4},{6,7},{7,6},{8,9},{9,8},{10,11... | collective-permute-start | bytes 2752520 | tf_op jit(solution)/shard_map/ppermute | solution.py:32
  95.3 1.4 collective-permute-done.3
  96.8 10.7 %conditional.1 = (bf16[16,2,128,228]{2,3,1,0:T(8,128)(2,1)}) conditional(s32[]{:T(128)} %convert_element_type.158, () %tuple.23, (s32[]{:T(128)}, s32[256]{0:T(256)S(1)}, s32[]{:T(128)}, s32[1,256]{1,0:T(1,128)}, bf16[16,1,128,224]{2,3,1,0:T(8,128)(2,1)S(1)}, /*index=5*/s32[]{:T(128)}, bf16[16,1,128,224]{2,3,1,0:T(8,128)(2,1)S(1)}, s32[]{:T(128)}, ...), branch_computations={%region_2.3_spmd, %region_3.6_spmd} | conditional | flops 962577408 | bytes 59117136 | solution.py:164
  96.8 0.7 compare_reduce_fusion
  97.5 0.7 compare_and_fusion
  98.1 0.3 broadcast_in_dim.34
  98.7 1.8 copy-done.1
  100.5 1.6 fusion
  102.1 1.5 fusion.1
  103.7 0.5 copy-done.2
  104.2 2.7 %fusion.10 = bf16[32,128,228]{1,2,0:T(8,128)(2,1)} fusion(bf16[32,256,228]{1,2,0:T(8,128)(2,1)S(1)} %copy-done.2, f32[32,128,256]{2,1,0:T(8,128)S(1)} %get-tuple-element.136, f32[32,128]{1,0:T(8,128)S(1)} %reduce-precision_add_fusion, pred[256]{0:T(512)(128)(4,1)S(1)} %compare_and_fusion), kind=kOutput, calls=%fused_computation.11 | convolution fusion | flops 484327424 | bytes 9814272 | tf_op jit(solution)/shard_map/cond/branch_1_fun/hqk,hkd->hqd/dot_general | solution.py:150
  106.8 0.6 copy_dynamic-update-slice_fusion
  107.5 1.6 constant_dynamic-slice_fusion.1
  109.2 0.6 collective-permute-start.4
  110.0 2.0 collective-permute-done.4
  112.0 0.4 fusion.39
  112.5 1.2 copy.51
  113.7 3.6 %all-to-all-start.4 = ((bf16[16,128,228]{1,2,0:T(8,128)(2,1)}), bf16[16,128,228]{1,2,0:T(8,128)(2,1)S(1)}, u32[]{:S(2)}, u32[]{:S(2)}) async-start(bf16[16,128,228]{1,2,0:T(8,128)(2,1)} %copy.51), calls=%async_computation.4 | async-start | bytes 1900544 | tf_op jit(solution)/shard_map/all_to_all | solution.py:171
  118.0 1.0 fusion.81
  119.1 13.3 %all-to-all-done.4 = bf16[16,128,228]{1,2,0:T(8,128)(2,1)S(1)} async-done(((bf16[16,128,228]{1,2,0:T(8,128)(2,1)}), bf16[16,128,228]{1,2,0:T(8,128)(2,1)S(1)}, u32[]{:S(2)}, u32[]{:S(2)}) %all-to-all-start.4) | async-done | bytes 933920 | tf_op jit(solution)/shard_map/all_to_all | solution.py:171
  132.5 0.2 multiply_reduce_fusion
  132.7 0.2 fusion.36
  133.0 0.4 convolution_convert_fusion.1
  133.4 1.1 reshape.285
  134.6 6.0 %all-to-all-start.5 = ((bf16[32,4,3584]{2,1,0:T(4,128)(2,1)}), bf16[32,4,3584]{2,1,0:T(4,128)(2,1)S(1)}, u32[]{:S(2)}, u32[]{:S(2)}) async-start(bf16[32,4,3584]{2,1,0:T(4,128)(2,1)} %reshape.285), calls=%async_computation.5 | async-start | bytes 1835008 | tf_op jit(solution)/shard_map/all_to_all | solution.py:42
  140.6 15.6 %all-to-all-done.5 = bf16[32,4,3584]{2,1,0:T(4,128)(2,1)S(1)} async-done(((bf16[32,4,3584]{2,1,0:T(4,128)(2,1)}), bf16[32,4,3584]{2,1,0:T(4,128)(2,1)S(1)}, u32[]{:S(2)}, u32[]{:S(2)}) %all-to-all-start.5) | async-done | bytes 917536 | tf_op jit(solution)/shard_map/all_to_all | solution.py:42
  156.2 0.4 convert_reduce_fusion
  156.6 0.1 multiply_reduce_fusion.1
  156.8 1.7 broadcast_in_dim.90
  158.6 7.5 %all-to-all-start.6 = ((bf16[64,4,3584]{2,1,0:T(4,128)(2,1)}), bf16[64,4,3584]{2,1,0:T(4,128)(2,1)S(1)}, u32[]{:S(2)}, u32[]{:S(2)}) async-start(bf16[64,4,3584]{2,1,0:T(4,128)(2,1)} %broadcast_in_dim.90), calls=%async_computation.6 | async-start | bytes 3670016 | tf_op jit(solution)/shard_map/all_to_all | solution.py:27
  166.1 0.8 collective-permute-start
  166.9 3.3 %collective-permute-done = bf16[2,112,3584]{2,1,0:T(8,128)(2,1)} collective-permute-done((bf16[2,112,3584]{2,1,0:T(8,128)(2,1)}, bf16[2,112,3584]{2,1,0:T(8,128)(2,1)}, u32[]{:S(2)}, u32[]{:S(2)}) %collective-permute-start) | collective-permute-done | bytes 1605664 | tf_op jit(solution)/shard_map/ppermute | solution.py:102
  170.3 21.2 %all-to-all-done.6 = bf16[64,4,3584]{2,1,0:T(4,128)(2,1)S(1)} async-done(((bf16[64,4,3584]{2,1,0:T(4,128)(2,1)}), bf16[64,4,3584]{2,1,0:T(4,128)(2,1)S(1)}, u32[]{:S(2)}, u32[]{:S(2)}) %all-to-all-start.6) | async-done | bytes 1835040 | tf_op jit(solution)/shard_map/all_to_all | solution.py:27
  191.5 3.1 %fusion.28 = f32[2,64,4,224]{3,1,2,0:T(8,128)S(1)} fusion(bf16[64,4,3584]{2,1,0:T(4,128)(2,1)S(1)} %all-to-all-done.6, bf16[2,112,3584]{2,1,0:T(8,128)(2,1)} %collective-permute-done, bf16[2,112,3584]{2,1,0:T(8,128)(2,1)} %param.25), kind=kOutput, calls=%fused_computation.46 | convolution fusion | flops 828506112 | bytes 5505024 | tf_op jit(solution)/shard_map/gtd,cfd->cgtf/dot_general | solution.py:215
  194.6 1.8 convolution_convert_fusion
  196.4 1.4 copy.55
  197.8 30.0 %all_to_all.42 = bf16[64,4,3584]{2,1,0:T(4,128)(2,1)S(1)} all-to-all(bf16[64,4,3584]{2,1,0:T(4,128)(2,1)S(1)} %copy.55), channel_id=1, replica_groups=mesh['req'=4,'chip'=16,'core'=2] {'req','chip'}, dimensions={0} | all-to-all | bytes 3670016 | tf_op jit(solution)/shard_map/all_to_all | solution.py:218
  227.9 1.4 reduce_sum.95
  (51 shorter events, 1.4 us)
Async XLA Ops:
  0.6 132.3 %copy-start = (bf16[224,3584]{1,0:T(8,128)(2,1)S(1)}, bf16[224,3584]{1,0:T(8,128)(2,1)}, u32[]{:S(2)}) copy-start(bf16[224,3584]{1,0:T(8,128)(2,1)} %param.23) | copy-start | bytes 4816900
  4.6 23.6 %all-to-all-start = ((bf16[16,4,7168]{2,1,0:T(4,128)(2,1)}), bf16[16,4,7168]{2,1,0:T(4,128)(2,1)S(1)}, u32[]{:S(2)}, u32[]{:S(2)}) async-start(bf16[16,4,7168]{2,1,0:T(4,128)(2,1)} %broadcast_in_dim.82), calls=%async_computation | async-start | bytes 1835008 | tf_op jit(solution)/shard_map/all_to_all | solution.py:27
  28.1 4.4 %collective-permute-start.1 = (bf16[16,1,4,7168]{3,2,1,0:T(4,128)(2,1)S(1)}, bf16[16,1,4,7168]{3,2,1,0:T(4,128)(2,1)S(1)}, u32[]{:S(2)}, u32[]{:S(2)}) collective-permute-start(bf16[16,1,4,7168]{3,2,1,0:T(4,128)(2,1)S(1)} %bitcast.137), channel_id=1, source_target_pairs={{0,1},{1,0},{2,3},{3,2},{4,5},{5,4},{6,7},{7,6},{8,9},{9,8},{10,11... | collective-permute-start | bytes 2752520 | tf_op jit(solution)/shard_map/ppermute | solution.py:32
  41.1 1.4 collective-permute-start.2
  57.3 12.7 %all-to-all-start.2 = ((bf16[32,4,384]{2,1,0:T(4,128)(2,1)}), bf16[32,4,384]{2,1,0:T(4,128)(2,1)S(1)}, u32[]{:S(2)}, u32[]{:S(2)}) async-start(bf16[32,4,384]{2,1,0:T(4,128)(2,1)} %broadcast_in_dim.84), calls=%async_computation.2 | async-start | bytes 196608 | tf_op jit(solution)/shard_map/all_to_all | solution.py:27
  71.3 0.7 copy-start.3
  72.0 46.0 %copy-start.5 = (bf16[128,224]{0,1:T(8,128)(2,1)}, bf16[128,224]{0,1:T(8,128)(2,1)S(1)}, u32[]{:S(2)}) copy-start(bf16[128,224]{0,1:T(8,128)(2,1)S(1)} %get-tuple-element.144) | copy-start | bytes 172036
  72.0 60.7 %copy-start.4 = (bf16[128,224]{0,1:T(8,128)(2,1)}, bf16[128,224]{0,1:T(8,128)(2,1)S(1)}, u32[]{:S(2)}) copy-start(bf16[128,224]{0,1:T(8,128)(2,1)S(1)} %get-tuple-element.143) | copy-start | bytes 172036
  92.3 4.4 %collective-permute-start.3 = (bf16[16,1,128,224]{2,3,1,0:T(8,128)(2,1)S(1)}, bf16[16,1,128,224]{2,3,1,0:T(8,128)(2,1)S(1)}, u32[]{:S(2)}, u32[]{:S(2)}) collective-permute-start(bf16[16,1,128,224]{2,3,1,0:T(8,128)(2,1)S(1)} %bitcast.135), channel_id=1, source_target_pairs={{0,1},{1,0},{2,3},{3,2},{4,5},{5,4},{6,7},{7,6},{8,9},{9,8},{10,11... | collective-permute-start | bytes 2752520 | tf_op jit(solution)/shard_map/ppermute | solution.py:32
  98.5 2.0 copy-start.1
  102.1 2.1 copy-start.2
  109.2 2.8 %collective-permute-start.4 = (bf16[16,128,228]{1,0,2:T(8,128)(2,1)S(1)}, bf16[16,128,228]{1,0,2:T(8,128)(2,1)S(1)}, u32[]{:S(2)}, u32[]{:S(2)}) collective-permute-start(bf16[16,128,228]{1,0,2:T(8,128)(2,1)S(1)} %bitcast.139), channel_id=1, source_target_pairs={{0,1},{1,0},{2,3},{3,2},{4,5},{5,4},{6,7},{7,6},{8,9},{9,8},{10,11... | collective-permute-start | bytes 2801672 | tf_op jit(solution)/shard_map/ppermute | solution.py:169
  113.7 18.7 %all-to-all-start.4 = ((bf16[16,128,228]{1,2,0:T(8,128)(2,1)}), bf16[16,128,228]{1,2,0:T(8,128)(2,1)S(1)}, u32[]{:S(2)}, u32[]{:S(2)}) async-start(bf16[16,128,228]{1,2,0:T(8,128)(2,1)} %copy.51), calls=%async_computation.4 | async-start | bytes 1900544 | tf_op jit(solution)/shard_map/all_to_all | solution.py:171
  133.0 1.6 copy-start.6
  133.4 7.2 %copy-start.7 = (bf16[3584]{0:T(1024)(128)(2,1)S(1)}, bf16[3584]{0:T(1024)(128)(2,1)}, u32[]{:S(2)}) copy-start(bf16[3584]{0:T(1024)(128)(2,1)} %param.24) | copy-start | bytes 21508
  134.6 21.7 %all-to-all-start.5 = ((bf16[32,4,3584]{2,1,0:T(4,128)(2,1)}), bf16[32,4,3584]{2,1,0:T(4,128)(2,1)S(1)}, u32[]{:S(2)}, u32[]{:S(2)}) async-start(bf16[32,4,3584]{2,1,0:T(4,128)(2,1)} %reshape.285), calls=%async_computation.5 | async-start | bytes 1835008 | tf_op jit(solution)/shard_map/all_to_all | solution.py:42
  158.6 32.9 %all-to-all-start.6 = ((bf16[64,4,3584]{2,1,0:T(4,128)(2,1)}), bf16[64,4,3584]{2,1,0:T(4,128)(2,1)S(1)}, u32[]{:S(2)}, u32[]{:S(2)}) async-start(bf16[64,4,3584]{2,1,0:T(4,128)(2,1)} %broadcast_in_dim.90), calls=%async_computation.6 | async-start | bytes 3670016 | tf_op jit(solution)/shard_map/all_to_all | solution.py:27
  166.1 4.2 %collective-permute-start = (bf16[2,112,3584]{2,1,0:T(8,128)(2,1)}, bf16[2,112,3584]{2,1,0:T(8,128)(2,1)}, u32[]{:S(2)}, u32[]{:S(2)}) collective-permute-start(bf16[2,112,3584]{2,1,0:T(8,128)(2,1)} %param.25), channel_id=1, source_target_pairs={{0,1},{1,0},{2,3},{3,2},{4,5},{5,4},{6,7},{7,6},{8,9},{9,8},{10,11... | collective-permute-start | bytes 4816904 | tf_op jit(solution)/shard_map/ppermute | solution.py:102
  166.9 27.7 %collective-permute-start.5 = (bf16[112,3584]{1,0:T(8,128)(2,1)}, bf16[112,3584]{1,0:T(8,128)(2,1)}, u32[]{:S(2)}, u32[]{:S(2)}) collective-permute-start(bf16[112,3584]{1,0:T(8,128)(2,1)} %param.26), channel_id=1, source_target_pairs={{0,1},{1,0},{2,3},{3,2},{4,5},{5,4},{6,7},{7,6},{8,9},{9,8},{10,11... | collective-permute-start | bytes 2408456 | tf_op jit(solution)/shard_map/ppermute | solution.py:103
  191.5 3.1 %copy-start.8 = (bf16[112,3584]{1,0:T(8,128)(2,1)S(1)}, bf16[112,3584]{1,0:T(8,128)(2,1)}, u32[]{:S(2)}) copy-start(bf16[112,3584]{1,0:T(8,128)(2,1)} %param.26) | copy-start | bytes 2408452

commit v12 on v10

--- a/solution.py
+++ b/solution.py
@@ -203,7 +203,12 @@
     attention = (numerator / totals[:, None]).astype(jnp.bfloat16)
 
     head_out = jnp.dot(attention, out_weight, preferred_element_type=jnp.float32)
-    out_parts = send_rows(head_out.astype(jnp.bfloat16), WIDE, wide_size)
+    out_sides = head_out.reshape(chips, 2, own_rows, -1)
+    out_kept = lax.dynamic_index_in_dim(out_sides, core, axis=1, keepdims=False)
+    out_given = lax.dynamic_index_in_dim(out_sides, 1 - core, axis=1, keepdims=False)
+    out_taken = lax.ppermute(out_given.astype(jnp.bfloat16), "core", [(0, 1), (1, 0)])
+    out_chip = (out_kept + out_taken.astype(jnp.float32)).astype(jnp.bfloat16)
+    out_parts = lax.all_to_all(out_chip, "chip", 0, 0, tiled=True)
     attn_out = jnp.sum(out_parts.astype(jnp.float32), axis=0)
     normed_mid = rms_scale(attn_out, mlp_gain)
     half_rows = gather_rows(normed_mid, HALF, half_size)

time: 232 us -> 228 us (0.983)
  starting transfers between devices: 41.2 us -> 35 us
  waiting for transfers between devices: 57.3 us -> 51.3 us
  matrix products: 16.8 us -> 21.6 us
  other arithmetic: 6.62 us -> 9.59 us
    ppermute x1, starting transfers between devices: 8.38 us -> 0.63 us  [body(): taken = lax.ppermute(given, 'core', [(0, 1), (1, 0)])]
    all_to_all x1, waiting for transfers between devices: 15.6 us -> 9.78 us  [body(): out_parts = lax.all_to_all(out_chip, 'chip', 0, 0, tiled=True)]
    dot_general x0 -> x2, matrix products: none -> 4.24 us  [the longest x1 2.68 us: cache_block(): jnp.einsum('hqk,hkd->hqd', weights.astype(jnp.bfloat16), value_heads, pre...]
    ppermute x0 -> x1, starting transfers between devices: none -> 2.52 us  [body(): lax.ppermute(out_given.astype(jnp.bfloat16), 'core', [(0, 1), (1, 0)])]
    all_to_all x1, starting transfers between devices: 6.06 us -> 3.56 us  [body(): out_parts = lax.all_to_all(out_chip, 'chip', 0, 0, tiled=True)]
    unnamed x16 -> x14, local copies, waits for them, and re-layouts: 12.5 us -> 12.5 us
  transfers between devices with their start and end apart: 10 -> 11, of which waited for: 7 -> 8; matrix products, arithmetic and copies ran while one was open for 13% -> 14% of each run, Pallas kernels for 0% -> 0%
where the time goes in v12:
time: 228 us; the launch traced here: 224 us
  blocking collectives  65.1 us (29%)
  waiting for transfers between devices  51.3 us (22%)
  local copies, waits for them, and re-layouts  39.4 us (17%)
  starting transfers between devices  35 us (15%)
  matrix products  21.6 us (9%)
  other arithmetic  9.59 us (4%)
  between operations  2.3 us (1%)
    all_to_all x1, blocking collectives, body(): lax.all_to_all(ffn_part.astype(jnp.bfloat16), HALF, 0, 0, tiled=True)  29.3 us
    all_to_all x3, waiting for transfers between devices, gather_rows(): return lax.all_to_all(spread, axis, 0, 0, tiled=True)  20.3 us
    all_to_all x1, blocking collectives, gather_rows(): return lax.all_to_all(spread, axis, 0, 0, tiled=True)  20.2 us
    all_to_all x3, starting transfers between devices, gather_rows(): return lax.all_to_all(spread, axis, 0, 0, tiled=True)  19.6 us
    all_to_all x1, blocking collectives, send_rows(): return lax.all_to_all(blocks, axis, 0, 0, tiled=True)  15.7 us
    all_to_all x1, waiting for transfers between devices, body(): parts = lax.all_to_all(joined, 'chip', 0, 0, tiled=True)  13 us
    unnamed x14, local copies, waits for them, and re-layouts  12.5 us
    all_to_all x1, waiting for transfers between devices, body(): out_parts = lax.all_to_all(out_chip, 'chip', 0, 0, tiled=True)  9.78 us
  transfers between devices with their start and end apart: 11, of which 8 were waited for; matrix products, arithmetic and copies ran while one was open for 14% of the time, Pallas kernels for 0%

profile of v12, /device:TPU:1, one launch (start us, length us, event | category | flops | bytes accessed | tf_op | source)
XLA Modules:
  0.0 224.5 jit_solution(9464750979587892697)
XLA Ops:
  0.6 0.8 convert_element_type.172
  1.5 1.0 fusion.45
  2.5 0.9 fusion.47
  3.4 1.1 broadcast_in_dim.82
  4.6 7.6 %all-to-all-start = ((bf16[16,4,7168]{2,1,0:T(4,128)(2,1)}), bf16[16,4,7168]{2,1,0:T(4,128)(2,1)S(1)}, u32[]{:S(2)}, u32[]{:S(2)}) async-start(bf16[16,4,7168]{2,1,0:T(4,128)(2,1)} %broadcast_in_dim.82), calls=%async_computation | async-start | bytes 1835008 | tf_op jit(solution)/shard_map/all_to_all | solution.py:27
  12.1 5.9 %copy.62 = bf16[1,256,7168]{1,2,0:T(8,128)(2,1)} copy(bf16[1,256,7168]{2,1,0:T(8,128)(2,1)} %param.28) | data formatting | bytes 7340032 | tf_op args[10]
  18.1 5.9 %copy.61 = bf16[1,256,7168]{1,2,0:T(8,128)(2,1)} copy(bf16[1,256,7168]{2,1,0:T(8,128)(2,1)} %param.27) | data formatting | bytes 7340032 | tf_op args[9]
  24.0 4.1 %pad.7 = bf16[32,256,228]{1,2,0:T(8,128)(2,1)} pad(bf16[32,256,224]{1,2,0:T(8,128)(2,1)} %bitcast.143, bf16[]{:T(256)} %constant.109.clone.1), padding=0_0x0_0x0_4 | pad | bytes 7405570 | tf_op jit(solution)/shard_map/jit(_pad)/pad | solution.py:109
  28.1 1.1 collective-permute-start.1
  29.2 2.0 broadcast_in_dim.81
  31.2 1.3 constant_dynamic-update-slice_fusion.7
  32.5 1.3 constant_dynamic-update-slice_fusion.6
  33.8 2.9 %reshape_reshape.3 = bf16[128,7168]{1,0:T(8,128)(2,1)S(1)} reshape(bf16[16,2,4,7168]{3,2,1,0:T(4,128)(2,1)} %constant_dynamic-update-slice_fusion.6) | data formatting | bytes 3670016 | tf_op jit(solution)/shard_map/reshape;reshape | solution.py:106
  36.7 1.8 fusion.53
  38.6 1.7 reshape.298
  40.2 15.7 %all_to_all.40 = f32[32,4,384]{2,1,0:T(4,128)} all-to-all(f32[32,4,384]{2,1,0:T(4,128)} %reshape.298), channel_id=1, replica_groups=mesh['req'=4,'chip'=16,'core'=2] {'chip','core'}, dimensions={0} | all-to-all | bytes 393216 | tf_op jit(solution)/shard_map/all_to_all | solution.py:42
  55.9 1.0 reduce_sum.95
  56.9 0.7 broadcast_in_dim.84
  57.5 3.8 %all-to-all-start.2 = ((bf16[32,4,384]{2,1,0:T(4,128)(2,1)}), bf16[32,4,384]{2,1,0:T(4,128)(2,1)S(1)}, u32[]{:S(2)}, u32[]{:S(2)}) async-start(bf16[32,4,384]{2,1,0:T(4,128)(2,1)} %broadcast_in_dim.84), calls=%async_computation.2 | async-start | bytes 196608 | tf_op jit(solution)/shard_map/all_to_all | solution.py:27
  61.3 7.1 %fusion.90 = f32[128,672]{0,1:T(8,128)} fusion(bf16[128,7168]{1,0:T(8,128)(2,1)S(1)} %reshape_reshape.3, bf16[7168,672]{0,1:T(8,128)(2,1)} %bitcast.141), kind=kOutput, calls=%fused_computation.150 | convolution fusion | flops 1233125376 | bytes 11812864 | tf_op jit(solution)/shard_map/dot_general | solution.py:115
  68.4 0.5 all-to-all-done.2
  69.0 1.3 fusion.34
  70.3 0.6 copy-done.3
  71.0 20.2 %all_to_all.41 = bf16[16,128,224]{1,2,0:T(8,128)(2,1)S(1)} all-to-all(bf16[16,128,224]{1,2,0:T(8,128)(2,1)S(1)} %broadcast_in_dim.86), channel_id=1, replica_groups=mesh['req'=4,'chip'=16,'core'=2] {'chip'}, dimensions={0} | all-to-all | bytes 1835008 | tf_op jit(solution)/shard_map/all_to_all | solution.py:27
  91.2 2.3 %collective-permute-start.2 = (bf16[16,1,128,224]{2,3,1,0:T(8,128)(2,1)S(1)}, bf16[16,1,128,224]{2,3,1,0:T(8,128)(2,1)S(1)}, u32[]{:S(2)}, u32[]{:S(2)}) collective-permute-start(bf16[16,1,128,224]{2,3,1,0:T(8,128)(2,1)S(1)} %bitcast.148), channel_id=1, source_target_pairs={{0,1},{1,0},{2,3},{3,2},{4,5},{5,4},{6,7},{7,6},{8,9},{9,8},{10,11... | collective-permute-start | bytes 2752520 | tf_op jit(solution)/shard_map/ppermute | solution.py:32
  94.2 1.4 collective-permute-done.2
  95.7 10.7 %conditional.1 = (bf16[16,2,128,228]{2,3,1,0:T(8,128)(2,1)}) conditional(s32[]{:T(128)} %convert_element_type.170, () %tuple.23, (s32[]{:T(128)}, s32[256]{0:T(256)S(1)}, s32[]{:T(128)}, s32[1,256]{1,0:T(1,128)}, bf16[16,1,128,224]{2,3,1,0:T(8,128)(2,1)S(1)}, /*index=5*/s32[]{:T(128)}, bf16[16,1,128,224]{2,3,1,0:T(8,128)(2,1)S(1)}, s32[]{:T(128)}, ...), branch_computations={%region_2.3_spmd, %region_3.6_spmd} | conditional | flops 962577408 | bytes 59117136 | solution.py:159
  95.7 0.7 compare_reduce_fusion
  96.4 0.7 compare_and_fusion
  97.0 0.3 broadcast_in_dim.34
  97.6 1.8 copy-done.1
  99.4 1.6 fusion
  101.0 1.5 fusion.1
  102.6 0.5 copy-done.2
  103.1 2.7 %fusion.10 = bf16[32,128,228]{1,2,0:T(8,128)(2,1)} fusion(bf16[32,256,228]{1,2,0:T(8,128)(2,1)S(1)} %copy-done.2, f32[32,128,256]{2,1,0:T(8,128)S(1)} %get-tuple-element.138, f32[32,128]{1,0:T(8,128)S(1)} %reduce-precision_add_fusion, pred[256]{0:T(512)(128)(4,1)S(1)} %compare_and_fusion), kind=kOutput, calls=%fused_computation.11 | convolution fusion | flops 484327424 | bytes 9814272 | tf_op jit(solution)/shard_map/cond/branch_1_fun/hqk,hkd->hqd/dot_general | solution.py:145
  105.7 0.6 copy_dynamic-update-slice_fusion
  106.4 1.6 constant_dynamic-slice_fusion.1
  108.1 0.6 collective-permute-start.3
  108.9 2.0 collective-permute-done.3
  110.9 0.4 fusion.37
  111.4 1.2 copy.66
  112.6 3.6 %all-to-all-start.4 = ((bf16[16,128,228]{1,2,0:T(8,128)(2,1)}), bf16[16,128,228]{1,2,0:T(8,128)(2,1)S(1)}, u32[]{:S(2)}, u32[]{:S(2)}) async-start(bf16[16,128,228]{1,2,0:T(8,128)(2,1)} %copy.66), calls=%async_computation.4 | async-start | bytes 1900544 | tf_op jit(solution)/shard_map/all_to_all | solution.py:166
  116.9 1.0 fusion.89
  118.3 13.0 %all-to-all-done.4 = bf16[16,128,228]{1,2,0:T(8,128)(2,1)S(1)} async-done(((bf16[16,128,228]{1,2,0:T(8,128)(2,1)}), bf16[16,128,228]{1,2,0:T(8,128)(2,1)S(1)}, u32[]{:S(2)}, u32[]{:S(2)}) %all-to-all-start.4) | async-done | bytes 933920 | tf_op jit(solution)/shard_map/all_to_all | solution.py:166
  131.7 0.2 multiply_reduce_fusion
  132.0 0.9 fusion.50
  133.2 0.4 fusion.28
  133.7 2.5 %collective-permute-start.4 = (bf16[16,4,3584]{2,0,1:T(8,128)(2,1)S(1)}, bf16[16,4,3584]{2,0,1:T(8,128)(2,1)S(1)}, u32[]{:S(2)}, u32[]{:S(2)}) collective-permute-start(bf16[16,4,3584]{2,0,1:T(8,128)(2,1)S(1)} %fusion.39), channel_id=1, source_target_pairs={{0,1},{1,0},{2,3},{3,2},{4,5},{5,4},{6,7},{7,6},{8,9},{9,8},{10,11... | collective-permute-start | bytes 1376264 | tf_op jit(solution)/shard_map/ppermute | solution.py:209
  136.2 1.4 collective-permute-done.4
  137.7 1.1 copy.72
  138.9 3.6 %all-to-all-start.5 = ((bf16[16,4,3584]{2,1,0:T(4,128)(2,1)}), bf16[16,4,3584]{2,1,0:T(4,128)(2,1)S(1)}, u32[]{:S(2)}, u32[]{:S(2)}) async-start(bf16[16,4,3584]{2,1,0:T(4,128)(2,1)} %copy.72), calls=%async_computation.5 | async-start | bytes 917504 | tf_op jit(solution)/shard_map/all_to_all | solution.py:211
  142.5 9.8 %all-to-all-done.5 = bf16[16,4,3584]{2,1,0:T(4,128)(2,1)S(1)} async-done(((bf16[16,4,3584]{2,1,0:T(4,128)(2,1)}), bf16[16,4,3584]{2,1,0:T(4,128)(2,1)S(1)}, u32[]{:S(2)}, u32[]{:S(2)}) %all-to-all-start.5) | async-done | bytes 458784 | tf_op jit(solution)/shard_map/all_to_all | solution.py:211
  152.2 0.2 convert_reduce_fusion
  152.4 0.1 multiply_reduce_fusion.1
  152.7 1.7 broadcast_in_dim.90
  154.4 8.2 %all-to-all-start.6 = ((bf16[64,4,3584]{2,1,0:T(4,128)(2,1)}), bf16[64,4,3584]{2,1,0:T(4,128)(2,1)S(1)}, u32[]{:S(2)}, u32[]{:S(2)}) async-start(bf16[64,4,3584]{2,1,0:T(4,128)(2,1)} %broadcast_in_dim.90), calls=%async_computation.6 | async-start | bytes 3670016 | tf_op jit(solution)/shard_map/all_to_all | solution.py:27
  162.6 1.6 collective-permute-start
  164.3 3.3 %collective-permute-done = bf16[2,112,3584]{2,1,0:T(8,128)(2,1)} collective-permute-done((bf16[2,112,3584]{2,1,0:T(8,128)(2,1)}, bf16[2,112,3584]{2,1,0:T(8,128)(2,1)}, u32[]{:S(2)}, u32[]{:S(2)}) %collective-permute-start) | collective-permute-done | bytes 1605664 | tf_op jit(solution)/shard_map/ppermute | solution.py:102
  167.7 19.8 %all-to-all-done.6 = bf16[64,4,3584]{2,1,0:T(4,128)(2,1)S(1)} async-done(((bf16[64,4,3584]{2,1,0:T(4,128)(2,1)}), bf16[64,4,3584]{2,1,0:T(4,128)(2,1)S(1)}, u32[]{:S(2)}, u32[]{:S(2)}) %all-to-all-start.6) | async-done | bytes 1835040 | tf_op jit(solution)/shard_map/all_to_all | solution.py:27
  187.5 3.1 %fusion.30 = f32[2,64,4,224]{3,1,2,0:T(8,128)S(1)} fusion(bf16[64,4,3584]{2,1,0:T(4,128)(2,1)S(1)} %all-to-all-done.6, bf16[2,112,3584]{2,1,0:T(8,128)(2,1)} %collective-permute-done, bf16[2,112,3584]{2,1,0:T(8,128)(2,1)} %param.25), kind=kOutput, calls=%fused_computation.46 | convolution fusion | flops 828506112 | bytes 5505024 | tf_op jit(solution)/shard_map/gtd,cfd->cgtf/dot_general | solution.py:215
  190.6 1.8 convolution_convert_fusion
  192.4 1.4 copy.74
  193.8 29.3 %all_to_all.42 = bf16[64,4,3584]{2,1,0:T(4,128)(2,1)S(1)} all-to-all(bf16[64,4,3584]{2,1,0:T(4,128)(2,1)S(1)} %copy.74), channel_id=1, replica_groups=mesh['req'=4,'chip'=16,'core'=2] {'req','chip'}, dimensions={0} | all-to-all | bytes 3670016 | tf_op jit(solution)/shard_map/all_to_all | solution.py:218
  223.1 1.4 reduce_sum.104
  (59 shorter events, 2.3 us)
Async XLA Ops:
  0.6 132.6 %copy-start = (bf16[224,3584]{1,0:T(8,128)(2,1)S(1)}, bf16[224,3584]{1,0:T(8,128)(2,1)}, u32[]{:S(2)}) copy-start(bf16[224,3584]{1,0:T(8,128)(2,1)} %param.23) | copy-start | bytes 4816900
  4.6 23.6 %all-to-all-start = ((bf16[16,4,7168]{2,1,0:T(4,128)(2,1)}), bf16[16,4,7168]{2,1,0:T(4,128)(2,1)S(1)}, u32[]{:S(2)}, u32[]{:S(2)}) async-start(bf16[16,4,7168]{2,1,0:T(4,128)(2,1)} %broadcast_in_dim.82), calls=%async_computation | async-start | bytes 1835008 | tf_op jit(solution)/shard_map/all_to_all | solution.py:27
  28.1 4.4 %collective-permute-start.1 = (bf16[16,1,4,7168]{3,2,1,0:T(4,128)(2,1)S(1)}, bf16[16,1,4,7168]{3,2,1,0:T(4,128)(2,1)S(1)}, u32[]{:S(2)}, u32[]{:S(2)}) collective-permute-start(bf16[16,1,4,7168]{3,2,1,0:T(4,128)(2,1)S(1)} %bitcast.150), channel_id=1, source_target_pairs={{0,1},{1,0},{2,3},{3,2},{4,5},{5,4},{6,7},{7,6},{8,9},{9,8},{10,11... | collective-permute-start | bytes 2752520 | tf_op jit(solution)/shard_map/ppermute | solution.py:32
  57.5 11.4 %all-to-all-start.2 = ((bf16[32,4,384]{2,1,0:T(4,128)(2,1)}), bf16[32,4,384]{2,1,0:T(4,128)(2,1)S(1)}, u32[]{:S(2)}, u32[]{:S(2)}) async-start(bf16[32,4,384]{2,1,0:T(4,128)(2,1)} %broadcast_in_dim.84), calls=%async_computation.2 | async-start | bytes 196608 | tf_op jit(solution)/shard_map/all_to_all | solution.py:27
  70.2 0.7 copy-start.3
  70.9 46.0 %copy-start.5 = (bf16[128,224]{0,1:T(8,128)(2,1)}, bf16[128,224]{0,1:T(8,128)(2,1)S(1)}, u32[]{:S(2)}) copy-start(bf16[128,224]{0,1:T(8,128)(2,1)S(1)} %get-tuple-element.146) | copy-start | bytes 172036
  70.9 61.0 %copy-start.4 = (bf16[128,224]{0,1:T(8,128)(2,1)}, bf16[128,224]{0,1:T(8,128)(2,1)S(1)}, u32[]{:S(2)}) copy-start(bf16[128,224]{0,1:T(8,128)(2,1)S(1)} %get-tuple-element.145) | copy-start | bytes 172036
  91.2 4.4 %collective-permute-start.2 = (bf16[16,1,128,224]{2,3,1,0:T(8,128)(2,1)S(1)}, bf16[16,1,128,224]{2,3,1,0:T(8,128)(2,1)S(1)}, u32[]{:S(2)}, u32[]{:S(2)}) collective-permute-start(bf16[16,1,128,224]{2,3,1,0:T(8,128)(2,1)S(1)} %bitcast.148), channel_id=1, source_target_pairs={{0,1},{1,0},{2,3},{3,2},{4,5},{5,4},{6,7},{7,6},{8,9},{9,8},{10,11... | collective-permute-start | bytes 2752520 | tf_op jit(solution)/shard_map/ppermute | solution.py:32
  97.4 2.0 copy-start.1
  101.0 2.1 copy-start.2
  108.1 2.8 %collective-permute-start.3 = (bf16[16,128,228]{1,0,2:T(8,128)(2,1)S(1)}, bf16[16,128,228]{1,0,2:T(8,128)(2,1)S(1)}, u32[]{:S(2)}, u32[]{:S(2)}) collective-permute-start(bf16[16,128,228]{1,0,2:T(8,128)(2,1)S(1)} %bitcast.152), channel_id=1, source_target_pairs={{0,1},{1,0},{2,3},{3,2},{4,5},{5,4},{6,7},{7,6},{8,9},{9,8},{10,11... | collective-permute-start | bytes 2801672 | tf_op jit(solution)/shard_map/ppermute | solution.py:164
  112.6 18.7 %all-to-all-start.4 = ((bf16[16,128,228]{1,2,0:T(8,128)(2,1)}), bf16[16,128,228]{1,2,0:T(8,128)(2,1)S(1)}, u32[]{:S(2)}, u32[]{:S(2)}) async-start(bf16[16,128,228]{1,2,0:T(8,128)(2,1)} %copy.66), calls=%async_computation.4 | async-start | bytes 1900544 | tf_op jit(solution)/shard_map/all_to_all | solution.py:166
  133.7 8.8 %copy-start.6 = (bf16[3584]{0:T(1024)(128)(2,1)S(1)}, bf16[3584]{0:T(1024)(128)(2,1)}, u32[]{:S(2)}) copy-start(bf16[3584]{0:T(1024)(128)(2,1)} %param.24) | copy-start | bytes 21508
  133.7 4.0 %collective-permute-start.4 = (bf16[16,4,3584]{2,0,1:T(8,128)(2,1)S(1)}, bf16[16,4,3584]{2,0,1:T(8,128)(2,1)S(1)}, u32[]{:S(2)}, u32[]{:S(2)}) collective-permute-start(bf16[16,4,3584]{2,0,1:T(8,128)(2,1)S(1)} %fusion.39), channel_id=1, source_target_pairs={{0,1},{1,0},{2,3},{3,2},{4,5},{5,4},{6,7},{7,6},{8,9},{9,8},{10,11... | collective-permute-start | bytes 1376264 | tf_op jit(solution)/shard_map/ppermute | solution.py:209
  138.9 13.4 %all-to-all-start.5 = ((bf16[16,4,3584]{2,1,0:T(4,128)(2,1)}), bf16[16,4,3584]{2,1,0:T(4,128)(2,1)S(1)}, u32[]{:S(2)}, u32[]{:S(2)}) async-start(bf16[16,4,3584]{2,1,0:T(4,128)(2,1)} %copy.72), calls=%async_computation.5 | async-start | bytes 917504 | tf_op jit(solution)/shard_map/all_to_all | solution.py:211
  154.4 33.1 %all-to-all-start.6 = ((bf16[64,4,3584]{2,1,0:T(4,128)(2,1)}), bf16[64,4,3584]{2,1,0:T(4,128)(2,1)S(1)}, u32[]{:S(2)}, u32[]{:S(2)}) async-start(bf16[64,4,3584]{2,1,0:T(4,128)(2,1)} %broadcast_in_dim.90), calls=%async_computation.6 | async-start | bytes 3670016 | tf_op jit(solution)/shard_map/all_to_all | solution.py:27
  162.6 5.0 %collective-permute-start = (bf16[2,112,3584]{2,1,0:T(8,128)(2,1)}, bf16[2,112,3584]{2,1,0:T(8,128)(2,1)}, u32[]{:S(2)}, u32[]{:S(2)}) collective-permute-start(bf16[2,112,3584]{2,1,0:T(8,128)(2,1)} %param.25), channel_id=1, source_target_pairs={{0,1},{1,0},{2,3},{3,2},{4,5},{5,4},{6,7},{7,6},{8,9},{9,8},{10,11... | collective-permute-start | bytes 4816904 | tf_op jit(solution)/shard_map/ppermute | solution.py:102
  164.2 26.4 %collective-permute-start.5 = (bf16[112,3584]{1,0:T(8,128)(2,1)}, bf16[112,3584]{1,0:T(8,128)(2,1)}, u32[]{:S(2)}, u32[]{:S(2)}) collective-permute-start(bf16[112,3584]{1,0:T(8,128)(2,1)} %param.26), channel_id=1, source_target_pairs={{0,1},{1,0},{2,3},{3,2},{4,5},{5,4},{6,7},{7,6},{8,9},{9,8},{10,11... | collective-permute-start | bytes 2408456 | tf_op jit(solution)/shard_map/ppermute | solution.py:103
  187.5 3.1 %copy-start.7 = (bf16[112,3584]{1,0:T(8,128)(2,1)S(1)}, bf16[112,3584]{1,0:T(8,128)(2,1)}, u32[]{:S(2)}) copy-start(bf16[112,3584]{1,0:T(8,128)(2,1)} %param.26) | copy-start | bytes 2408452

commit v13 on v12

--- a/solution.py
+++ b/solution.py
@@ -99,8 +99,8 @@
     feature_start = wide_index * local_width
 
     swap = [(0, 1), (1, 0)]
-    chip_gate = jnp.concatenate([gate_up, lax.ppermute(gate_up, "core", swap)], axis=1)
-    chip_down = jnp.concatenate([down_weight, lax.ppermute(down_weight, "core", swap)], axis=0)
+    sibling_gate = lax.ppermute(gate_up, "core", swap)
+    sibling_down = lax.ppermute(down_weight, "core", swap)
 
     normed = rms_scale(tokens, attn_gain)
     shard_rows = gather_wide(normed, chips).reshape(SPAN, D)
@@ -212,9 +212,12 @@
     attn_out = jnp.sum(out_parts.astype(jnp.float32), axis=0)
     normed_mid = rms_scale(attn_out, mlp_gain)
     half_rows = gather_rows(normed_mid, HALF, half_size)
-    both = jnp.einsum("gtd,cfd->cgtf", half_rows, chip_gate, preferred_element_type=jnp.float32)
-    hidden = (jax.nn.silu(both[0]) * both[1]).astype(jnp.bfloat16)
-    ffn_part = jnp.einsum("gtf,fd->gtd", hidden, chip_down, preferred_element_type=jnp.float32)
+    ffn_part = None
+    for gate_rows, down_rows in ((gate_up, down_weight), (sibling_gate, sibling_down)):
+        both = jnp.einsum("gtd,cfd->cgtf", half_rows, gate_rows, preferred_element_type=jnp.float32)
+        hidden = (jax.nn.silu(both[0]) * both[1]).astype(jnp.bfloat16)
+        term = jnp.einsum("gtf,fd->gtd", hidden, down_rows, preferred_element_type=jnp.float32)
+        ffn_part = term if ffn_part is None else ffn_part + term
     ffn_parts = lax.all_to_all(ffn_part.astype(jnp.bfloat16), HALF, 0, 0, tiled=True)
     hidden_out = jnp.sum(ffn_parts.astype(jnp.float32), axis=0).astype(jnp.bfloat16)
     return (hidden_out, attention, new_keys, new_values)

time: 228 us -> 230 us (level)
    all_to_all x3, waiting for transfers between devices: 20.3 us -> 23.6 us  [gather_rows(): return lax.all_to_all(spread, axis, 0, 0, tiled=True)]
    ppermute x2, waiting for transfers between devices: 3.33 us -> 0.01 us  [the longest x1 0.01 us: body(): sibling_gate = lax.ppermute(gate_up, 'core', swap)]
    dot_general x2 -> x4, matrix products: 4.9 us -> 6.68 us  [the longest x2 4.28 us: body(): jnp.einsum('gtd,cfd->cgtf', half_rows, gate_rows, preferred_element_type=...]
  transfers between devices with their start and end apart: 11 -> 11, of which waited for: 8 -> 7; matrix products, arithmetic and copies ran while one was open for 14% -> 14% of each run, Pallas kernels for 0% -> 0%
where the time goes in v13:
time: 230 us; the launch traced here: 226 us
  blocking collectives  65.2 us (28%)
  waiting for transfers between devices  51 us (22%)
  local copies, waits for them, and re-layouts  39.4 us (17%)
  starting transfers between devices  35.4 us (15%)
  matrix products  23.4 us (10%)
  other arithmetic  9.59 us (4%)
  between operations  2.32 us (1%)
    all_to_all x1, blocking collectives, body(): lax.all_to_all(ffn_part.astype(jnp.bfloat16), HALF, 0, 0, tiled=True)  29.3 us
    all_to_all x3, waiting for transfers between devices, gather_rows(): return lax.all_to_all(spread, axis, 0, 0, tiled=True)  23.6 us
    all_to_all x1, blocking collectives, gather_rows(): return lax.all_to_all(spread, axis, 0, 0, tiled=True)  20.2 us
    all_to_all x3, starting transfers between devices, gather_rows(): return lax.all_to_all(spread, axis, 0, 0, tiled=True)  19.6 us
    all_to_all x1, blocking collectives, send_rows(): return lax.all_to_all(blocks, axis, 0, 0, tiled=True)  15.7 us
    all_to_all x1, waiting for transfers between devices, body(): parts = lax.all_to_all(joined, 'chip', 0, 0, tiled=True)  12.7 us
    unnamed x14, local copies, waits for them, and re-layouts  12.5 us
    all_to_all x1, waiting for transfers between devices, body(): out_parts = lax.all_to_all(out_chip, 'chip', 0, 0, tiled=True)  9.78 us
  transfers between devices with their start and end apart: 11, of which 7 were waited for; matrix products, arithmetic and copies ran while one was open for 14% of the time, Pallas kernels for 0%

profile of v13, /device:TPU:1, one launch (start us, length us, event | category | flops | bytes accessed | tf_op | source)
XLA Modules:
  0.0 226.3 jit_solution(11291343181125295770)
XLA Ops:
  0.6 0.8 convert_element_type.175
  1.5 1.0 fusion.56
  2.5 0.9 fusion.58
  3.4 1.1 broadcast_in_dim.82
  4.6 7.6 %all-to-all-start = ((bf16[16,4,7168]{2,1,0:T(4,128)(2,1)}), bf16[16,4,7168]{2,1,0:T(4,128)(2,1)S(1)}, u32[]{:S(2)}, u32[]{:S(2)}) async-start(bf16[16,4,7168]{2,1,0:T(4,128)(2,1)} %broadcast_in_dim.82), calls=%async_computation | async-start | bytes 1835008 | tf_op jit(solution)/shard_map/all_to_all | solution.py:27
  12.1 5.9 %copy.72 = bf16[1,256,7168]{1,2,0:T(8,128)(2,1)} copy(bf16[1,256,7168]{2,1,0:T(8,128)(2,1)} %param.28) | data formatting | bytes 7340032 | tf_op args[10]
  18.1 5.9 %copy.71 = bf16[1,256,7168]{1,2,0:T(8,128)(2,1)} copy(bf16[1,256,7168]{2,1,0:T(8,128)(2,1)} %param.27) | data formatting | bytes 7340032 | tf_op args[9]
  24.0 4.1 %pad.7 = bf16[32,256,228]{1,2,0:T(8,128)(2,1)} pad(bf16[32,256,224]{1,2,0:T(8,128)(2,1)} %bitcast.168, bf16[]{:T(256)} %constant.110.clone.1), padding=0_0x0_0x0_4 | pad | bytes 7405570 | tf_op jit(solution)/shard_map/jit(_pad)/pad | solution.py:109
  28.1 1.1 collective-permute-start
  29.2 2.0 broadcast_in_dim.81
  31.2 1.3 constant_dynamic-update-slice_fusion.7
  32.5 1.3 constant_dynamic-update-slice_fusion.6
  33.8 2.9 %reshape_reshape.3 = bf16[128,7168]{1,0:T(8,128)(2,1)S(1)} reshape(bf16[16,2,4,7168]{3,2,1,0:T(4,128)(2,1)} %constant_dynamic-update-slice_fusion.6) | data formatting | bytes 3670016 | tf_op jit(solution)/shard_map/reshape;reshape | solution.py:106
  36.7 1.8 fusion.68
  38.6 1.7 reshape.298
  40.2 15.7 %all_to_all.40 = f32[32,4,384]{2,1,0:T(4,128)} all-to-all(f32[32,4,384]{2,1,0:T(4,128)} %reshape.298), channel_id=1, replica_groups=mesh['req'=4,'chip'=16,'core'=2] {'chip','core'}, dimensions={0} | all-to-all | bytes 393216 | tf_op jit(solution)/shard_map/all_to_all | solution.py:42
  55.9 1.0 reduce_sum.95
  56.9 0.7 broadcast_in_dim.84
  57.5 3.8 %all-to-all-start.2 = ((bf16[32,4,384]{2,1,0:T(4,128)(2,1)}), bf16[32,4,384]{2,1,0:T(4,128)(2,1)S(1)}, u32[]{:S(2)}, u32[]{:S(2)}) async-start(bf16[32,4,384]{2,1,0:T(4,128)(2,1)} %broadcast_in_dim.84), calls=%async_computation.2 | async-start | bytes 196608 | tf_op jit(solution)/shard_map/all_to_all | solution.py:27
  61.3 7.1 %fusion.104 = f32[128,672]{0,1:T(8,128)} fusion(bf16[128,7168]{1,0:T(8,128)(2,1)S(1)} %reshape_reshape.3, bf16[7168,672]{0,1:T(8,128)(2,1)} %bitcast.166), kind=kOutput, calls=%fused_computation.157 | convolution fusion | flops 1233125376 | bytes 11812864 | tf_op jit(solution)/shard_map/dot_general | solution.py:115
  68.4 0.5 all-to-all-done.2
  69.0 1.3 fusion.42
  70.3 0.6 copy-done.4
  71.0 20.2 %all_to_all.41 = bf16[16,128,224]{1,2,0:T(8,128)(2,1)S(1)} all-to-all(bf16[16,128,224]{1,2,0:T(8,128)(2,1)S(1)} %broadcast_in_dim.86), channel_id=1, replica_groups=mesh['req'=4,'chip'=16,'core'=2] {'chip'}, dimensions={0} | all-to-all | bytes 1835008 | tf_op jit(solution)/shard_map/all_to_all | solution.py:27
  91.2 2.3 %collective-permute-start.1 = (bf16[16,1,128,224]{2,3,1,0:T(8,128)(2,1)S(1)}, bf16[16,1,128,224]{2,3,1,0:T(8,128)(2,1)S(1)}, u32[]{:S(2)}, u32[]{:S(2)}) collective-permute-start(bf16[16,1,128,224]{2,3,1,0:T(8,128)(2,1)S(1)} %bitcast.173), channel_id=1, source_target_pairs={{0,1},{1,0},{2,3},{3,2},{4,5},{5,4},{6,7},{7,6},{8,9},{9,8},{10,11... | collective-permute-start | bytes 2752520 | tf_op jit(solution)/shard_map/ppermute | solution.py:32
  94.2 1.4 collective-permute-done.1
  95.7 10.7 %conditional.1 = (bf16[16,2,128,228]{2,3,1,0:T(8,128)(2,1)}) conditional(s32[]{:T(128)} %convert_element_type.173, () %tuple.23, (s32[]{:T(128)}, s32[256]{0:T(256)S(1)}, s32[]{:T(128)}, s32[1,256]{1,0:T(1,128)}, bf16[16,1,128,224]{2,3,1,0:T(8,128)(2,1)S(1)}, /*index=5*/s32[]{:T(128)}, bf16[16,1,128,224]{2,3,1,0:T(8,128)(2,1)S(1)}, s32[]{:T(128)}, ...), branch_computations={%region_2.3_spmd, %region_3.6_spmd} | conditional | flops 962577408 | bytes 59117136 | solution.py:159
  95.7 0.7 compare_reduce_fusion
  96.4 0.7 compare_and_fusion
  97.0 0.3 broadcast_in_dim.34
  97.6 1.8 copy-done.1
  99.4 1.6 fusion
  101.0 1.5 fusion.1
  102.6 0.5 copy-done.2
  103.1 2.7 %fusion.10 = bf16[32,128,228]{1,2,0:T(8,128)(2,1)} fusion(bf16[32,256,228]{1,2,0:T(8,128)(2,1)S(1)} %copy-done.2, f32[32,128,256]{2,1,0:T(8,128)S(1)} %get-tuple-element.138, f32[32,128]{1,0:T(8,128)S(1)} %reduce-precision_add_fusion, pred[256]{0:T(512)(128)(4,1)S(1)} %compare_and_fusion), kind=kOutput, calls=%fused_computation.11 | convolution fusion | flops 484327424 | bytes 9814272 | tf_op jit(solution)/shard_map/cond/branch_1_fun/hqk,hkd->hqd/dot_general | solution.py:145
  105.7 0.6 copy_dynamic-update-slice_fusion
  106.4 1.6 constant_dynamic-slice_fusion.1
  108.1 0.6 collective-permute-start.2
  108.9 2.0 collective-permute-done.2
  110.9 0.4 fusion.45
  111.4 1.2 copy.76
  112.6 3.6 %all-to-all-start.4 = ((bf16[16,128,228]{1,2,0:T(8,128)(2,1)}), bf16[16,128,228]{1,2,0:T(8,128)(2,1)S(1)}, u32[]{:S(2)}, u32[]{:S(2)}) async-start(bf16[16,128,228]{1,2,0:T(8,128)(2,1)} %copy.76), calls=%async_computation.4 | async-start | bytes 1900544 | tf_op jit(solution)/shard_map/all_to_all | solution.py:166
  116.9 1.0 fusion.103
  118.3 12.7 %all-to-all-done.4 = bf16[16,128,228]{1,2,0:T(8,128)(2,1)S(1)} async-done(((bf16[16,128,228]{1,2,0:T(8,128)(2,1)}), bf16[16,128,228]{1,2,0:T(8,128)(2,1)S(1)}, u32[]{:S(2)}, u32[]{:S(2)}) %all-to-all-start.4) | async-done | bytes 933920 | tf_op jit(solution)/shard_map/all_to_all | solution.py:166
  131.3 0.2 multiply_reduce_fusion
  131.6 0.9 fusion.61
  132.9 0.4 fusion.28
  133.4 2.9 %collective-permute-start.3 = (bf16[16,4,3584]{2,0,1:T(8,128)(2,1)S(1)}, bf16[16,4,3584]{2,0,1:T(8,128)(2,1)S(1)}, u32[]{:S(2)}, u32[]{:S(2)}) collective-permute-start(bf16[16,4,3584]{2,0,1:T(8,128)(2,1)S(1)} %fusion.50), channel_id=1, source_target_pairs={{0,1},{1,0},{2,3},{3,2},{4,5},{5,4},{6,7},{7,6},{8,9},{9,8},{10,11... | collective-permute-start | bytes 1376264 | tf_op jit(solution)/shard_map/ppermute | solution.py:209
  136.2 1.4 collective-permute-done.3
  137.7 1.1 copy.82
  138.9 3.6 %all-to-all-start.5 = ((bf16[16,4,3584]{2,1,0:T(4,128)(2,1)}), bf16[16,4,3584]{2,1,0:T(4,128)(2,1)S(1)}, u32[]{:S(2)}, u32[]{:S(2)}) async-start(bf16[16,4,3584]{2,1,0:T(4,128)(2,1)} %copy.82), calls=%async_computation.5 | async-start | bytes 917504 | tf_op jit(solution)/shard_map/all_to_all | solution.py:211
  142.5 9.8 %all-to-all-done.5 = bf16[16,4,3584]{2,1,0:T(4,128)(2,1)S(1)} async-done(((bf16[16,4,3584]{2,1,0:T(4,128)(2,1)}), bf16[16,4,3584]{2,1,0:T(4,128)(2,1)S(1)}, u32[]{:S(2)}, u32[]{:S(2)}) %all-to-all-start.5) | async-done | bytes 458784 | tf_op jit(solution)/shard_map/all_to_all | solution.py:211
  152.2 0.2 convert_reduce_fusion
  152.7 1.7 broadcast_in_dim.90
  154.4 8.2 %all-to-all-start.6 = ((bf16[64,4,3584]{2,1,0:T(4,128)(2,1)}), bf16[64,4,3584]{2,1,0:T(4,128)(2,1)S(1)}, u32[]{:S(2)}, u32[]{:S(2)}) async-start(bf16[64,4,3584]{2,1,0:T(4,128)(2,1)} %broadcast_in_dim.90), calls=%async_computation.6 | async-start | bytes 3670016 | tf_op jit(solution)/shard_map/all_to_all | solution.py:27
  162.7 1.6 collective-permute-start.4
  164.3 23.2 %all-to-all-done.6 = bf16[64,4,3584]{2,1,0:T(4,128)(2,1)S(1)} async-done(((bf16[64,4,3584]{2,1,0:T(4,128)(2,1)}), bf16[64,4,3584]{2,1,0:T(4,128)(2,1)S(1)}, u32[]{:S(2)}, u32[]{:S(2)}) %all-to-all-start.6) | async-done | bytes 1835040 | tf_op jit(solution)/shard_map/all_to_all | solution.py:27
  187.5 2.1 fusion.32
  189.6 2.2 fusion.37
  191.8 0.6 fusion.48
  192.5 1.8 fusion.21
  194.2 1.4 copy.87
  195.7 29.3 %all_to_all.42 = bf16[64,4,3584]{2,1,0:T(4,128)(2,1)S(1)} all-to-all(bf16[64,4,3584]{2,1,0:T(4,128)(2,1)S(1)} %copy.87), channel_id=1, replica_groups=mesh['req'=4,'chip'=16,'core'=2] {'req','chip'}, dimensions={0} | all-to-all | bytes 3670016 | tf_op jit(solution)/shard_map/all_to_all | solution.py:221
  225.0 1.4 reduce_sum.104
  (61 shorter events, 2.4 us)
Async XLA Ops:
  0.6 132.2 %copy-start = (bf16[224,3584]{1,0:T(8,128)(2,1)S(1)}, bf16[224,3584]{1,0:T(8,128)(2,1)}, u32[]{:S(2)}) copy-start(bf16[224,3584]{1,0:T(8,128)(2,1)} %param.23) | copy-start | bytes 4816900
  4.6 23.6 %all-to-all-start = ((bf16[16,4,7168]{2,1,0:T(4,128)(2,1)}), bf16[16,4,7168]{2,1,0:T(4,128)(2,1)S(1)}, u32[]{:S(2)}, u32[]{:S(2)}) async-start(bf16[16,4,7168]{2,1,0:T(4,128)(2,1)} %broadcast_in_dim.82), calls=%async_computation | async-start | bytes 1835008 | tf_op jit(solution)/shard_map/all_to_all | solution.py:27
  28.1 4.4 %collective-permute-start = (bf16[16,1,4,7168]{3,2,1,0:T(4,128)(2,1)S(1)}, bf16[16,1,4,7168]{3,2,1,0:T(4,128)(2,1)S(1)}, u32[]{:S(2)}, u32[]{:S(2)}) collective-permute-start(bf16[16,1,4,7168]{3,2,1,0:T(4,128)(2,1)S(1)} %bitcast.175), channel_id=1, source_target_pairs={{0,1},{1,0},{2,3},{3,2},{4,5},{5,4},{6,7},{7,6},{8,9},{9,8},{10,11... | collective-permute-start | bytes 2752520 | tf_op jit(solution)/shard_map/ppermute | solution.py:32
  57.5 11.4 %all-to-all-start.2 = ((bf16[32,4,384]{2,1,0:T(4,128)(2,1)}), bf16[32,4,384]{2,1,0:T(4,128)(2,1)S(1)}, u32[]{:S(2)}, u32[]{:S(2)}) async-start(bf16[32,4,384]{2,1,0:T(4,128)(2,1)} %broadcast_in_dim.84), calls=%async_computation.2 | async-start | bytes 196608 | tf_op jit(solution)/shard_map/all_to_all | solution.py:27
  70.2 0.7 copy-start.4
  70.9 46.0 %copy-start.6 = (bf16[128,224]{0,1:T(8,128)(2,1)}, bf16[128,224]{0,1:T(8,128)(2,1)S(1)}, u32[]{:S(2)}) copy-start(bf16[128,224]{0,1:T(8,128)(2,1)S(1)} %get-tuple-element.146) | copy-start | bytes 172036
  70.9 60.7 %copy-start.5 = (bf16[128,224]{0,1:T(8,128)(2,1)}, bf16[128,224]{0,1:T(8,128)(2,1)S(1)}, u32[]{:S(2)}) copy-start(bf16[128,224]{0,1:T(8,128)(2,1)S(1)} %get-tuple-element.145) | copy-start | bytes 172036
  91.2 4.4 %collective-permute-start.1 = (bf16[16,1,128,224]{2,3,1,0:T(8,128)(2,1)S(1)}, bf16[16,1,128,224]{2,3,1,0:T(8,128)(2,1)S(1)}, u32[]{:S(2)}, u32[]{:S(2)}) collective-permute-start(bf16[16,1,128,224]{2,3,1,0:T(8,128)(2,1)S(1)} %bitcast.173), channel_id=1, source_target_pairs={{0,1},{1,0},{2,3},{3,2},{4,5},{5,4},{6,7},{7,6},{8,9},{9,8},{10,11... | collective-permute-start | bytes 2752520 | tf_op jit(solution)/shard_map/ppermute | solution.py:32
  97.4 2.0 copy-start.1
  101.0 2.1 copy-start.2
  108.1 2.8 %collective-permute-start.2 = (bf16[16,128,228]{1,0,2:T(8,128)(2,1)S(1)}, bf16[16,128,228]{1,0,2:T(8,128)(2,1)S(1)}, u32[]{:S(2)}, u32[]{:S(2)}) collective-permute-start(bf16[16,128,228]{1,0,2:T(8,128)(2,1)S(1)} %bitcast.178), channel_id=1, source_target_pairs={{0,1},{1,0},{2,3},{3,2},{4,5},{5,4},{6,7},{7,6},{8,9},{9,8},{10,11... | collective-permute-start | bytes 2801672 | tf_op jit(solution)/shard_map/ppermute | solution.py:164
  112.6 18.4 %all-to-all-start.4 = ((bf16[16,128,228]{1,2,0:T(8,128)(2,1)}), bf16[16,128,228]{1,2,0:T(8,128)(2,1)S(1)}, u32[]{:S(2)}, u32[]{:S(2)}) async-start(bf16[16,128,228]{1,2,0:T(8,128)(2,1)} %copy.76), calls=%async_computation.4 | async-start | bytes 1900544 | tf_op jit(solution)/shard_map/all_to_all | solution.py:166
  133.3 9.1 %copy-start.7 = (bf16[3584]{0:T(1024)(128)(2,1)S(1)}, bf16[3584]{0:T(1024)(128)(2,1)}, u32[]{:S(2)}) copy-start(bf16[3584]{0:T(1024)(128)(2,1)} %param.24) | copy-start | bytes 21508
  133.4 4.3 %collective-permute-start.3 = (bf16[16,4,3584]{2,0,1:T(8,128)(2,1)S(1)}, bf16[16,4,3584]{2,0,1:T(8,128)(2,1)S(1)}, u32[]{:S(2)}, u32[]{:S(2)}) collective-permute-start(bf16[16,4,3584]{2,0,1:T(8,128)(2,1)S(1)} %fusion.50), channel_id=1, source_target_pairs={{0,1},{1,0},{2,3},{3,2},{4,5},{5,4},{6,7},{7,6},{8,9},{9,8},{10,11... | collective-permute-start | bytes 1376264 | tf_op jit(solution)/shard_map/ppermute | solution.py:209
  138.9 13.4 %all-to-all-start.5 = ((bf16[16,4,3584]{2,1,0:T(4,128)(2,1)}), bf16[16,4,3584]{2,1,0:T(4,128)(2,1)S(1)}, u32[]{:S(2)}, u32[]{:S(2)}) async-start(bf16[16,4,3584]{2,1,0:T(4,128)(2,1)} %copy.82), calls=%async_computation.5 | async-start | bytes 917504 | tf_op jit(solution)/shard_map/all_to_all | solution.py:211
  154.4 33.1 %all-to-all-start.6 = ((bf16[64,4,3584]{2,1,0:T(4,128)(2,1)}), bf16[64,4,3584]{2,1,0:T(4,128)(2,1)S(1)}, u32[]{:S(2)}, u32[]{:S(2)}) async-start(bf16[64,4,3584]{2,1,0:T(4,128)(2,1)} %broadcast_in_dim.90), calls=%async_computation.6 | async-start | bytes 3670016 | tf_op jit(solution)/shard_map/all_to_all | solution.py:27
  162.7 27.0 %collective-permute-start.4 = (bf16[2,112,3584]{2,1,0:T(8,128)(2,1)}, bf16[2,112,3584]{2,1,0:T(8,128)(2,1)}, u32[]{:S(2)}, u32[]{:S(2)}) collective-permute-start(bf16[2,112,3584]{2,1,0:T(8,128)(2,1)} %param.25), channel_id=1, source_target_pairs={{0,1},{1,0},{2,3},{3,2},{4,5},{5,4},{6,7},{7,6},{8,9},{9,8},{10,11... | collective-permute-start | bytes 4816904 | tf_op jit(solution)/shard_map/ppermute | solution.py:102
  164.2 28.2 %collective-permute-start.5 = (bf16[112,3584]{1,0:T(8,128)(2,1)}, bf16[112,3584]{1,0:T(8,128)(2,1)}, u32[]{:S(2)}, u32[]{:S(2)}) collective-permute-start(bf16[112,3584]{1,0:T(8,128)(2,1)} %param.26), channel_id=1, source_target_pairs={{0,1},{1,0},{2,3},{3,2},{4,5},{5,4},{6,7},{7,6},{8,9},{9,8},{10,11... | collective-permute-start | bytes 2408456 | tf_op jit(solution)/shard_map/ppermute | solution.py:103
  189.6 2.2 copy-start.3
